TPU v7x, 256 devices: a whole 4x4x8 slice. The times are simulated.
256 devices in a mesh: blk: 4 (over x), shard: 64 (over y, z, core).
Axes of the slice: x: 4, y: 4, z: 8, core: 2. Of those that a mesh axis runs over, the one named last changes fastest.
Arguments:
- table: bfloat16 [524288, 400], P(('blk', 'shard')), may hold values from -3 to 3
- relation: bfloat16 [1345, 400], replicated, may hold values from -3 to 3
- owners: int32 [262144, 2], P(('blk', 'shard')), may hold values from 0 to 63, all different within a row; in each aligned block of 1024 rows (0 to 1023, 1024 to 2047, ...) at most 64 rows name the same one
- rows: int32 [262144, 2], P(('blk', 'shard')), may hold values from 0 to 2047
- rel_ids: int32 [262144], P(('blk', 'shard')), may hold values from 0 to 1344
- span_ids: int32 [256], P(('blk', 'shard')), may hold values from 0 to 1
Outputs:
- entity_grad: float32 [524288, 400], P(('blk', 'shard'))
- relation_grad: float32 [1345, 400], replicated
Inputs may be any that keep to these rules, and one draw needn't show every extreme that they name: Among the 1024 edges of one device no owner index is named by more than 64 edge ends; an edge's source and target owners differ; ends address rows of the devices with the same blk index.
All inputs are finite; a program needn't handle non-finite values.
Results may differ from a plain program's by a relative error of at most 0.0016.
Values may be sent and summed in bfloat16 or wider, within the bound.
No kernel may reach another device: no remote copies, remote signals or barrier semaphores. Data moves between devices by JAX's collectives and lax.ppermute only.
A program may use at most 128 MiB of HBM per device.

v0:
```python
import math

import jax
import jax.numpy as jnp
from jax import lax
from jax.sharding import PartitionSpec as P

NEG = 1024


def from_behind(value, axis, by):
    length = lax.axis_size(axis)
    return lax.ppermute(value, axis, [(i, (i + by) % length) for i in range(length)])


def score_span(query_bf, span, weight):
    neg_score = lax.dot_general(
        query_bf, span, (((1,), (1,)), ((), ())), preferred_element_type=jnp.float32
    )
    neg_grad = (weight * jax.nn.sigmoid(neg_score)).astype(jnp.bfloat16)
    query_part = jnp.dot(neg_grad, span, preferred_element_type=jnp.float32)
    span_part = lax.dot_general(
        neg_grad, query_bf, (((0,), (0,)), ((), ())), preferred_element_type=jnp.float32
    )
    return (query_part, span_part)


def shards(table, relation, owners, rows, rel_ids, span_ids):
    n_shard = lax.axis_size("shard")
    n_blk = lax.axis_size("blk")
    edges = owners.shape[0]
    rows_own = table.shape[0]
    width = table.shape[1]
    half = width // 2
    capacity = 4 * edges // n_shard
    negatives = NEG
    flat_owner = owners.reshape(-1)
    flat_row = rows.reshape(-1)
    onehot = (flat_owner[:, None] == jnp.arange(n_shard, dtype=jnp.int32)[None, :]).astype(
        jnp.int32
    )
    ranking = jnp.sum(jnp.cumsum(onehot, axis=0) * onehot, axis=1) - 1
    slots = flat_owner * capacity + ranking
    requests = (
        jnp.zeros((n_shard * capacity,), jnp.int32)
        .at[slots]
        .set(flat_row)
        .reshape(n_shard, capacity)
    )
    asked_rows = lax.all_to_all(requests, "shard", split_axis=0, concat_axis=0, tiled=True)
    fetched = lax.all_to_all(table[asked_rows], "shard", split_axis=0, concat_axis=0, tiled=True)
    gotten = fetched.reshape(n_shard * capacity, width)[slots].reshape(edges, 2, width)
    source = gotten[:, 0].astype(jnp.float32)
    target = gotten[:, 1].astype(jnp.float32)
    rel_rows = relation[rel_ids].astype(jnp.float32)
    s_re, s_im = (source[:, :half], source[:, half:])
    r_re, r_im = (rel_rows[:, :half], rel_rows[:, half:])
    query = jnp.concatenate([s_re * r_re - s_im * r_im, s_re * r_im + s_im * r_re], axis=1)
    pos_grad = jax.nn.sigmoid(jnp.sum(query * target, axis=1)) - 1.0
    query_bf = query.astype(jnp.bfloat16)
    weight = 1.0 / math.sqrt(n_blk * negatives)
    span_start = span_ids[0] * negatives
    span = lax.dynamic_slice_in_dim(table, span_start, negatives, 0)
    query_grad = pos_grad[:, None] * target
    carried = jnp.zeros((negatives, width), jnp.float32)
    for visit in range(n_blk):
        query_part, span_part = score_span(query_bf, span, weight)
        query_grad = query_grad + query_part
        carried = carried + span_part
        if visit + 1 < n_blk:
            span = from_behind(span, "blk", 1)
        carried = from_behind(carried, "blk", 1)
    q_re, q_im = (query_grad[:, :half], query_grad[:, half:])
    source_grad = jnp.concatenate([q_re * r_re + q_im * r_im, q_im * r_re - q_re * r_im], axis=1)
    rel_term = jnp.concatenate([q_re * s_re + q_im * s_im, q_im * s_re - q_re * s_im], axis=1)
    target_grad = pos_grad[:, None] * query
    local_relation = jnp.zeros((relation.shape[0], width), jnp.float32).at[rel_ids].add(rel_term)
    relation_grad = lax.psum(local_relation, ("blk", "shard"))
    end_grads = jnp.stack([source_grad, target_grad], axis=1).reshape(2 * edges, width)
    outgoing = jnp.zeros((n_shard * capacity, width), jnp.float32).at[slots].set(end_grads)
    arrived = lax.all_to_all(
        outgoing.reshape(n_shard, capacity, width), "shard", split_axis=0, concat_axis=0, tiled=True
    )
    entity_grad = (
        jnp.zeros((rows_own, width), jnp.float32)
        .at[asked_rows.reshape(-1)]
        .add(arrived.reshape(-1, width))
    )
    current = lax.dynamic_slice_in_dim(entity_grad, span_start, negatives, 0)
    entity_grad = lax.dynamic_update_slice_in_dim(entity_grad, current + carried, span_start, 0)
    return (entity_grad, relation_grad)


def solution(mesh):
    in_specs = (
        P(("blk", "shard"), None),
        P(),
        P(("blk", "shard"), None),
        P(("blk", "shard"), None),
        P(("blk", "shard")),
        P(("blk", "shard")),
    )
    out_specs = (P(("blk", "shard"), None), P())
    return jax.shard_map(shards, mesh=mesh, in_specs=in_specs, out_specs=out_specs, check_vma=False)
```

profile of v0, /device:TPU:1, one launch (start us, length us, event | category | flops | bytes accessed | tf_op | source)
XLA Modules:
  0.0 730.2 jit_solution(13740159022034079875)
XLA Ops:
  9.9 18.1 %reduce-window.6 = s32[64,16,128]{2,1,0:T(8,128)S(1)} reduce-window(s32[64,16,128]{2,1,0:T(8,128)S(1)} %fusion.14, s32[]{:T(128)} %constant.12.clone.1), window={size=1x1x128 pad=0_0x0_0x127_0}, to_apply=%region_0.0 | reduce-window | flops 16646144 | bytes 1048580 | tf_op jit(solution)/shard_map/reduce-window
  29.9 8.1 %scatter_custom_fusion = s32[4096]{0:T(1024)S(1)} fusion(s32[2048]{0:T(1024)S(1)} %bitcast.72, s32[2048]{0:T(1024)S(1)} %reshape.235, s32[]{:T(128)} %constant.12.clone.1), kind=kCustom, calls=%fused_computation.50 | custom fusion | bytes 16388 | tf_op jit(solution)/shard_map/scatter | solution.py:47
  38.6 13.2 %all-to-all-start = ((s32[64,1,64]{2,1,0:T(1,128)}), s32[64,1,64]{2,1,0:T(1,128)S(1)}, u32[]{:S(2)}, u32[]{:S(2)}) async-start(s32[64,1,64]{2,1,0:T(1,128)} %all_to_all.14), calls=%async_computation | async-start | bytes 65536 | tf_op jit(solution)/shard_map/all_to_all | solution.py:50
  51.8 2.8 copy.17
  54.6 6.4 all-to-all-done
  61.1 17.3 %gather_fusion = bf16[4096,400]{1,0:T(8,128)(2,1)} fusion(bf16[2048,400]{1,0:T(8,128)(2,1)S(1)} %copy.17, s32[4096]{0:T(1024)S(1)} %broadcast_clamp_fusion), kind=kCustom, calls=%fused_computation | custom fusion | bytes 6569984 | tf_op jit(solution)/shard_map/gather | solution.py:51
  78.4 5.8 all-to-all-start.1
  85.1 1.3 collective-permute-start
  86.4 19.3 %collective-permute-done = bf16[1024,400]{0,1:T(8,128)(2,1)} collective-permute-done((bf16[1024,400]{0,1:T(8,128)(2,1)S(1)}, bf16[1024,400]{0,1:T(8,128)(2,1)}, u32[]{:S(2)}, u32[]{:S(2)}) %collective-permute-start) | collective-permute-done | bytes 819232 | tf_op jit(solution)/shard_map/ppermute | solution.py:13
  106.6 4.0 gather_fusion.2
  111.0 1.3 convert_element_type.38
  112.4 13.0 %collective-permute-done.1 = bf16[1024,400]{0,1:T(8,128)(2,1)} collective-permute-done((bf16[1024,400]{0,1:T(8,128)(2,1)}, bf16[1024,400]{0,1:T(8,128)(2,1)}, u32[]{:S(2)}, u32[]{:S(2)}) %collective-permute-start.1) | collective-permute-done | bytes 819232 | tf_op jit(solution)/shard_map/ppermute | solution.py:13
  125.4 54.8 %all-to-all-done.1 = bf16[64,64,400]{2,1,0:T(8,128)(2,1)} async-done(((bf16[64,64,400]{2,1,0:T(8,128)(2,1)}), bf16[64,64,400]{2,1,0:T(8,128)(2,1)}, u32[]{:S(2)}, u32[]{:S(2)}) %all-to-all-start.1) | async-done | bytes 3276832 | tf_op jit(solution)/shard_map/all_to_all | solution.py:51
  180.1 12.0 %gather_fusion.1 = bf16[2048,400]{1,0:T(8,128)(2,1)} fusion(bf16[4096,400]{1,0:T(8,128)(2,1)} %bitcast.8, s32[2048]{0:T(1024)S(1)} %broadcast_clamp_fusion.1), kind=kCustom, calls=%fused_computation.1 | custom fusion | bytes 3284992 | tf_op jit(solution)/shard_map/gather | solution.py:52
  192.1 2.8 reshape.201
  195.0 4.2 fusion.17
  199.1 4.6 copy.30
  203.8 4.9 copy.29
  210.8 1.9 multiply_convert_fusion.3
  212.7 1.1 fusion.18
  214.0 3.0 multiply_convert_fusion.1
  217.1 3.7 multiply_convert_fusion.2
  220.8 3.6 multiply_convert_fusion
  224.4 2.8 fusion.20
  227.2 2.2 fusion.19
  229.5 2.3 fusion.8
  231.8 2.2 multiply_add_fusion
  234.9 4.6 copy.22
  239.4 6.2 reshape.243
  245.7 13.4 %scatter_custom_fusion.1 = f32[4096,400]{1,0:T(8,128)} fusion(s32[2048]{0:T(1024)S(1)} %bitcast.74, f32[2048,400]{1,0:T(8,128)} %reshape.243, f32[]{:T(128)} %constant.11.clone.1), kind=kCustom, calls=%fused_computation.11 | custom fusion | bytes 6554112 | tf_op jit(solution)/shard_map/scatter | solution.py:80
  259.0 6.3 all-to-all-start.2
  266.4 1.3 collective-permute-start.3
  267.7 36.9 %collective-permute-done.3 = f32[1024,400]{0,1:T(8,128)S(1)} collective-permute-done((f32[1024,400]{0,1:T(8,128)S(1)}, f32[1024,400]{0,1:T(8,128)S(1)}, u32[]{:S(2)}, u32[]{:S(2)}) %collective-permute-start.3) | collective-permute-done | bytes 1638432 | tf_op jit(solution)/shard_map/ppermute | solution.py:13
  306.8 36.3 %collective-permute-done.4 = f32[1024,400]{0,1:T(8,128)S(1)} collective-permute-done((f32[1024,400]{0,1:T(8,128)S(1)}, f32[1024,400]{0,1:T(8,128)S(1)}, u32[]{:S(2)}, u32[]{:S(2)}) %collective-permute-start.4) | collective-permute-done | bytes 1638432 | tf_op jit(solution)/shard_map/ppermute | solution.py:13
  343.6 1.0 fusion.23
  344.6 35.4 %collective-permute-done.5 = f32[1024,400]{0,1:T(8,128)S(1)} collective-permute-done((f32[1024,400]{0,1:T(8,128)S(1)}, f32[1024,400]{0,1:T(8,128)S(1)}, u32[]{:S(2)}, u32[]{:S(2)}) %collective-permute-start.5) | collective-permute-done | bytes 1638432 | tf_op jit(solution)/shard_map/ppermute | solution.py:13
  380.1 1.5 add.150
  381.9 1.8 copy.25
  383.7 8.9 %scatter_custom_fusion.3 = f32[1345,400]{1,0:T(8,128)} fusion(s32[1024]{0:T(1024)S(1)} %get-tuple-element.14, f32[1024,400]{1,0:T(8,128)} %copy.25, f32[]{:T(128)} %constant.11.clone.1), kind=kCustom, calls=%fused_computation.28 | custom fusion | flops 409600 | bytes 2152512 | tf_op jit(solution)/shard_map/scatter-add | solution.py:77
  394.0 280.9 %all-reduce.2.cloned.1.call-done = f32[1345,400]{1,0:T(8,128)} async-done(((f32[1345,400]{1,0:T(8,128)}), f32[1345,400]{1,0:T(8,128)}) %all-reduce.2.cloned.1.call-update) | async-done | bytes 2152016 | tf_op jit(solution)/shard_map/psum | solution.py:78
  674.9 3.3 copy.27
  678.1 29.3 %scatter_custom_fusion.2 = f32[2048,400]{1,0:T(8,128)} fusion(s32[4096]{0:T(1024)S(1)} %bitcast.76, f32[4096,400]{1,0:T(8,128)} %bitcast.17, f32[]{:T(128)} %constant.11.clone.1), kind=kCustom, calls=%fused_computation.14 | custom fusion | flops 1638400 | bytes 3277312 | tf_op jit(solution)/shard_map/scatter-add | solution.py:87
  707.5 1.8 constant_dynamic-slice_fusion
  709.2 1.7 copy.31
  710.9 3.5 add.151
  714.4 1.8 copy.24
  716.2 1.5 constant_dynamic-update-slice_fusion
  717.7 5.2 copy.26
  (90 shorter events, 15.2 us)
Async XLA Ops:
  9.9 19.4 %copy-start.11 = (s32[1024,2]{0,1:T(2,128)S(1)}, s32[1024,2]{0,1:T(2,128)}, u32[]{:S(2)}) copy-start(s32[1024,2]{0,1:T(2,128)} %param.9) | copy-start | bytes 24580
  38.6 22.4 %all-to-all-start = ((s32[64,1,64]{2,1,0:T(1,128)}), s32[64,1,64]{2,1,0:T(1,128)S(1)}, u32[]{:S(2)}, u32[]{:S(2)}) async-start(s32[64,1,64]{2,1,0:T(1,128)} %all_to_all.14), calls=%async_computation | async-start | bytes 65536 | tf_op jit(solution)/shard_map/all_to_all | solution.py:50
  78.4 6.6 copy-start.1
  78.4 101.8 %all-to-all-start.1 = ((bf16[64,64,400]{2,1,0:T(8,128)(2,1)}), bf16[64,64,400]{2,1,0:T(8,128)(2,1)}, u32[]{:S(2)}, u32[]{:S(2)}) async-start(bf16[64,64,400]{2,1,0:T(8,128)(2,1)} %bitcast.65), calls=%async_computation.1 | async-start | bytes 8388608 | tf_op jit(solution)/shard_map/all_to_all | solution.py:51
  84.2 21.4 %copy-start.6 = (bf16[1345,400]{0,1:T(8,128)(2,1)S(1)}, bf16[1345,400]{0,1:T(8,128)(2,1)}, u32[]{:S(2)}) copy-start(bf16[1345,400]{0,1:T(8,128)(2,1)} %param.7) | copy-start | bytes 3228004
  84.2 22.3 %copy-start.12 = (s32[1024]{0:T(1024)S(1)}, s32[1024]{0:T(1024)}, u32[]{:S(2)}) copy-start(s32[1024]{0:T(1024)} %param.10) | copy-start | bytes 12292
  85.1 20.6 %copy-start.9 = (bf16[1024,400]{0,1:T(8,128)(2,1)}, bf16[1024,400]{0,1:T(8,128)(2,1)S(1)}, u32[]{:S(2)}) copy-start(bf16[1024,400]{0,1:T(8,128)(2,1)S(1)} %constant_dynamic-slice_fusion.1) | copy-start | bytes 2457604
  85.1 20.5 %collective-permute-start = (bf16[1024,400]{0,1:T(8,128)(2,1)S(1)}, bf16[1024,400]{0,1:T(8,128)(2,1)}, u32[]{:S(2)}, u32[]{:S(2)}) collective-permute-start(bf16[1024,400]{0,1:T(8,128)(2,1)S(1)} %constant_dynamic-slice_fusion.1), channel_id=1, source_target_pairs={{0,64},{64,128},{128,192},{192,0},{1,65},{65,129},{129,193},{193,1... | collective-permute-start | bytes 2457608 | tf_op jit(solution)/shard_map/ppermute | solution.py:13
  105.6 19.8 %collective-permute-start.1 = (bf16[1024,400]{0,1:T(8,128)(2,1)}, bf16[1024,400]{0,1:T(8,128)(2,1)}, u32[]{:S(2)}, u32[]{:S(2)}) collective-permute-start(bf16[1024,400]{0,1:T(8,128)(2,1)} %collective-permute-done), channel_id=1, source_target_pairs={{0,64},{64,128},{128,192},{192,0},{1,65},{65,129},{129,193},{193,1... | collective-permute-start | bytes 2457608 | tf_op jit(solution)/shard_map/ppermute | solution.py:13
  125.4 95.4 %collective-permute-start.2 = (bf16[1024,400]{0,1:T(8,128)(2,1)}, bf16[1024,400]{0,1:T(8,128)(2,1)}, u32[]{:S(2)}, u32[]{:S(2)}) collective-permute-start(bf16[1024,400]{0,1:T(8,128)(2,1)} %collective-permute-done.1), channel_id=1, source_target_pairs={{0,64},{64,128},{128,192},{192,0},{1,65},{65,129},{129,193},{193,1... | collective-permute-start | bytes 2457608 | tf_op jit(solution)/shard_map/ppermute | solution.py:13
  203.8 5.1 copy-start
  209.4 1.4 copy-start.10
  209.5 11.3 %copy-start.7 = (bf16[1024,400]{0,1:T(8,128)(2,1)}, bf16[1024,400]{0,1:T(8,128)(2,1)S(1)}, u32[]{:S(2)}) copy-start(bf16[1024,400]{0,1:T(8,128)(2,1)S(1)} %fusion.11) | copy-start | bytes 2457604
  212.7 1.3 copy-start.17
  217.0 7.4 %copy-start.15 = (bf16[1024,1024]{1,0:T(8,128)(2,1)}, bf16[1024,1024]{1,0:T(8,128)(2,1)S(1)}, u32[]{:S(2)}) copy-start(bf16[1024,1024]{1,0:T(8,128)(2,1)S(1)} %multiply_convert_fusion.1) | copy-start | bytes 6291460
  220.7 6.5 copy-start.13
  224.4 5.1 copy-start.4
  259.0 6.3 copy-start.8
  259.0 6.3 copy-start.18
  259.0 419.1 %all-to-all-start.2 = ((f32[64,64,400]{2,1,0:T(8,128)}), f32[64,64,400]{2,1,0:T(8,128)}, u32[]{:S(2)}, u32[]{:S(2)}) async-start(f32[64,64,400]{2,1,0:T(8,128)} %bitcast.64), calls=%async_computation.2 | async-start | bytes 16777216 | tf_op jit(solution)/shard_map/all_to_all | solution.py:81
  265.3 409.6 %all-reduce.2.cloned.1.call-start = ((), (), s32[]{:S(2)}) async-start(), calls=%async_computation.3 | async-start | bytes 5537792 | tf_op jit(solution)/shard_map/psum | solution.py:78
  265.4 39.3 %copy-start.14 = (bf16[1024,1024]{1,0:T(8,128)(2,1)S(1)}, bf16[1024,1024]{1,0:T(8,128)(2,1)}, u32[]{:S(2)}) copy-start(bf16[1024,1024]{1,0:T(8,128)(2,1)} %copy-done.13) | copy-start | bytes 6291460
  266.4 39.4 %copy-start.16 = (bf16[1024,1024]{1,0:T(8,128)(2,1)S(1)}, bf16[1024,1024]{1,0:T(8,128)(2,1)}, u32[]{:S(2)}) copy-start(bf16[1024,1024]{1,0:T(8,128)(2,1)} %copy-done.15) | copy-start | bytes 6291460
  266.4 38.2 %collective-permute-start.3 = (f32[1024,400]{0,1:T(8,128)S(1)}, f32[1024,400]{0,1:T(8,128)S(1)}, u32[]{:S(2)}, u32[]{:S(2)}) collective-permute-start(f32[1024,400]{0,1:T(8,128)S(1)} %fusion.21), channel_id=1, source_target_pairs={{0,64},{64,128},{128,192},{192,0},{1,65},{65,129},{129,193},{193,1... | collective-permute-start | bytes 4915208 | tf_op jit(solution)/shard_map/ppermute | solution.py:13
  305.7 37.4 %collective-permute-start.4 = (f32[1024,400]{0,1:T(8,128)S(1)}, f32[1024,400]{0,1:T(8,128)S(1)}, u32[]{:S(2)}, u32[]{:S(2)}) collective-permute-start(f32[1024,400]{0,1:T(8,128)S(1)} %convolution_add_fusion), channel_id=1, source_target_pairs={{0,64},{64,128},{128,192},{192,0},{1,65},{65,129},{129,193},{193,1... | collective-permute-start | bytes 4915208 | tf_op jit(solution)/shard_map/ppermute | solution.py:13
  306.8 36.8 %copy-start.5 = (bf16[1024,1024]{1,0:T(8,128)(2,1)S(1)}, bf16[1024,1024]{1,0:T(8,128)(2,1)}, u32[]{:S(2)}) copy-start(bf16[1024,1024]{1,0:T(8,128)(2,1)} %copy-done.4) | copy-start | bytes 6291460
  343.5 36.6 %collective-permute-start.5 = (f32[1024,400]{0,1:T(8,128)S(1)}, f32[1024,400]{0,1:T(8,128)S(1)}, u32[]{:S(2)}, u32[]{:S(2)}) collective-permute-start(f32[1024,400]{0,1:T(8,128)S(1)} %add.149), channel_id=1, source_target_pairs={{0,64},{64,128},{128,192},{192,0},{1,65},{65,129},{129,193},{193,1... | collective-permute-start | bytes 4915208 | tf_op jit(solution)/shard_map/ppermute | solution.py:13
  344.6 37.2 %copy-start.2 = (f32[1024,200]{0,1:T(8,128)S(1)}, f32[1024,200]{0,1:T(8,128)}, u32[]{:S(2)}) copy-start(f32[1024,200]{0,1:T(8,128)} %get-tuple-element.4) | copy-start | bytes 2457604
  344.6 37.2 %copy-start.3 = (f32[1024,200]{0,1:T(8,128)S(1)}, f32[1024,200]{0,1:T(8,128)}, u32[]{:S(2)}) copy-start(f32[1024,200]{0,1:T(8,128)} %get-tuple-element.5) | copy-start | bytes 2457604
  381.5 329.4 %collective-permute-start.6 = (f32[1024,400]{0,1:T(8,128)}, f32[1024,400]{0,1:T(8,128)}, u32[]{:S(2)}, u32[]{:S(2)}) collective-permute-start(f32[1024,400]{0,1:T(8,128)} %add.150), channel_id=1, source_target_pairs={{0,64},{64,128},{128,192},{192,0},{1,65},{65,129},{129,193},{193,1... | collective-permute-start | bytes 4915208 | tf_op jit(solution)/shard_map/ppermute | solution.py:13
Sparse Core Ops, SparseCore 0:
  392.8 282.0 all-reduce.1
where the time goes:
time: 741 us; the launch traced here: 730 us
  waiting for transfers between devices  483 us (65%)
  local copies, waits for them, and re-layouts  109 us (15%)
  other arithmetic  69.3 us (9%)
  starting transfers between devices  28.3 us (4%)
  matrix products  24.7 us (3%)
  between operations  15.9 us (2%)
    psum x1, waiting for transfers between devices, shards(): relation_grad = lax.psum(local_relation, ('blk', 'shard'))  281 us
    ppermute x7, waiting for transfers between devices, from_behind(): lax.ppermute(value, axis, [(i, (i + by) % length) for i in range(length)])  141 us
    all_to_all x1, waiting for transfers between devices, shards(): lax.all_to_all(table[asked_rows], 'shard', split_axis=0, concat_axis=0, t...  54.8 us
    scatter-add x1, other arithmetic, shards(): entity_grad = jnp.zeros((rows_own, width), jnp.float32).at[asked_rows.res...  29.3 us
    unnamed x47, local copies, waits for them, and re-layouts  25.8 us
    another operation x3, other arithmetic  18.5 us
    gather x1, local copies, waits for them, and re-layouts, shards(): table[asked_rows]  17.3 us
  transfers between devices with their start and end apart: 11, of which 8 were waited for; matrix products, arithmetic and copies ran while one was open for 14% of the time, Pallas kernels for 0%

commit v1 on v0

--- a/solution.py
+++ b/solution.py
@@ -8,21 +8,22 @@
 NEG = 1024
 
 
-def from_behind(value, axis, by):
-    length = lax.axis_size(axis)
-    return lax.ppermute(value, axis, [(i, (i + by) % length) for i in range(length)])
+def spread(value, axis, n):
+    copies = jnp.broadcast_to(value[None], (n,) + value.shape)
+    return lax.all_to_all(copies, axis, 0, 0, tiled=False)
 
 
-def score_span(query_bf, span, weight):
-    neg_score = lax.dot_general(
-        query_bf, span, (((1,), (1,)), ((), ())), preferred_element_type=jnp.float32
-    )
-    neg_grad = (weight * jax.nn.sigmoid(neg_score)).astype(jnp.bfloat16)
-    query_part = jnp.dot(neg_grad, span, preferred_element_type=jnp.float32)
-    span_part = lax.dot_general(
-        neg_grad, query_bf, (((0,), (0,)), ((), ())), preferred_element_type=jnp.float32
-    )
-    return (query_part, span_part)
+def owner_rank(flat_owner, n_shard):
+    count = flat_owner.shape[0]
+    onehot = flat_owner[:, None] == jnp.arange(n_shard, dtype=jnp.int32)[None, :]
+    index = jnp.arange(count, dtype=jnp.int32)
+    earlier = (index[:, None] > index[None, :]).astype(jnp.bfloat16)
+    before = jnp.dot(earlier, onehot.astype(jnp.bfloat16), preferred_element_type=jnp.float32)
+    return jnp.sum(jnp.where(onehot, before, 0.0), axis=1).astype(jnp.int32)
+
+
+def reduce_relation(local_relation):
+    return lax.psum(local_relation, ("blk", "shard"))
 
 
 def shards(table, relation, owners, rows, rel_ids, span_ids):
@@ -34,12 +35,12 @@
     half = width // 2
     capacity = 4 * edges // n_shard
     negatives = NEG
+    span_start = span_ids[0] * negatives
+    span = lax.dynamic_slice_in_dim(table, span_start, negatives, 0)
+    spans = spread(span, "blk", n_blk).reshape(n_blk * negatives, width)
     flat_owner = owners.reshape(-1)
     flat_row = rows.reshape(-1)
-    onehot = (flat_owner[:, None] == jnp.arange(n_shard, dtype=jnp.int32)[None, :]).astype(
-        jnp.int32
-    )
-    ranking = jnp.sum(jnp.cumsum(onehot, axis=0) * onehot, axis=1) - 1
+    ranking = owner_rank(flat_owner, n_shard)
     slots = flat_owner * capacity + ranking
     requests = (
         jnp.zeros((n_shard * capacity,), jnp.int32)
@@ -59,23 +60,25 @@
     pos_grad = jax.nn.sigmoid(jnp.sum(query * target, axis=1)) - 1.0
     query_bf = query.astype(jnp.bfloat16)
     weight = 1.0 / math.sqrt(n_blk * negatives)
-    span_start = span_ids[0] * negatives
-    span = lax.dynamic_slice_in_dim(table, span_start, negatives, 0)
-    query_grad = pos_grad[:, None] * target
-    carried = jnp.zeros((negatives, width), jnp.float32)
-    for visit in range(n_blk):
-        query_part, span_part = score_span(query_bf, span, weight)
-        query_grad = query_grad + query_part
-        carried = carried + span_part
-        if visit + 1 < n_blk:
-            span = from_behind(span, "blk", 1)
-        carried = from_behind(carried, "blk", 1)
+    neg_score = lax.dot_general(
+        query_bf, spans, (((1,), (1,)), ((), ())), preferred_element_type=jnp.float32
+    )
+    neg_grad = (weight * jax.nn.sigmoid(neg_score)).astype(jnp.bfloat16)
+    query_grad = pos_grad[:, None] * target + jnp.dot(
+        neg_grad, spans, preferred_element_type=jnp.float32
+    )
+    span_part = lax.dot_general(
+        neg_grad, query_bf, (((0,), (0,)), ((), ())), preferred_element_type=jnp.float32
+    )
+    carried = lax.all_to_all(
+        span_part.reshape(n_blk, negatives, width), "blk", 0, 0, tiled=False
+    ).sum(axis=0)
     q_re, q_im = (query_grad[:, :half], query_grad[:, half:])
     source_grad = jnp.concatenate([q_re * r_re + q_im * r_im, q_im * r_re - q_re * r_im], axis=1)
     rel_term = jnp.concatenate([q_re * s_re + q_im * s_im, q_im * s_re - q_re * s_im], axis=1)
     target_grad = pos_grad[:, None] * query
     local_relation = jnp.zeros((relation.shape[0], width), jnp.float32).at[rel_ids].add(rel_term)
-    relation_grad = lax.psum(local_relation, ("blk", "shard"))
+    relation_grad = reduce_relation(local_relation)
     end_grads = jnp.stack([source_grad, target_grad], axis=1).reshape(2 * edges, width)
     outgoing = jnp.zeros((n_shard * capacity, width), jnp.float32).at[slots].set(end_grads)
     arrived = lax.all_to_all(

time: 741 us -> 703 us (0.949)
  waiting for transfers between devices: 483 us -> 448 us
  other arithmetic: 69.3 us -> 54.3 us
  local copies, waits for them, and re-layouts: 109 us -> 118 us
  starting transfers between devices: 28.3 us -> 37.3 us
    ppermute x7 -> x0, waiting for transfers between devices: 141 us -> none  [from_behind(): lax.ppermute(value, axis, [(i, (i + by) % length) for i in range(length)])]
    all_to_all x0 -> x2, waiting for transfers between devices: none -> 48.4 us  [the longest x1 30.2 us: shards(): lax.all_to_all(span_part.reshape(n_blk, negatives, width), 'blk', 0, 0, t...]
    all_to_all x1, waiting for transfers between devices: 54.8 us -> 84.8 us  [shards(): lax.all_to_all(table[asked_rows], 'shard', split_axis=0, concat_axis=0, t...]
    psum x1, waiting for transfers between devices: 281 us -> 306 us  [reduce_relation(): return lax.psum(local_relation, ('blk', 'shard'))]
    another operation x3 -> x0, other arithmetic: 18.5 us -> none
    all_to_all x0 -> x2, starting transfers between devices: none -> 10.2 us  [the longest x1 5.51 us: shards(): lax.all_to_all(span_part.reshape(n_blk, negatives, width), 'blk', 0, 0, t...]
    reshape x0 -> x2, local copies, waits for them, and re-layouts: none -> 7.71 us  [the longest x1 4.1 us: shards(): spans = spread(span, 'blk', n_blk).reshape(n_blk * negatives, width)]
    dot_general x12 -> x4, matrix products: 24.7 us -> 20.9 us  [the longest x1 8.1 us: shards(): jnp.dot(neg_grad, spans, preferred_element_type=jnp.float32)]
  transfers between devices with their start and end apart: 11 -> 6, of which waited for: 8 -> 5; matrix products, arithmetic and copies ran while one was open for 14% -> 14% of each run, Pallas kernels for 0% -> 0%
where the time goes in v1:
time: 703 us; the launch traced here: 694 us
  waiting for transfers between devices  448 us (64%)
  local copies, waits for them, and re-layouts  118 us (17%)
  other arithmetic  54.3 us (8%)
  starting transfers between devices  37.3 us (5%)
  matrix products  20.9 us (3%)
  between operations  15.5 us (2%)
    psum x1, waiting for transfers between devices, reduce_relation(): return lax.psum(local_relation, ('blk', 'shard'))  306 us
    all_to_all x1, waiting for transfers between devices, shards(): lax.all_to_all(table[asked_rows], 'shard', split_axis=0, concat_axis=0, t...  84.8 us
    all_to_all x1, waiting for transfers between devices, shards(): lax.all_to_all(span_part.reshape(n_blk, negatives, width), 'blk', 0, 0, t...  30.2 us
    unnamed x32, local copies, waits for them, and re-layouts  29.1 us
    scatter-add x1, other arithmetic, shards(): entity_grad = jnp.zeros((rows_own, width), jnp.float32).at[asked_rows.res...  27.8 us
    all_to_all x1, waiting for transfers between devices, spread(): return lax.all_to_all(copies, axis, 0, 0, tiled=False)  18.2 us
    gather x1, local copies, waits for them, and re-layouts, shards(): table[asked_rows]  17.4 us
  transfers between devices with their start and end apart: 6, of which 5 were waited for; matrix products, arithmetic and copies ran while one was open for 14% of the time, Pallas kernels for 0%

profile of v1, /device:TPU:1, one launch (start us, length us, event | category | flops | bytes accessed | tf_op | source)
XLA Modules:
  0.0 693.5 jit_solution(672101288420316935)
XLA Ops:
  7.2 0.7 broadcast_multiply_fusion
  7.9 0.9 copy.41
  9.3 0.9 copy.42
  10.8 1.7 fusion.11
  12.5 8.1 %scatter_custom_fusion = s32[4096]{0:T(1024)S(1)} fusion(s32[2048]{0:T(1024)S(1)} %bitcast.43, s32[2048]{0:T(1024)S(1)} %reshape.226, s32[]{:T(128)} %constant.11.clone.1), kind=kCustom, calls=%fused_computation.45 | custom fusion | bytes 16388 | tf_op jit(solution)/shard_map/scatter | solution.py:48
  21.3 13.2 %all-to-all-start = ((s32[64,1,64]{2,1,0:T(1,128)}), s32[64,1,64]{2,1,0:T(1,128)S(1)}, u32[]{:S(2)}, u32[]{:S(2)}) async-start(s32[64,1,64]{2,1,0:T(1,128)} %all_to_all.20), calls=%async_computation | async-start | bytes 65536 | tf_op jit(solution)/shard_map/all_to_all | solution.py:51
  35.2 8.5 %all-to-all-done = s32[64,1,64]{2,1,0:T(1,128)S(1)} async-done(((s32[64,1,64]{2,1,0:T(1,128)}), s32[64,1,64]{2,1,0:T(1,128)S(1)}, u32[]{:S(2)}, u32[]{:S(2)}) %all-to-all-start) | async-done | bytes 16416 | tf_op jit(solution)/shard_map/all_to_all | solution.py:51
  43.7 2.1 broadcast_in_dim.18
  45.8 4.7 all-to-all-start.2
  50.5 2.8 copy.43
  53.4 17.4 %gather_fusion = bf16[4096,400]{1,0:T(8,128)(2,1)} fusion(bf16[2048,400]{1,0:T(8,128)(2,1)S(1)} %copy.43, s32[4096]{0:T(1024)S(1)} %broadcast_clamp_fusion), kind=kCustom, calls=%fused_computation | custom fusion | bytes 6569984 | tf_op jit(solution)/shard_map/gather | solution.py:52
  70.8 18.2 %all-to-all-done.2 = bf16[4,1024,400]{1,2,0:T(8,128)(2,1)} async-done(((bf16[4,1024,400]{1,2,0:T(8,128)(2,1)}), bf16[4,1024,400]{1,2,0:T(8,128)(2,1)}, u32[]{:S(2)}, u32[]{:S(2)}) %all-to-all-start.2) | async-done | bytes 3276832 | tf_op jit(solution)/shard_map/all_to_all | solution.py:13
  89.0 7.1 %all-to-all-start.1 = ((bf16[64,64,400]{2,1,0:T(8,128)(2,1)}), bf16[64,64,400]{2,1,0:T(8,128)(2,1)}, u32[]{:S(2)}, u32[]{:S(2)}) async-start(bf16[64,64,400]{2,1,0:T(8,128)(2,1)} %bitcast.36), calls=%async_computation.1 | async-start | bytes 8388608 | tf_op jit(solution)/shard_map/all_to_all | solution.py:52
  96.0 0.9 copy.45
  97.0 4.0 gather_fusion.2
  101.4 1.4 convert_element_type.40
  102.9 4.1 copy.60
  107.0 84.8 %all-to-all-done.1 = bf16[64,64,400]{2,1,0:T(8,128)(2,1)} async-done(((bf16[64,64,400]{2,1,0:T(8,128)(2,1)}), bf16[64,64,400]{2,1,0:T(8,128)(2,1)}, u32[]{:S(2)}, u32[]{:S(2)}) %all-to-all-start.1) | async-done | bytes 3276832 | tf_op jit(solution)/shard_map/all_to_all | solution.py:52
  191.8 12.0 %gather_fusion.1 = bf16[2048,400]{1,0:T(8,128)(2,1)} fusion(bf16[4096,400]{1,0:T(8,128)(2,1)} %bitcast.5, s32[2048]{0:T(1024)S(1)} %broadcast_clamp_fusion.1), kind=kCustom, calls=%fused_computation.1 | custom fusion | bytes 3284992 | tf_op jit(solution)/shard_map/gather | solution.py:53
  203.8 2.8 reshape.190
  206.6 4.2 fusion.20
  210.8 6.0 copy.57
  216.8 1.3 bitcast_convert_fusion
  218.4 2.2 copy-done.6
  220.6 7.5 %multiply_convert_fusion = bf16[1024,4096]{1,0:T(8,128)(2,1)S(1)} fusion(bf16[4096,400]{0,1:T(8,128)(2,1)S(1)} %bitcast.41, f32[1024,200]{0,1:T(8,128)S(1)} %get-tuple-element.13, f32[1024,200]{0,1:T(8,128)S(1)} %get-tuple-element.12), kind=kOutput, calls=%fused_computation.7 | convolution fusion | flops 3378053120 | bytes 13303808 | tf_op jit(solution)/shard_map/dot_general | solution.py:63
  228.1 3.6 fusion.13
  231.8 3.6 copy.62
  235.4 5.5 all-to-all-start.4
  240.9 5.8 copy.58
  246.7 1.9 fusion.6
  248.6 8.1 %fusion.7 = f32[1024,400]{0,1:T(8,128)S(1)} fusion(bf16[1024,4096]{1,0:T(8,128)(2,1)} %copy-done.11, bf16[4096,400]{0,1:T(8,128)(2,1)} %bitcast.40, bf16[1024,1,400]{0,2,1:T(8,128)(2,1)} %copy.58, f32[1024]{0:T(1024)S(1)} %divide_add_fusion), kind=kOutput, calls=%fused_computation.21 | convolution fusion | flops 3356672000 | bytes 14127104 | tf_op jit(solution)/shard_map/dot_general | solution.py:67
  256.7 1.9 multiply_add_fusion
  258.8 1.0 copy-done.2
  260.6 4.5 copy.49
  265.1 6.2 reshape.234
  271.3 13.4 %scatter_custom_fusion.1 = f32[4096,400]{1,0:T(8,128)} fusion(s32[2048]{0:T(1024)S(1)} %bitcast.45, f32[2048,400]{1,0:T(8,128)} %reshape.234, f32[]{:T(128)} %constant.10.clone.1), kind=kCustom, calls=%fused_computation.11 | custom fusion | bytes 6554112 | tf_op jit(solution)/shard_map/scatter | solution.py:83
  284.6 30.2 %all-to-all-done.4 = f32[4,1024,400]{1,2,0:T(8,128)} async-done(((f32[4,1024,400]{1,2,0:T(8,128)}), f32[4,1024,400]{1,2,0:T(8,128)}, u32[]{:S(2)}, u32[]{:S(2)}) %all-to-all-start.4) | async-done | bytes 6553632 | tf_op jit(solution)/shard_map/all_to_all | solution.py:73
  314.8 6.5 all-to-all-start.3
  321.8 1.8 copy.53
  323.6 8.9 %scatter_custom_fusion.3 = f32[1345,400]{1,0:T(8,128)} fusion(s32[1024]{0:T(1024)S(1)} %get-tuple-element.18, f32[1024,400]{1,0:T(8,128)} %copy.53, f32[]{:T(128)} %constant.10.clone.1), kind=kCustom, calls=%fused_computation.26 | custom fusion | flops 409600 | bytes 2152512 | tf_op jit(solution)/shard_map/scatter-add | solution.py:80
  333.1 0.7 reduce.3
  333.9 305.9 %all-reduce.2.cloned.1.call-done = f32[1345,400]{1,0:T(8,128)} async-done(((f32[1345,400]{1,0:T(8,128)}), f32[1345,400]{1,0:T(8,128)}) %all-reduce.2.cloned.1.call-update) | async-done | bytes 2152016 | tf_op jit(solution)/shard_map/psum | solution.py:26
  639.8 3.3 copy.55
  643.0 4.9 reduce_sum.29
  648.0 1.8 copy.52
  649.8 27.8 %scatter_custom_fusion.2 = f32[2048,400]{1,0:T(8,128)} fusion(s32[4096]{0:T(1024)S(1)} %bitcast.47, f32[4096,400]{1,0:T(8,128)} %bitcast.14, f32[]{:T(128)} %constant.10.clone.1), kind=kCustom, calls=%fused_computation.16 | custom fusion | flops 1638400 | bytes 3277312 | tf_op jit(solution)/shard_map/scatter-add | solution.py:90
  677.7 3.4 add_dynamic-update-slice_fusion
  681.1 5.2 copy.54
  (48 shorter events, 4.9 us)
Async XLA Ops:
  10.8 24.3 %copy-start.5 = (bf16[2048,400]{0,1:T(8,128)(2,1)S(1)}, bf16[2048,400]{0,1:T(8,128)(2,1)}, u32[]{:S(2)}) copy-start(bf16[2048,400]{0,1:T(8,128)(2,1)} %param.6) | copy-start | bytes 4915204
  21.3 22.4 %all-to-all-start = ((s32[64,1,64]{2,1,0:T(1,128)}), s32[64,1,64]{2,1,0:T(1,128)S(1)}, u32[]{:S(2)}, u32[]{:S(2)}) async-start(s32[64,1,64]{2,1,0:T(1,128)} %all_to_all.20), calls=%async_computation | async-start | bytes 65536 | tf_op jit(solution)/shard_map/all_to_all | solution.py:51
  45.8 43.2 %all-to-all-start.2 = ((bf16[4,1024,400]{1,2,0:T(8,128)(2,1)}), bf16[4,1024,400]{1,2,0:T(8,128)(2,1)}, u32[]{:S(2)}, u32[]{:S(2)}) async-start(bf16[4,1024,400]{1,2,0:T(8,128)(2,1)} %broadcast_in_dim.18), calls=%async_computation.2 | async-start | bytes 6553600 | tf_op jit(solution)/shard_map/all_to_all | solution.py:13
  89.0 7.1 %copy-start.9 = (bf16[1345,400]{0,1:T(8,128)(2,1)S(1)}, bf16[1345,400]{0,1:T(8,128)(2,1)}, u32[]{:S(2)}) copy-start(bf16[1345,400]{0,1:T(8,128)(2,1)} %param.7) | copy-start | bytes 3228004
  89.0 8.0 %copy-start.10 = (s32[1024]{0:T(1024)S(1)}, s32[1024]{0:T(1024)}, u32[]{:S(2)}) copy-start(s32[1024]{0:T(1024)} %param.10) | copy-start | bytes 12292
  89.0 102.8 %all-to-all-start.1 = ((bf16[64,64,400]{2,1,0:T(8,128)(2,1)}), bf16[64,64,400]{2,1,0:T(8,128)(2,1)}, u32[]{:S(2)}, u32[]{:S(2)}) async-start(bf16[64,64,400]{2,1,0:T(8,128)(2,1)} %bitcast.36), calls=%async_computation.1 | async-start | bytes 8388608 | tf_op jit(solution)/shard_map/all_to_all | solution.py:52
  210.8 7.3 %copy-start = (f32[1024,400]{0,1:T(8,128)S(1)}, f32[1024,400]{0,1:T(8,128)}, u32[]{:S(2)}) copy-start(f32[1024,400]{0,1:T(8,128)} %convert_element_type.40) | copy-start | bytes 4915204
  218.1 2.5 copy-start.6
  218.4 9.7 %copy-start.1 = (f32[1024,200]{0,1:T(8,128)}, f32[1024,200]{0,1:T(8,128)S(1)}, u32[]{:S(2)}) copy-start(f32[1024,200]{0,1:T(8,128)S(1)} %get-tuple-element.12) | copy-start | bytes 2457604
  218.4 9.7 %copy-start.3 = (f32[1024,200]{0,1:T(8,128)}, f32[1024,200]{0,1:T(8,128)S(1)}, u32[]{:S(2)}) copy-start(f32[1024,200]{0,1:T(8,128)S(1)} %get-tuple-element.13) | copy-start | bytes 2457604
  228.1 3.7 copy-start.11
  235.4 79.4 %all-to-all-start.4 = ((f32[4,1024,400]{1,2,0:T(8,128)}), f32[4,1024,400]{1,2,0:T(8,128)}, u32[]{:S(2)}, u32[]{:S(2)}) async-start(f32[4,1024,400]{1,2,0:T(8,128)} %bitcast.35), calls=%async_computation.4 | async-start | bytes 13107200 | tf_op jit(solution)/shard_map/all_to_all | solution.py:73
  258.6 1.1 copy-start.2
  258.6 1.4 copy-start.4
  314.8 6.8 copy-start.7
  314.8 6.9 copy-start.8
  314.8 335.0 %all-to-all-start.3 = ((f32[64,64,400]{2,1,0:T(8,128)}), f32[64,64,400]{2,1,0:T(8,128)}, u32[]{:S(2)}, u32[]{:S(2)}) async-start(f32[64,64,400]{2,1,0:T(8,128)} %bitcast.34), calls=%async_computation.3 | async-start | bytes 16777216 | tf_op jit(solution)/shard_map/all_to_all | solution.py:84
  321.3 318.5 %all-reduce.2.cloned.1.call-start = ((), (), s32[]{:S(2)}) async-start(), calls=%async_computation.5 | async-start | bytes 5537792 | tf_op jit(solution)/shard_map/psum | solution.py:26
Sparse Core Ops, SparseCore 0:
  332.7 307.0 all-reduce.1

commit v2 on v1

--- a/solution.py
+++ b/solution.py
@@ -22,8 +22,20 @@
     return jnp.sum(jnp.where(onehot, before, 0.0), axis=1).astype(jnp.int32)
 
 
-def reduce_relation(local_relation):
-    return lax.psum(local_relation, ("blk", "shard"))
+def reduce_relation(local_relation, n_blk, n_shard):
+    rows, width = local_relation.shape
+    total = rows * width
+    lane = 128
+    per_peer = -(-total // (n_blk * n_shard * lane)) * lane
+    piece = n_shard * per_peer
+    flat = jnp.pad(local_relation.reshape(-1), (0, n_blk * piece - total))
+    parts = flat.reshape(n_blk, 8, piece // 8)
+    mine = lax.all_to_all(parts, "blk", 0, 0, tiled=False).sum(axis=0)
+    mine = mine.reshape(n_shard, per_peer)
+    small = lax.all_to_all(mine, "shard", 0, 0, tiled=False).sum(axis=0)
+    gathered = spread(small, "shard", n_shard).reshape(8, piece // 8)
+    whole = spread(gathered, "blk", n_blk)
+    return whole.reshape(-1)[:total].reshape(rows, width)
 
 
 def shards(table, relation, owners, rows, rel_ids, span_ids):
@@ -78,7 +90,7 @@
     rel_term = jnp.concatenate([q_re * s_re + q_im * s_im, q_im * s_re - q_re * s_im], axis=1)
     target_grad = pos_grad[:, None] * query
     local_relation = jnp.zeros((relation.shape[0], width), jnp.float32).at[rel_ids].add(rel_term)
-    relation_grad = reduce_relation(local_relation)
+    relation_grad = reduce_relation(local_relation, n_blk, n_shard)
     end_grads = jnp.stack([source_grad, target_grad], axis=1).reshape(2 * edges, width)
     outgoing = jnp.zeros((n_shard * capacity, width), jnp.float32).at[slots].set(end_grads)
     arrived = lax.all_to_all(

time: 703 us -> 679 us (0.966)
  waiting for transfers between devices: 448 us -> 363 us
  blocking collectives: 0 us -> 55.1 us
  between operations: 15.5 us -> 2.07 us
  local copies, waits for them, and re-layouts: 118 us -> 131 us
  starting transfers between devices: 37.3 us -> 50.3 us
    psum x1 -> x0, waiting for transfers between devices: 306 us -> none  [reduce_relation(): return lax.psum(local_relation, ('blk', 'shard'))]
    all_to_all x1, waiting for transfers between devices: 0.01 us -> 169 us  [shards(): lax.all_to_all(outgoing.reshape(n_shard, capacity, width), 'shard', split...]
    all_to_all x0 -> x2, blocking collectives: none -> 55.1 us  [the longest x1 31.1 us: reduce_relation(): mine = lax.all_to_all(parts, 'blk', 0, 0, tiled=False).sum(axis=0)]
    all_to_all x1, waiting for transfers between devices: 30.2 us -> 72.4 us  [shards(): lax.all_to_all(span_part.reshape(n_blk, negatives, width), 'blk', 0, 0, t...]
    all_to_all x1 -> x3, starting transfers between devices: 4.73 us -> 15.9 us  [spread(): return lax.all_to_all(copies, axis, 0, 0, tiled=False)]
    all_to_all x1 -> x3, waiting for transfers between devices: 18.2 us -> 28.2 us  [spread(): return lax.all_to_all(copies, axis, 0, 0, tiled=False)]
    reshape x0 -> x3, local copies, waits for them, and re-layouts: none -> 9.18 us  [the longest x1 3.96 us: reduce_relation(): return whole.reshape(-1)[:total].reshape(rows, width)]
    unnamed x32 -> x35, local copies, waits for them, and re-layouts: 29.1 us -> 26.1 us
  transfers between devices with their start and end apart: 6 -> 7, of which waited for: 5 -> 7; matrix products, arithmetic and copies ran while one was open for 14% -> 12% of each run, Pallas kernels for 0% -> 0%
where the time goes in v2:
time: 679 us; the launch traced here: 672 us
  waiting for transfers between devices  363 us (53%)
  local copies, waits for them, and re-layouts  131 us (19%)
  blocking collectives  55.1 us (8%)
  other arithmetic  52.4 us (8%)
  starting transfers between devices  50.3 us (7%)
  matrix products  18.7 us (3%)
    all_to_all x1, waiting for transfers between devices, shards(): lax.all_to_all(outgoing.reshape(n_shard, capacity, width), 'shard', split...  169 us
    all_to_all x1, waiting for transfers between devices, shards(): lax.all_to_all(table[asked_rows], 'shard', split_axis=0, concat_axis=0, t...  84.9 us
    all_to_all x1, waiting for transfers between devices, shards(): lax.all_to_all(span_part.reshape(n_blk, negatives, width), 'blk', 0, 0, t...  72.4 us
    all_to_all x1, blocking collectives, reduce_relation(): mine = lax.all_to_all(parts, 'blk', 0, 0, tiled=False).sum(axis=0)  31.1 us
    scatter-add x1, other arithmetic, shards(): entity_grad = jnp.zeros((rows_own, width), jnp.float32).at[asked_rows.res...  29 us
    all_to_all x3, waiting for transfers between devices, spread(): return lax.all_to_all(copies, axis, 0, 0, tiled=False)  28.2 us
    unnamed x35, local copies, waits for them, and re-layouts  26.1 us
    all_to_all x1, blocking collectives, reduce_relation(): small = lax.all_to_all(mine, 'shard', 0, 0, tiled=False).sum(axis=0)  24 us
  transfers between devices with their start and end apart: 7, of which 7 were waited for; matrix products, arithmetic and copies ran while one was open for 12% of the time, Pallas kernels for 0%

profile of v2, /device:TPU:1, one launch (start us, length us, event | category | flops | bytes accessed | tf_op | source)
XLA Modules:
  0.0 672.4 jit_solution(7645032176584790251)
XLA Ops:
  4.3 1.7 fusion.11
  6.0 8.1 %scatter_custom_fusion = s32[4096]{0:T(1024)S(1)} fusion(s32[2048]{0:T(1024)S(1)} %bitcast.46, s32[2048]{0:T(1024)S(1)} %reshape.254, s32[]{:T(128)} %constant.11.clone.1), kind=kCustom, calls=%fused_computation.45 | custom fusion | bytes 16388 | tf_op jit(solution)/shard_map/scatter | solution.py:60
  14.7 13.2 %all-to-all-start = ((s32[64,1,64]{2,1,0:T(1,128)}), s32[64,1,64]{2,1,0:T(1,128)S(1)}, u32[]{:S(2)}, u32[]{:S(2)}) async-start(s32[64,1,64]{2,1,0:T(1,128)} %all_to_all.36), calls=%async_computation | async-start | bytes 65536 | tf_op jit(solution)/shard_map/all_to_all | solution.py:63
  28.7 8.5 %all-to-all-done = s32[64,1,64]{2,1,0:T(1,128)S(1)} async-done(((s32[64,1,64]{2,1,0:T(1,128)}), s32[64,1,64]{2,1,0:T(1,128)S(1)}, u32[]{:S(2)}, u32[]{:S(2)}) %all-to-all-start) | async-done | bytes 16416 | tf_op jit(solution)/shard_map/all_to_all | solution.py:63
  37.1 2.1 broadcast_in_dim.24
  39.3 4.7 all-to-all-start.2
  44.0 2.8 copy.59
  46.8 17.4 %gather_fusion = bf16[4096,400]{1,0:T(8,128)(2,1)} fusion(bf16[2048,400]{1,0:T(8,128)(2,1)S(1)} %copy.59, s32[4096]{0:T(1024)S(1)} %broadcast_clamp_fusion), kind=kCustom, calls=%fused_computation | custom fusion | bytes 6569984 | tf_op jit(solution)/shard_map/gather | solution.py:64
  64.3 18.2 %all-to-all-done.2 = bf16[4,1024,400]{1,2,0:T(8,128)(2,1)} async-done(((bf16[4,1024,400]{1,2,0:T(8,128)(2,1)}), bf16[4,1024,400]{1,2,0:T(8,128)(2,1)}, u32[]{:S(2)}, u32[]{:S(2)}) %all-to-all-start.2) | async-done | bytes 3276832 | tf_op jit(solution)/shard_map/all_to_all | solution.py:13
  82.4 7.3 %all-to-all-start.1 = ((bf16[64,64,400]{2,1,0:T(8,128)(2,1)}), bf16[64,64,400]{2,1,0:T(8,128)(2,1)}, u32[]{:S(2)}, u32[]{:S(2)}) async-start(bf16[64,64,400]{2,1,0:T(8,128)(2,1)} %bitcast.38), calls=%async_computation.1 | async-start | bytes 8388608 | tf_op jit(solution)/shard_map/all_to_all | solution.py:64
  90.7 4.0 gather_fusion.2
  96.6 4.1 copy.77
  100.7 84.9 %all-to-all-done.1 = bf16[64,64,400]{2,1,0:T(8,128)(2,1)} async-done(((bf16[64,64,400]{2,1,0:T(8,128)(2,1)}), bf16[64,64,400]{2,1,0:T(8,128)(2,1)}, u32[]{:S(2)}, u32[]{:S(2)}) %all-to-all-start.1) | async-done | bytes 3276832 | tf_op jit(solution)/shard_map/all_to_all | solution.py:64
  185.6 12.0 %gather_fusion.1 = bf16[2048,400]{1,0:T(8,128)(2,1)} fusion(bf16[4096,400]{1,0:T(8,128)(2,1)} %bitcast.5, s32[2048]{0:T(1024)S(1)} %broadcast_clamp_fusion.1), kind=kCustom, calls=%fused_computation.1 | custom fusion | bytes 3284992 | tf_op jit(solution)/shard_map/gather | solution.py:65
  197.5 2.8 reshape.214
  200.4 4.2 fusion.20
  204.5 4.6 copy.75
  209.2 4.8 copy.74
  214.8 1.8 copy-done.7
  216.7 7.5 %multiply_convert_fusion = bf16[1024,4096]{1,0:T(8,128)(2,1)S(1)} fusion(bf16[4096,400]{0,1:T(8,128)(2,1)S(1)} %bitcast.43, f32[1024,200]{0,1:T(8,128)S(1)} %get-tuple-element.15, f32[1024,200]{0,1:T(8,128)S(1)} %get-tuple-element.14), kind=kOutput, calls=%fused_computation.7 | convolution fusion | flops 3378053120 | bytes 13303808 | tf_op jit(solution)/shard_map/dot_general | solution.py:75
  224.2 3.6 fusion.7
  227.8 1.8 multiply_add_fusion
  229.8 2.0 copy.69
  231.8 7.9 %scatter_custom_fusion.3 = f32[1345,400]{1,0:T(8,128)S(1)} fusion(s32[1024]{0:T(1024)S(1)} %get-tuple-element.20, f32[1024,400]{1,0:T(8,128)} %copy.69, f32[]{:T(128)} %constant.10.clone.1), kind=kCustom, calls=%fused_computation.26 | custom fusion | flops 409600 | bytes 2152512 | tf_op jit(solution)/shard_map/scatter-add | solution.py:92
  239.7 3.7 reshape.220
  243.4 1.8 pad.4
  246.7 31.1 %all_to_all.58 = f32[4,8,17408]{2,1,0:T(8,128)S(1)} all-to-all(f32[4,8,17408]{2,1,0:T(8,128)} %reshape.221), channel_id=1, replica_groups=mesh['blk'=4,'shard'=64] {'blk'}, dimensions={0} | all-to-all | bytes 4456448 | tf_op jit(solution)/shard_map/all_to_all | solution.py:33
  278.6 24.0 %all_to_all.59 = f32[64,1,2176]{2,1,0:T(1,128)S(1)} all-to-all(f32[64,1,2176]{2,1,0:T(1,128)S(1)} %all_to_all.48), channel_id=1, replica_groups=mesh['blk'=4,'shard'=64] {'shard'}, dimensions={0} | all-to-all | bytes 1114112 | tf_op jit(solution)/shard_map/all_to_all | solution.py:35
  304.0 6.6 all-to-all-start.7
  310.6 5.9 fusion.13
  316.6 3.6 copy.80
  320.1 8.4 %all-to-all-done.7 = f32[64,1,2176]{2,1,0:T(1,128)S(1)} async-done(((f32[64,1,2176]{2,1,0:T(1,128)}), f32[64,1,2176]{2,1,0:T(1,128)S(1)}, u32[]{:S(2)}, u32[]{:S(2)}) %all-to-all-start.7) | async-done | bytes 557088 | tf_op jit(solution)/shard_map/all_to_all | solution.py:13
  328.6 5.3 all-to-all-start.4
  335.3 72.4 %all-to-all-done.4 = f32[4,1024,400]{1,2,0:T(8,128)} async-done(((f32[4,1024,400]{1,2,0:T(8,128)}), f32[4,1024,400]{1,2,0:T(8,128)}, u32[]{:S(2)}, u32[]{:S(2)}) %all-to-all-start.4) | async-done | bytes 6553632 | tf_op jit(solution)/shard_map/all_to_all | solution.py:85
  409.2 4.6 all-to-all-start.8
  414.7 4.6 copy.65
  419.3 6.2 reshape.262
  425.5 13.3 %scatter_custom_fusion.1 = f32[4096,400]{1,0:T(8,128)} fusion(s32[2048]{0:T(1024)S(1)} %bitcast.48, f32[2048,400]{1,0:T(8,128)} %reshape.262, f32[]{:T(128)} %constant.10.clone.1), kind=kCustom, calls=%fused_computation.11 | custom fusion | bytes 6554112 | tf_op jit(solution)/shard_map/scatter | solution.py:95
  440.4 8.6 %all-to-all-start.3 = ((f32[64,64,400]{2,1,0:T(8,128)}), f32[64,64,400]{2,1,0:T(8,128)}, u32[]{:S(2)}, u32[]{:S(2)}) async-start(f32[64,64,400]{2,1,0:T(8,128)} %bitcast.36), calls=%async_computation.3 | async-start | bytes 16777216 | tf_op jit(solution)/shard_map/all_to_all | solution.py:96
  450.4 3.8 reduce_sum.47
  454.1 1.8 copy.68
  455.9 2.0 copy.78
  459.4 4.0 reshape.223
  463.4 2.1 copy.72
  465.5 169.1 %all-to-all-done.3 = f32[64,64,400]{2,1,0:T(8,128)} async-done(((f32[64,64,400]{2,1,0:T(8,128)}), f32[64,64,400]{2,1,0:T(8,128)}, u32[]{:S(2)}, u32[]{:S(2)}) %all-to-all-start.3) | async-done | bytes 6553632 | tf_op jit(solution)/shard_map/all_to_all | solution.py:96
  634.6 29.0 %scatter_custom_fusion.2 = f32[2048,400]{1,0:T(8,128)} fusion(s32[4096]{0:T(1024)S(1)} %bitcast.50, f32[4096,400]{1,0:T(8,128)} %bitcast.14, f32[]{:T(128)} %constant.10.clone.1), kind=kCustom, calls=%fused_computation.16 | custom fusion | flops 1638400 | bytes 3277312 | tf_op jit(solution)/shard_map/scatter-add | solution.py:102
  663.6 3.4 add_dynamic-update-slice_fusion
  666.9 5.2 copy.71
  (66 shorter events, 20.3 us)
Async XLA Ops:
  4.3 24.3 %copy-start.6 = (bf16[2048,400]{0,1:T(8,128)(2,1)S(1)}, bf16[2048,400]{0,1:T(8,128)(2,1)}, u32[]{:S(2)}) copy-start(bf16[2048,400]{0,1:T(8,128)(2,1)} %param.6) | copy-start | bytes 4915204
  14.7 22.4 %all-to-all-start = ((s32[64,1,64]{2,1,0:T(1,128)}), s32[64,1,64]{2,1,0:T(1,128)S(1)}, u32[]{:S(2)}, u32[]{:S(2)}) async-start(s32[64,1,64]{2,1,0:T(1,128)} %all_to_all.36), calls=%async_computation | async-start | bytes 65536 | tf_op jit(solution)/shard_map/all_to_all | solution.py:63
  39.3 43.2 %all-to-all-start.2 = ((bf16[4,1024,400]{1,2,0:T(8,128)(2,1)}), bf16[4,1024,400]{1,2,0:T(8,128)(2,1)}, u32[]{:S(2)}, u32[]{:S(2)}) async-start(bf16[4,1024,400]{1,2,0:T(8,128)(2,1)} %broadcast_in_dim.24), calls=%async_computation.2 | async-start | bytes 6553600 | tf_op jit(solution)/shard_map/all_to_all | solution.py:13
  82.4 7.4 %copy-start.10 = (bf16[1345,400]{0,1:T(8,128)(2,1)S(1)}, bf16[1345,400]{0,1:T(8,128)(2,1)}, u32[]{:S(2)}) copy-start(bf16[1345,400]{0,1:T(8,128)(2,1)} %param.7) | copy-start | bytes 3228004
  82.4 8.3 %copy-start.11 = (s32[1024]{0:T(1024)S(1)}, s32[1024]{0:T(1024)}, u32[]{:S(2)}) copy-start(s32[1024]{0:T(1024)} %param.10) | copy-start | bytes 12292
  82.4 103.1 %all-to-all-start.1 = ((bf16[64,64,400]{2,1,0:T(8,128)(2,1)}), bf16[64,64,400]{2,1,0:T(8,128)(2,1)}, u32[]{:S(2)}, u32[]{:S(2)}) async-start(bf16[64,64,400]{2,1,0:T(8,128)(2,1)} %bitcast.38), calls=%async_computation.1 | async-start | bytes 8388608 | tf_op jit(solution)/shard_map/all_to_all | solution.py:64
  209.2 5.0 copy-start
  214.1 2.5 copy-start.7
  214.5 9.7 %copy-start.2 = (f32[1024,200]{0,1:T(8,128)}, f32[1024,200]{0,1:T(8,128)S(1)}, u32[]{:S(2)}) copy-start(f32[1024,200]{0,1:T(8,128)S(1)} %get-tuple-element.14) | copy-start | bytes 2457604
  214.5 9.7 %copy-start.4 = (f32[1024,200]{0,1:T(8,128)}, f32[1024,200]{0,1:T(8,128)S(1)}, u32[]{:S(2)}) copy-start(f32[1024,200]{0,1:T(8,128)S(1)} %get-tuple-element.15) | copy-start | bytes 2457604
  224.2 3.6 copy-start.12
  277.9 32.7 %copy-start.3 = (f32[1024,200]{0,1:T(8,128)S(1)}, f32[1024,200]{0,1:T(8,128)}, u32[]{:S(2)}) copy-start(f32[1024,200]{0,1:T(8,128)} %copy-done.2) | copy-start | bytes 2457604
  277.9 32.7 %copy-start.5 = (f32[1024,200]{0,1:T(8,128)S(1)}, f32[1024,200]{0,1:T(8,128)}, u32[]{:S(2)}) copy-start(f32[1024,200]{0,1:T(8,128)} %copy-done.4) | copy-start | bytes 2457604
  304.0 24.5 %all-to-all-start.7 = ((f32[64,1,2176]{2,1,0:T(1,128)}), f32[64,1,2176]{2,1,0:T(1,128)S(1)}, u32[]{:S(2)}, u32[]{:S(2)}) async-start(f32[64,1,2176]{2,1,0:T(1,128)} %broadcast_in_dim.26), calls=%async_computation.7 | async-start | bytes 1114112 | tf_op jit(solution)/shard_map/all_to_all | solution.py:13
  328.6 79.2 %all-to-all-start.4 = ((f32[4,1024,400]{1,2,0:T(8,128)}), f32[4,1024,400]{1,2,0:T(8,128)}, u32[]{:S(2)}, u32[]{:S(2)}) async-start(f32[4,1024,400]{1,2,0:T(8,128)} %bitcast.37), calls=%async_computation.4 | async-start | bytes 13107200 | tf_op jit(solution)/shard_map/all_to_all | solution.py:85
  409.2 4.6 copy-start.8
  409.2 4.6 copy-start.9
  409.2 31.2 %all-to-all-start.8 = ((f32[4,8,17408]{2,1,0:T(8,128)}), f32[4,8,17408]{2,1,0:T(8,128)}, u32[]{:S(2)}, u32[]{:S(2)}) async-start(f32[4,8,17408]{2,1,0:T(8,128)} %broadcast_in_dim.54), calls=%async_computation.8 | async-start | bytes 4456448 | tf_op jit(solution)/shard_map/all_to_all | solution.py:13
  440.4 194.1 %all-to-all-start.3 = ((f32[64,64,400]{2,1,0:T(8,128)}), f32[64,64,400]{2,1,0:T(8,128)}, u32[]{:S(2)}, u32[]{:S(2)}) async-start(f32[64,64,400]{2,1,0:T(8,128)} %bitcast.36), calls=%async_computation.3 | async-start | bytes 16777216 | tf_op jit(solution)/shard_map/all_to_all | solution.py:96
  465.5 198.0 %copy-start.1 = (f32[1024,400]{1,0:T(8,128)S(1)}, f32[1024,400]{1,0:T(8,128)}, u32[]{:S(2)}) copy-start(f32[1024,400]{1,0:T(8,128)} %copy.68) | copy-start | bytes 4915204

commit v3 on v1

--- a/solution.py
+++ b/solution.py
@@ -6,6 +6,11 @@
 from jax.sharding import PartitionSpec as P
 
 NEG = 1024
+LANE = 128
+
+
+def shifted(value, axis, n, by):
+    return lax.ppermute(value, axis, [(i, (i + by) % n) for i in range(n)])
 
 
 def spread(value, axis, n):
@@ -22,13 +27,10 @@
     return jnp.sum(jnp.where(onehot, before, 0.0), axis=1).astype(jnp.int32)
 
 
-def reduce_relation(local_relation):
-    return lax.psum(local_relation, ("blk", "shard"))
-
-
 def shards(table, relation, owners, rows, rel_ids, span_ids):
     n_shard = lax.axis_size("shard")
     n_blk = lax.axis_size("blk")
+    me_blk = lax.axis_index("blk")
     edges = owners.shape[0]
     rows_own = table.shape[0]
     width = table.shape[1]
@@ -37,7 +39,9 @@
     negatives = NEG
     span_start = span_ids[0] * negatives
     span = lax.dynamic_slice_in_dim(table, span_start, negatives, 0)
-    spans = spread(span, "blk", n_blk).reshape(n_blk * negatives, width)
+    spans = jnp.concatenate(
+        [span] + [shifted(span, "blk", n_blk, d) for d in range(1, n_blk)], axis=0
+    )
     flat_owner = owners.reshape(-1)
     flat_row = rows.reshape(-1)
     ranking = owner_rank(flat_owner, n_shard)
@@ -69,25 +73,46 @@
     )
     span_part = lax.dot_general(
         neg_grad, query_bf, (((0,), (0,)), ((), ())), preferred_element_type=jnp.float32
-    )
-    carried = lax.all_to_all(
-        span_part.reshape(n_blk, negatives, width), "blk", 0, 0, tiled=False
-    ).sum(axis=0)
+    ).reshape(n_blk, negatives, width)
+    carried = span_part[0]
+    for d in range(1, n_blk):
+        carried = carried + shifted(span_part[d], "blk", n_blk, -d)
     q_re, q_im = (query_grad[:, :half], query_grad[:, half:])
     source_grad = jnp.concatenate([q_re * r_re + q_im * r_im, q_im * r_re - q_re * r_im], axis=1)
     rel_term = jnp.concatenate([q_re * s_re + q_im * s_im, q_im * s_re - q_re * s_im], axis=1)
     target_grad = pos_grad[:, None] * query
-    local_relation = jnp.zeros((relation.shape[0], width), jnp.float32).at[rel_ids].add(rel_term)
-    relation_grad = reduce_relation(local_relation)
+
+    rel_rows_n = relation.shape[0]
+    total = rel_rows_n * width
+    per_peer = -(-total // (n_blk * n_shard * LANE)) * LANE
+    local_relation = jnp.zeros((rel_rows_n, width), jnp.float32).at[rel_ids].add(rel_term)
+    quarters = jnp.pad(local_relation.reshape(-1), (0, n_blk * n_shard * per_peer - total))
+    quarters = quarters.reshape(n_blk, n_shard, per_peer)
+    mine = lax.dynamic_index_in_dim(quarters, me_blk, 0, keepdims=False)
+    for d in range(1, n_blk):
+        outgoing_quarter = lax.dynamic_index_in_dim(quarters, (me_blk + d) % n_blk, 0, keepdims=False)
+        mine = mine + shifted(outgoing_quarter, "blk", n_blk, d)
+
+    sub = 8
+    grad_lanes = capacity * width // sub
+    rel_lanes = -(-per_peer // (sub * LANE)) * LANE
     end_grads = jnp.stack([source_grad, target_grad], axis=1).reshape(2 * edges, width)
     outgoing = jnp.zeros((n_shard * capacity, width), jnp.float32).at[slots].set(end_grads)
-    arrived = lax.all_to_all(
-        outgoing.reshape(n_shard, capacity, width), "shard", split_axis=0, concat_axis=0, tiled=True
-    )
+    rel_out = jnp.pad(mine, ((0, 0), (0, sub * rel_lanes - per_peer))).reshape(n_shard, sub, rel_lanes)
+    payload = jnp.concatenate([outgoing.reshape(n_shard, sub, grad_lanes), rel_out], axis=2)
+    arrived = lax.all_to_all(payload, "shard", split_axis=0, concat_axis=0, tiled=True)
+    arrived_grads = arrived[:, :, :grad_lanes].reshape(n_shard * capacity, width)
+    piece = arrived[:, :, grad_lanes:].reshape(n_shard, sub * rel_lanes)[:, :per_peer].sum(axis=0)
+
+    quarter = spread(piece, "shard", n_shard)
+    held = jnp.stack([quarter] + [shifted(quarter, "blk", n_blk, d) for d in range(1, n_blk)])
+    order = (me_blk - jnp.arange(n_blk, dtype=jnp.int32)) % n_blk
+    relation_grad = jnp.take(held, order, axis=0).reshape(-1)[:total].reshape(rel_rows_n, width)
+
     entity_grad = (
         jnp.zeros((rows_own, width), jnp.float32)
         .at[asked_rows.reshape(-1)]
-        .add(arrived.reshape(-1, width))
+        .add(arrived_grads)
     )
     current = lax.dynamic_slice_in_dim(entity_grad, span_start, negatives, 0)
     entity_grad = lax.dynamic_update_slice_in_dim(entity_grad, current + carried, span_start, 0)

time: 703 us -> 560 us (0.80)
  waiting for transfers between devices: 448 us -> 250 us
  local copies, waits for them, and re-layouts: 118 us -> 166 us
  between operations: 15.5 us -> 2.42 us
  starting transfers between devices: 37.3 us -> 47.2 us
  other arithmetic: 54.3 us -> 61.5 us
    psum x1 -> x0, waiting for transfers between devices: 306 us -> none  [reduce_relation(): return lax.psum(local_relation, ('blk', 'shard'))]
    all_to_all x2 -> x1, waiting for transfers between devices: 30.2 us -> 150 us  [shards(): lax.all_to_all(payload, 'shard', split_axis=0, concat_axis=0, tiled=True)]
    reshape x2 -> x5, local copies, waits for them, and re-layouts: 7.71 us -> 31.3 us  [the longest x1 11.8 us: shards(): arrived[:, :, :grad_lanes].reshape(n_shard * capacity, width)]
    all_to_all x1, waiting for transfers between devices: 18.2 us -> 0.01 us  [spread(): return lax.all_to_all(copies, axis, 0, 0, tiled=False)]
    ppermute x0 -> x12, starting transfers between devices: none -> 15.7 us  [shifted(): return lax.ppermute(value, axis, [(i, (i + by) % n) for i in range(n)])]
    slice x0 -> x4, local copies, waits for them, and re-layouts: none -> 12.9 us  [the longest x1 6.08 us: shards(): arrived[:, :, :grad_lanes].reshape(n_shard * capacity, width)]
    ppermute x0 -> x12, waiting for transfers between devices: none -> 9.57 us  [shifted(): return lax.ppermute(value, axis, [(i, (i + by) % n) for i in range(n)])]
    add x1 -> x3, other arithmetic: 1.89 us -> 9.05 us  [the longest x1 5.63 us: shards(): current + carried]
  transfers between devices with their start and end apart: 6 -> 16, of which waited for: 5 -> 4; matrix products, arithmetic and copies ran while one was open for 14% -> 28% of each run, Pallas kernels for 0% -> 0%
where the time goes in v3:
time: 560 us; the launch traced here: 551 us
  waiting for transfers between devices  250 us (45%)
  local copies, waits for them, and re-layouts  166 us (30%)
  other arithmetic  61.5 us (11%)
  starting transfers between devices  47.2 us (8%)
  matrix products  25.2 us (4%)
    all_to_all x1, waiting for transfers between devices, shards(): lax.all_to_all(payload, 'shard', split_axis=0, concat_axis=0, tiled=True)  150 us
    all_to_all x1, waiting for transfers between devices, shards(): lax.all_to_all(table[asked_rows], 'shard', split_axis=0, concat_axis=0, t...  83.3 us
    unnamed x44, local copies, waits for them, and re-layouts  28.7 us
    scatter-add x1, other arithmetic, shards(): entity_grad = jnp.zeros((rows_own, width), jnp.float32).at[asked_rows.res...  28.4 us
    gather x1, local copies, waits for them, and re-layouts, shards(): table[asked_rows]  17.4 us
    ppermute x12, starting transfers between devices, shifted(): return lax.ppermute(value, axis, [(i, (i + by) % n) for i in range(n)])  15.7 us
    scatter x1, local copies, waits for them, and re-layouts, shards(): jnp.zeros((n_shard * capacity, width), jnp.float32).at[slots].set(end_grads)  13.5 us
    all_to_all x1, starting transfers between devices, shards(): lax.all_to_all(requests, 'shard', split_axis=0, concat_axis=0, tiled=True)  13.2 us
  transfers between devices with their start and end apart: 16, of which 4 were waited for; matrix products, arithmetic and copies ran while one was open for 28% of the time, Pallas kernels for 0%

profile of v3, /device:TPU:1, one launch (start us, length us, event | category | flops | bytes accessed | tf_op | source)
XLA Modules:
  0.0 551.3 jit_solution(1205079751427363066)
XLA Ops:
  6.0 8.1 %scatter_custom_fusion = s32[4096]{0:T(1024)S(1)} fusion(s32[2048]{0:T(1024)S(1)} %bitcast.63, s32[2048]{0:T(1024)S(1)} %reshape.320, s32[]{:T(128)} %constant.80.clone.1), kind=kCustom, calls=%fused_computation.61 | custom fusion | bytes 16388 | tf_op jit(solution)/shard_map/scatter | solution.py:52
  14.7 13.2 %all-to-all-start = ((s32[64,1,64]{2,1,0:T(1,128)}), s32[64,1,64]{2,1,0:T(1,128)S(1)}, u32[]{:S(2)}, u32[]{:S(2)}) async-start(s32[64,1,64]{2,1,0:T(1,128)} %all_to_all.20), calls=%async_computation | async-start | bytes 65536 | tf_op jit(solution)/shard_map/all_to_all | solution.py:55
  27.9 2.8 copy.14
  30.7 6.4 %all-to-all-done = s32[64,1,64]{2,1,0:T(1,128)S(1)} async-done(((s32[64,1,64]{2,1,0:T(1,128)}), s32[64,1,64]{2,1,0:T(1,128)S(1)}, u32[]{:S(2)}, u32[]{:S(2)}) %all-to-all-start) | async-done | bytes 16416 | tf_op jit(solution)/shard_map/all_to_all | solution.py:55
  37.2 17.4 %gather_fusion = bf16[4096,400]{1,0:T(8,128)(2,1)} fusion(bf16[2048,400]{1,0:T(8,128)(2,1)S(1)} %copy.14, s32[4096]{0:T(1024)S(1)} %broadcast_clamp_fusion), kind=kCustom, calls=%fused_computation | custom fusion | bytes 6569984 | tf_op jit(solution)/shard_map/gather | solution.py:56
  54.6 5.8 %all-to-all-start.1 = ((bf16[64,64,400]{2,1,0:T(8,128)(2,1)}), bf16[64,64,400]{2,1,0:T(8,128)(2,1)}, u32[]{:S(2)}, u32[]{:S(2)}) async-start(bf16[64,64,400]{2,1,0:T(8,128)(2,1)} %bitcast.50), calls=%async_computation.1 | async-start | bytes 8388608 | tf_op jit(solution)/shard_map/all_to_all | solution.py:56
  62.2 2.5 collective-permute-start.2
  67.2 4.0 gather_fusion.2
  73.1 83.3 %all-to-all-done.1 = bf16[64,64,400]{2,1,0:T(8,128)(2,1)} async-done(((bf16[64,64,400]{2,1,0:T(8,128)(2,1)}), bf16[64,64,400]{2,1,0:T(8,128)(2,1)}, u32[]{:S(2)}, u32[]{:S(2)}) %all-to-all-start.1) | async-done | bytes 3276832 | tf_op jit(solution)/shard_map/all_to_all | solution.py:56
  156.4 12.0 %gather_fusion.1 = bf16[2048,400]{1,0:T(8,128)(2,1)} fusion(bf16[4096,400]{1,0:T(8,128)(2,1)} %bitcast.5, s32[2048]{0:T(1024)S(1)} %broadcast_clamp_fusion.1), kind=kCustom, calls=%fused_computation.1 | custom fusion | bytes 3284992 | tf_op jit(solution)/shard_map/gather | solution.py:57
  168.3 2.8 reshape.273
  171.2 4.2 fusion.31
  175.3 5.8 %copy.27 = bf16[1024,1,400]{0,2,1:T(8,128)(2,1)} copy(bf16[1024,1,400]{2,1,0:T(2,128)(2,1)} %get-tuple-element.17) | data formatting | bytes 1638400
  182.5 5.8 %copy.28 = bf16[1024,1,400]{0,2,1:T(8,128)(2,1)} copy(bf16[1024,1,400]{2,1,0:T(2,128)(2,1)} %get-tuple-element.16) | data formatting | bytes 1638400
  189.8 9.2 %multiply_convert_fusion = bf16[1024,4096]{1,0:T(8,128)(2,1)S(1)} fusion(bf16[1024,400]{0,1:T(8,128)(2,1)} %collective-permute-done.2, bf16[1024,400]{0,1:T(8,128)(2,1)} %collective-permute-done.1, bf16[1024,400]{0,1:T(8,128)(2,1)} %collective-permute-done, bf16[1024,400]{0,1:T(8,128)(2,1)} %constant_dynamic-slice_fusion.1, ...), kind=kOutput, calls=%fused_computation.8 | convolution fusion | flops 3391160320 | bytes 13303808 | tf_op jit(solution)/shard_map/dot_general | solution.py:67
  199.0 8.4 %fusion.7 = f32[1024,400]{0,1:T(8,128)S(1)} fusion(bf16[1024,4096]{1,0:T(8,128)(2,1)S(1)} %multiply_convert_fusion, bf16[1024,1,400]{0,2,1:T(8,128)(2,1)S(1)} %copy-done.10, f32[1024]{0:T(1024)S(1)} %divide_add_fusion, bf16[1024,400]{0,1:T(8,128)(2,1)} %collective-permute-done.2, bf16[1024,400]{0,1:T(8,128)(2,1)} %collective-permute-done.1, ...), kind=kOutput, calls=%fused_computation.23 | convolution fusion | flops 3369779200 | bytes 14127104 | tf_op jit(solution)/shard_map/dot_general | solution.py:71
  207.4 1.8 multiply_add_fusion.1
  209.4 1.8 copy.20
  211.1 8.1 %scatter_custom_fusion.2 = f32[1345,400]{1,0:T(8,128)S(1)} fusion(s32[1024]{0:T(1024)S(1)} %get-tuple-element.23, f32[1024,400]{1,0:T(8,128)} %copy.20, f32[]{:T(128)} %constant.79.clone.1), kind=kCustom, calls=%fused_computation.32 | custom fusion | flops 409600 | bytes 2152512 | tf_op jit(solution)/shard_map/scatter-add | solution.py:88
  219.2 3.7 reshape.276
  222.9 3.1 pad.8
  226.0 1.8 reshape.277
  234.0 4.7 copy.19
  238.8 6.2 %reshape.328 = f32[2048,400]{1,0:T(8,128)} reshape(f32[1024,2,400]{2,1,0:T(2,128)} %copy.19) | data formatting | bytes 6553600 | tf_op jit(solution)/shard_map/reshape | solution.py:99
  244.9 13.5 %scatter_custom_fusion.1 = f32[4096,400]{1,0:T(8,128)} fusion(s32[2048]{0:T(1024)S(1)} %bitcast.65, f32[2048,400]{1,0:T(8,128)} %reshape.328, f32[]{:T(128)} %constant.79.clone.1), kind=kCustom, calls=%fused_computation.12 | custom fusion | bytes 6554112 | tf_op jit(solution)/shard_map/scatter | solution.py:100
  258.5 10.1 %reshape.275 = f32[64,8,3200]{2,1,0:T(8,128)} reshape(f32[4096,400]{1,0:T(8,128)} %scatter_custom_fusion.1) | data formatting | bytes 13107200 | tf_op jit(solution)/shard_map/reshape | solution.py:102
  268.5 1.7 fusion.16
  270.4 6.8 %pad_maximum_fusion = f32[64,8,3584]{2,1,0:T(8,128)} fusion(f32[64,8,384]{2,1,0:T(8,128)S(1)} %bitcast.53, f32[64,8,3200]{2,1,0:T(8,128)} %reshape.275), kind=kLoop, calls=%fused_computation.11 | loop fusion | flops 1835008 | bytes 14680064 | tf_op jit(solution)/shard_map/concatenate | solution.py:102
  277.2 6.7 %all-to-all-start.2 = ((f32[64,8,3584]{2,1,0:T(8,128)}), f32[64,8,3584]{2,1,0:T(8,128)}, u32[]{:S(2)}, u32[]{:S(2)}) async-start(f32[64,8,3584]{2,1,0:T(8,128)} %pad_maximum_fusion), calls=%async_computation.2 | async-start | bytes 14680064 | tf_op jit(solution)/shard_map/all_to_all | solution.py:103
  284.0 5.9 %fusion.18 = f32[4096,400]{0,1:T(8,128)S(1)} fusion(bf16[1024,4096]{1,0:T(8,128)(2,1)} %copy-done.15, f32[1024,200]{0,1:T(8,128)S(1)} %copy-done.7, f32[1024,200]{0,1:T(8,128)S(1)} %copy-done.4), kind=kOutput, calls=%fused_computation.55 | convolution fusion | flops 3357081600 | bytes 16580608 | tf_op jit(solution)/shard_map/dot_general | solution.py:74
  289.9 2.5 fusion.30
  297.0 150.2 %all-to-all-done.2 = f32[64,8,3584]{2,1,0:T(8,128)} async-done(((f32[64,8,3584]{2,1,0:T(8,128)}), f32[64,8,3584]{2,1,0:T(8,128)}, u32[]{:S(2)}, u32[]{:S(2)}) %all-to-all-start.2) | async-done | bytes 7340064 | tf_op jit(solution)/shard_map/all_to_all | solution.py:103
  449.7 5.8 %all-to-all-start.3 = ((f32[64,1,2176]{2,1,0:T(1,128)}), f32[64,1,2176]{2,1,0:T(1,128)S(1)}, u32[]{:S(2)}, u32[]{:S(2)}) async-start(f32[64,1,2176]{2,1,0:T(1,128)} %broadcast_in_dim.49), calls=%async_computation.3 | async-start | bytes 1114112 | tf_op jit(solution)/shard_map/all_to_all | solution.py:18
  456.9 6.1 %slice.84 = f32[64,8,3200]{2,1,0:T(8,128)} slice(f32[64,8,3584]{2,1,0:T(8,128)} %all-to-all-done.2), slice={[0:64], [0:8], [0:3200]} | slice | bytes 13107200 | tf_op jit(solution)/shard_map/slice | solution.py:104
  463.0 11.8 %reshape.344 = f32[4096,400]{1,0:T(8,128)} reshape(f32[64,8,3200]{2,1,0:T(8,128)} %slice.84) | data formatting | bytes 13107200 | tf_op jit(solution)/shard_map/reshape | solution.py:104
  474.8 28.4 %scatter_custom_fusion.3 = f32[2048,400]{1,0:T(8,128)} fusion(s32[4096]{0:T(1024)S(1)} %bitcast.67, f32[4096,400]{1,0:T(8,128)} %reshape.344, f32[]{:T(128)} %constant.79.clone.1), kind=kCustom, calls=%fused_computation.18 | custom fusion | flops 1638400 | bytes 3277312 | tf_op jit(solution)/shard_map/scatter-add | solution.py:115
  503.1 1.8 constant_dynamic-slice_fusion
  504.9 1.7 copy.29
  508.1 2.9 collective-permute-start.11
  511.1 5.6 %fusion.10 = f32[1024,400]{0,1:T(8,128)} fusion(f32[1024,400]{0,1:T(8,128)} %copy.29, f32[1024,400]{0,1:T(8,128)} %collective-permute-done.8, f32[1024,400]{0,1:T(8,128)} %collective-permute-done.7, f32[1024,400]{0,1:T(8,128)} %collective-permute-done.6, f32[4096,400]{0,1:T(8,128)} %copy-done.8), kind=kLoop, calls=%fused_computation.27 | loop fusion | flops 1638400 | bytes 9830400 | tf_op jit(solution)/shard_map/add | solution.py:118
  516.7 1.8 copy.22
  520.1 5.2 copy.23
  525.3 9.5 %collective-permute-done.9 = f32[64,2176]{1,0:T(8,128)} collective-permute-done((f32[64,2176]{1,0:T(8,128)S(1)}, f32[64,2176]{1,0:T(8,128)}, u32[]{:S(2)}, u32[]{:S(2)}) %collective-permute-start.9) | collective-permute-done | bytes 557088 | tf_op jit(solution)/shard_map/ppermute | solution.py:13
  536.2 2.1 gather_fusion.3
  538.2 1.8 broadcast_select_fusion
  541.6 3.1 slice.91
  544.7 4.0 reshape.281
  548.6 2.1 copy.24
  (100 shorter events, 35.2 us)
Async XLA Ops:
  14.7 22.4 %all-to-all-start = ((s32[64,1,64]{2,1,0:T(1,128)}), s32[64,1,64]{2,1,0:T(1,128)S(1)}, u32[]{:S(2)}, u32[]{:S(2)}) async-start(s32[64,1,64]{2,1,0:T(1,128)} %all_to_all.20), calls=%async_computation | async-start | bytes 65536 | tf_op jit(solution)/shard_map/all_to_all | solution.py:55
  54.6 6.6 %copy-start.9 = (bf16[2048,400]{0,1:T(8,128)(2,1)S(1)}, bf16[2048,400]{0,1:T(8,128)(2,1)}, u32[]{:S(2)}) copy-start(bf16[2048,400]{0,1:T(8,128)(2,1)} %param.6) | copy-start | bytes 4915204
  54.6 101.8 %all-to-all-start.1 = ((bf16[64,64,400]{2,1,0:T(8,128)(2,1)}), bf16[64,64,400]{2,1,0:T(8,128)(2,1)}, u32[]{:S(2)}, u32[]{:S(2)}) async-start(bf16[64,64,400]{2,1,0:T(8,128)(2,1)} %bitcast.50), calls=%async_computation.1 | async-start | bytes 8388608 | tf_op jit(solution)/shard_map/all_to_all | solution.py:56
  60.4 5.9 %copy-start.13 = (bf16[1345,400]{0,1:T(8,128)(2,1)S(1)}, bf16[1345,400]{0,1:T(8,128)(2,1)}, u32[]{:S(2)}) copy-start(bf16[1345,400]{0,1:T(8,128)(2,1)} %param.7) | copy-start | bytes 3228004
  60.4 6.8 %copy-start.14 = (s32[1024]{0:T(1024)S(1)}, s32[1024]{0:T(1024)}, u32[]{:S(2)}) copy-start(s32[1024]{0:T(1024)} %param.10) | copy-start | bytes 12292
  62.2 127.6 %collective-permute-start.2 = (bf16[1024,400]{0,1:T(8,128)(2,1)}, bf16[1024,400]{0,1:T(8,128)(2,1)}, u32[]{:S(2)}, u32[]{:S(2)}) collective-permute-start(bf16[1024,400]{0,1:T(8,128)(2,1)} %constant_dynamic-slice_fusion.1), channel_id=1, source_target_pairs={{0,192},{64,0},{128,64},{192,128},{1,193},{65,1},{129,65},{193,129... | collective-permute-start | bytes 2457608 | tf_op jit(solution)/shard_map/ppermute | solution.py:13
  64.7 125.1 %collective-permute-start.1 = (bf16[1024,400]{0,1:T(8,128)(2,1)}, bf16[1024,400]{0,1:T(8,128)(2,1)}, u32[]{:S(2)}, u32[]{:S(2)}) collective-permute-start(bf16[1024,400]{0,1:T(8,128)(2,1)} %constant_dynamic-slice_fusion.1), channel_id=1, source_target_pairs={{0,128},{64,192},{128,0},{192,64},{1,129},{65,193},{129,1},{193,65... | collective-permute-start | bytes 2457608 | tf_op jit(solution)/shard_map/ppermute | solution.py:13
  65.2 124.6 %collective-permute-start = (bf16[1024,400]{0,1:T(8,128)(2,1)}, bf16[1024,400]{0,1:T(8,128)(2,1)}, u32[]{:S(2)}, u32[]{:S(2)}) collective-permute-start(bf16[1024,400]{0,1:T(8,128)(2,1)} %constant_dynamic-slice_fusion.1), channel_id=1, source_target_pairs={{0,64},{64,128},{128,192},{192,0},{1,65},{65,129},{129,193},{193,1... | collective-permute-start | bytes 2457608 | tf_op jit(solution)/shard_map/ppermute | solution.py:13
  181.1 7.2 %copy-start = (f32[1024,400]{0,1:T(8,128)S(1)}, f32[1024,400]{0,1:T(8,128)}, u32[]{:S(2)}) copy-start(f32[1024,400]{0,1:T(8,128)} %convert_element_type.44) | copy-start | bytes 4915204
  188.3 1.1 copy-start.10
  188.8 10.2 %copy-start.2 = (f32[1024,200]{0,1:T(8,128)}, f32[1024,200]{0,1:T(8,128)S(1)}, u32[]{:S(2)}) copy-start(f32[1024,200]{0,1:T(8,128)S(1)} %get-tuple-element.11) | copy-start | bytes 2457604
  188.8 10.2 %copy-start.5 = (f32[1024,200]{0,1:T(8,128)}, f32[1024,200]{0,1:T(8,128)S(1)}, u32[]{:S(2)}) copy-start(f32[1024,200]{0,1:T(8,128)S(1)} %get-tuple-element.12) | copy-start | bytes 2457604
  199.0 8.4 %copy-start.15 = (bf16[1024,4096]{1,0:T(8,128)(2,1)}, bf16[1024,4096]{1,0:T(8,128)(2,1)S(1)}, u32[]{:S(2)}) copy-start(bf16[1024,4096]{1,0:T(8,128)(2,1)S(1)} %multiply_convert_fusion) | copy-start | bytes 25165828
  227.8 5.6 %copy-start.1 = (f32[4,64,2176]{2,1,0:T(8,128)}, f32[4,64,2176]{2,1,0:T(8,128)S(1)}, u32[]{:S(2)}) copy-start(f32[4,64,2176]{2,1,0:T(8,128)S(1)} %reshape.277) | copy-start | bytes 6684676
  227.8 5.5 copy-start.11
  227.8 5.5 copy-start.12
  229.1 4.3 copy-start.3
  229.1 4.4 copy-start.6
  229.1 39.4 %collective-permute-start.3 = (f32[64,2176]{1,0:T(8,128)}, f32[64,2176]{1,0:T(8,128)}, u32[]{:S(2)}, u32[]{:S(2)}) collective-permute-start(f32[64,2176]{1,0:T(8,128)} %get-tuple-element.13), channel_id=1, source_target_pairs={{0,64},{64,128},{128,192},{192,0},{1,65},{65,129},{129,193},{193,1... | collective-permute-start | bytes 1671176 | tf_op jit(solution)/shard_map/ppermute | solution.py:13
  230.3 38.2 %collective-permute-start.5 = (f32[64,2176]{1,0:T(8,128)}, f32[64,2176]{1,0:T(8,128)}, u32[]{:S(2)}, u32[]{:S(2)}) collective-permute-start(f32[64,2176]{1,0:T(8,128)} %get-tuple-element.14), channel_id=1, source_target_pairs={{0,192},{64,0},{128,64},{192,128},{1,193},{65,1},{129,65},{193,129... | collective-permute-start | bytes 1671176 | tf_op jit(solution)/shard_map/ppermute | solution.py:13
  231.8 36.8 %collective-permute-start.4 = (f32[64,2176]{1,0:T(8,128)}, f32[64,2176]{1,0:T(8,128)}, u32[]{:S(2)}, u32[]{:S(2)}) collective-permute-start(f32[64,2176]{1,0:T(8,128)} %get-tuple-element.15), channel_id=1, source_target_pairs={{0,128},{64,192},{128,0},{192,64},{1,129},{65,193},{129,1},{193,65... | collective-permute-start | bytes 1671176 | tf_op jit(solution)/shard_map/ppermute | solution.py:13
  277.2 6.7 %copy-start.4 = (f32[1024,200]{0,1:T(8,128)S(1)}, f32[1024,200]{0,1:T(8,128)}, u32[]{:S(2)}) copy-start(f32[1024,200]{0,1:T(8,128)} %copy-done.2) | copy-start | bytes 2457604
  277.2 6.8 %copy-start.7 = (f32[1024,200]{0,1:T(8,128)S(1)}, f32[1024,200]{0,1:T(8,128)}, u32[]{:S(2)}) copy-start(f32[1024,200]{0,1:T(8,128)} %copy-done.5) | copy-start | bytes 2457604
  277.2 170.1 %all-to-all-start.2 = ((f32[64,8,3584]{2,1,0:T(8,128)}), f32[64,8,3584]{2,1,0:T(8,128)}, u32[]{:S(2)}, u32[]{:S(2)}) async-start(f32[64,8,3584]{2,1,0:T(8,128)} %pad_maximum_fusion), calls=%async_computation.2 | async-start | bytes 14680064 | tf_op jit(solution)/shard_map/all_to_all | solution.py:103
  289.9 4.2 copy-start.8
  294.1 214.1 %collective-permute-start.6 = (f32[1024,400]{0,1:T(8,128)}, f32[1024,400]{0,1:T(8,128)}, u32[]{:S(2)}, u32[]{:S(2)}) collective-permute-start(f32[1024,400]{0,1:T(8,128)} %get-tuple-element.4), channel_id=1, source_target_pairs={{0,192},{64,0},{128,64},{192,128},{1,193},{65,1},{129,65},{193,129... | collective-permute-start | bytes 4915208 | tf_op jit(solution)/shard_map/ppermute | solution.py:13
  295.0 216.1 %collective-permute-start.8 = (f32[1024,400]{0,1:T(8,128)}, f32[1024,400]{0,1:T(8,128)}, u32[]{:S(2)}, u32[]{:S(2)}) collective-permute-start(f32[1024,400]{0,1:T(8,128)} %get-tuple-element.5), channel_id=1, source_target_pairs={{0,64},{64,128},{128,192},{192,0},{1,65},{65,129},{129,193},{193,1... | collective-permute-start | bytes 4915208 | tf_op jit(solution)/shard_map/ppermute | solution.py:13
  295.6 215.5 %collective-permute-start.7 = (f32[1024,400]{0,1:T(8,128)}, f32[1024,400]{0,1:T(8,128)}, u32[]{:S(2)}, u32[]{:S(2)}) collective-permute-start(f32[1024,400]{0,1:T(8,128)} %get-tuple-element.6), channel_id=1, source_target_pairs={{0,128},{64,192},{128,0},{192,64},{1,129},{65,193},{129,1},{193,65... | collective-permute-start | bytes 4915208 | tf_op jit(solution)/shard_map/ppermute | solution.py:13
  449.7 56.8 %all-to-all-start.3 = ((f32[64,1,2176]{2,1,0:T(1,128)}), f32[64,1,2176]{2,1,0:T(1,128)S(1)}, u32[]{:S(2)}, u32[]{:S(2)}) async-start(f32[64,1,2176]{2,1,0:T(1,128)} %broadcast_in_dim.49), calls=%async_computation.3 | async-start | bytes 1114112 | tf_op jit(solution)/shard_map/all_to_all | solution.py:18
  506.6 18.6 %collective-permute-start.10 = (f32[64,2176]{1,0:T(8,128)S(1)}, f32[64,2176]{1,0:T(8,128)S(1)}, u32[]{:S(2)}, u32[]{:S(2)}) collective-permute-start(f32[64,2176]{1,0:T(8,128)S(1)} %bitcast.57), channel_id=1, source_target_pairs={{0,128},{64,192},{128,0},{192,64},{1,129},{65,193},{129,1},{193,65... | collective-permute-start | bytes 1671176 | tf_op jit(solution)/shard_map/ppermute | solution.py:13
  508.1 26.7 %collective-permute-start.9 = (f32[64,2176]{1,0:T(8,128)S(1)}, f32[64,2176]{1,0:T(8,128)}, u32[]{:S(2)}, u32[]{:S(2)}) collective-permute-start(f32[64,2176]{1,0:T(8,128)S(1)} %bitcast.58), channel_id=1, source_target_pairs={{0,64},{64,128},{128,192},{192,0},{1,65},{65,129},{129,193},{193,1... | collective-permute-start | bytes 1671176 | tf_op jit(solution)/shard_map/ppermute | solution.py:13
  508.1 26.6 %collective-permute-start.11 = (f32[64,2176]{1,0:T(8,128)S(1)}, f32[64,2176]{1,0:T(8,128)}, u32[]{:S(2)}, u32[]{:S(2)}) collective-permute-start(f32[64,2176]{1,0:T(8,128)S(1)} %bitcast.59), channel_id=1, source_target_pairs={{0,192},{64,0},{128,64},{192,128},{1,193},{65,1},{129,65},{193,129... | collective-permute-start | bytes 1671176 | tf_op jit(solution)/shard_map/ppermute | solution.py:13

commit v4 on v3

--- a/solution.py
+++ b/solution.py
@@ -83,31 +83,30 @@
     target_grad = pos_grad[:, None] * query
 
     rel_rows_n = relation.shape[0]
-    total = rel_rows_n * width
-    per_peer = -(-total // (n_blk * n_shard * LANE)) * LANE
-    local_relation = jnp.zeros((rel_rows_n, width), jnp.float32).at[rel_ids].add(rel_term)
-    quarters = jnp.pad(local_relation.reshape(-1), (0, n_blk * n_shard * per_peer - total))
-    quarters = quarters.reshape(n_blk, n_shard, per_peer)
+    chunk = -(-rel_rows_n // (n_blk * n_shard))
+    quarter_rows = n_shard * chunk
+    local_relation = (
+        jnp.zeros((n_blk * quarter_rows, width), jnp.float32).at[rel_ids].add(rel_term)
+    )
+    quarters = local_relation.reshape(n_blk, quarter_rows, width)
     mine = lax.dynamic_index_in_dim(quarters, me_blk, 0, keepdims=False)
     for d in range(1, n_blk):
         outgoing_quarter = lax.dynamic_index_in_dim(quarters, (me_blk + d) % n_blk, 0, keepdims=False)
         mine = mine + shifted(outgoing_quarter, "blk", n_blk, d)
 
-    sub = 8
-    grad_lanes = capacity * width // sub
-    rel_lanes = -(-per_peer // (sub * LANE)) * LANE
     end_grads = jnp.stack([source_grad, target_grad], axis=1).reshape(2 * edges, width)
     outgoing = jnp.zeros((n_shard * capacity, width), jnp.float32).at[slots].set(end_grads)
-    rel_out = jnp.pad(mine, ((0, 0), (0, sub * rel_lanes - per_peer))).reshape(n_shard, sub, rel_lanes)
-    payload = jnp.concatenate([outgoing.reshape(n_shard, sub, grad_lanes), rel_out], axis=2)
+    payload = jnp.concatenate(
+        [outgoing.reshape(n_shard, capacity, width), mine.reshape(n_shard, chunk, width)], axis=1
+    )
     arrived = lax.all_to_all(payload, "shard", split_axis=0, concat_axis=0, tiled=True)
-    arrived_grads = arrived[:, :, :grad_lanes].reshape(n_shard * capacity, width)
-    piece = arrived[:, :, grad_lanes:].reshape(n_shard, sub * rel_lanes)[:, :per_peer].sum(axis=0)
+    arrived_grads = arrived[:, :capacity].reshape(n_shard * capacity, width)
+    piece = arrived[:, capacity:].sum(axis=0)
 
-    quarter = spread(piece, "shard", n_shard)
+    quarter = spread(piece, "shard", n_shard).reshape(quarter_rows, width)
     held = jnp.stack([quarter] + [shifted(quarter, "blk", n_blk, d) for d in range(1, n_blk)])
     order = (me_blk - jnp.arange(n_blk, dtype=jnp.int32)) % n_blk
-    relation_grad = jnp.take(held, order, axis=0).reshape(-1)[:total].reshape(rel_rows_n, width)
+    relation_grad = jnp.take(held, order, axis=0).reshape(n_blk * quarter_rows, width)[:rel_rows_n]
 
     entity_grad = (
         jnp.zeros((rows_own, width), jnp.float32)

time: 560 us -> 585 us (1.045)
  waiting for transfers between devices: 250 us -> 303 us
  local copies, waits for them, and re-layouts: 166 us -> 137 us
    all_to_all x1, waiting for transfers between devices: 150 us -> 197 us  [shards(): lax.all_to_all(payload, 'shard', split_axis=0, concat_axis=0, tiled=True)]
    reshape x5 -> x3, local copies, waits for them, and re-layouts: 31.3 us -> 1.31 us  [the longest x2 1.18 us: shards(): quarter = spread(piece, 'shard', n_shard).reshape(quarter_rows, width)]
    ppermute x12, waiting for transfers between devices: 9.57 us -> 16.7 us  [shifted(): return lax.ppermute(value, axis, [(i, (i + by) % n) for i in range(n)])]
    unnamed x44 -> x46, local copies, waits for them, and re-layouts: 28.7 us -> 33.4 us
  transfers between devices with their start and end apart: 16 -> 16, of which waited for: 4 -> 5; matrix products, arithmetic and copies ran while one was open for 28% -> 24% of each run, Pallas kernels for 0% -> 0%
where the time goes in v4:
time: 585 us; the launch traced here: 575 us
  waiting for transfers between devices  303 us (52%)
  local copies, waits for them, and re-layouts  137 us (23%)
  other arithmetic  63.4 us (11%)
  starting transfers between devices  44.6 us (8%)
  matrix products  25.2 us (4%)
    all_to_all x1, waiting for transfers between devices, shards(): lax.all_to_all(payload, 'shard', split_axis=0, concat_axis=0, tiled=True)  197 us
    all_to_all x1, waiting for transfers between devices, shards(): lax.all_to_all(table[asked_rows], 'shard', split_axis=0, concat_axis=0, t...  83.4 us
    unnamed x46, local copies, waits for them, and re-layouts  33.4 us
    scatter-add x1, other arithmetic, shards(): entity_grad = jnp.zeros((rows_own, width), jnp.float32).at[asked_rows.res...  27.7 us
    gather x1, local copies, waits for them, and re-layouts, shards(): table[asked_rows]  17.3 us
    ppermute x12, waiting for transfers between devices, shifted(): return lax.ppermute(value, axis, [(i, (i + by) % n) for i in range(n)])  16.7 us
    scatter x1, local copies, waits for them, and re-layouts, shards(): jnp.zeros((n_shard * capacity, width), jnp.float32).at[slots].set(end_grads)  13.6 us
    all_to_all x1, starting transfers between devices, shards(): lax.all_to_all(requests, 'shard', split_axis=0, concat_axis=0, tiled=True)  13.2 us
  transfers between devices with their start and end apart: 16, of which 5 were waited for; matrix products, arithmetic and copies ran while one was open for 24% of the time, Pallas kernels for 0%

profile of v4, /device:TPU:1, one launch (start us, length us, event | category | flops | bytes accessed | tf_op | source)
XLA Modules:
  0.0 575.5 jit_solution(14032020935590359825)
XLA Ops:
  4.3 1.7 fusion.14
  6.0 8.1 %scatter_custom_fusion = s32[4096]{0:T(1024)S(1)} fusion(s32[2048]{0:T(1024)S(1)} %bitcast.60, s32[2048]{0:T(1024)S(1)} %reshape.304, s32[]{:T(128)} %constant.80.clone.1), kind=kCustom, calls=%fused_computation.57 | custom fusion | bytes 16388 | tf_op jit(solution)/shard_map/scatter | solution.py:52
  14.7 13.2 %all-to-all-start = ((s32[64,1,64]{2,1,0:T(1,128)}), s32[64,1,64]{2,1,0:T(1,128)S(1)}, u32[]{:S(2)}, u32[]{:S(2)}) async-start(s32[64,1,64]{2,1,0:T(1,128)} %all_to_all.17), calls=%async_computation | async-start | bytes 65536 | tf_op jit(solution)/shard_map/all_to_all | solution.py:55
  27.9 2.8 copy.32
  30.7 6.4 %all-to-all-done = s32[64,1,64]{2,1,0:T(1,128)S(1)} async-done(((s32[64,1,64]{2,1,0:T(1,128)}), s32[64,1,64]{2,1,0:T(1,128)S(1)}, u32[]{:S(2)}, u32[]{:S(2)}) %all-to-all-start) | async-done | bytes 16416 | tf_op jit(solution)/shard_map/all_to_all | solution.py:55
  37.2 17.3 %gather_fusion = bf16[4096,400]{1,0:T(8,128)(2,1)} fusion(bf16[2048,400]{1,0:T(8,128)(2,1)S(1)} %copy.32, s32[4096]{0:T(1024)S(1)} %broadcast_clamp_fusion), kind=kCustom, calls=%fused_computation | custom fusion | bytes 6569984 | tf_op jit(solution)/shard_map/gather | solution.py:56
  54.5 6.0 %all-to-all-start.1 = ((bf16[64,64,400]{2,1,0:T(8,128)(2,1)}), bf16[64,64,400]{2,1,0:T(8,128)(2,1)}, u32[]{:S(2)}, u32[]{:S(2)}) async-start(bf16[64,64,400]{2,1,0:T(8,128)(2,1)} %bitcast.49), calls=%async_computation.1 | async-start | bytes 8388608 | tf_op jit(solution)/shard_map/all_to_all | solution.py:56
  62.2 2.5 collective-permute-start.2
  67.1 4.0 gather_fusion.2
  73.0 83.4 %all-to-all-done.1 = bf16[64,64,400]{2,1,0:T(8,128)(2,1)} async-done(((bf16[64,64,400]{2,1,0:T(8,128)(2,1)}), bf16[64,64,400]{2,1,0:T(8,128)(2,1)}, u32[]{:S(2)}, u32[]{:S(2)}) %all-to-all-start.1) | async-done | bytes 3276832 | tf_op jit(solution)/shard_map/all_to_all | solution.py:56
  156.4 12.0 %gather_fusion.1 = bf16[2048,400]{1,0:T(8,128)(2,1)} fusion(bf16[4096,400]{1,0:T(8,128)(2,1)} %bitcast.5, s32[2048]{0:T(1024)S(1)} %broadcast_clamp_fusion.1), kind=kCustom, calls=%fused_computation.1 | custom fusion | bytes 3284992 | tf_op jit(solution)/shard_map/gather | solution.py:57
  168.4 2.8 reshape.259
  171.2 4.2 fusion.32
  175.4 5.8 %copy.54 = bf16[1024,1,400]{0,2,1:T(8,128)(2,1)} copy(bf16[1024,1,400]{2,1,0:T(2,128)(2,1)} %get-tuple-element.20) | data formatting | bytes 1638400
  182.6 5.8 %copy.55 = bf16[1024,1,400]{0,2,1:T(8,128)(2,1)} copy(bf16[1024,1,400]{2,1,0:T(2,128)(2,1)} %get-tuple-element.19) | data formatting | bytes 1638400
  189.9 9.2 %multiply_convert_fusion = bf16[1024,4096]{1,0:T(8,128)(2,1)S(1)} fusion(bf16[1024,400]{0,1:T(8,128)(2,1)} %collective-permute-done.2, bf16[1024,400]{0,1:T(8,128)(2,1)} %collective-permute-done.1, bf16[1024,400]{0,1:T(8,128)(2,1)} %collective-permute-done, bf16[1024,400]{0,1:T(8,128)(2,1)} %constant_dynamic-slice_fusion.5, ...), kind=kOutput, calls=%fused_computation.8 | convolution fusion | flops 3391160320 | bytes 13303808 | tf_op jit(solution)/shard_map/dot_general | solution.py:67
  199.1 8.4 %fusion.7 = f32[1024,400]{0,1:T(8,128)S(1)} fusion(bf16[1024,4096]{1,0:T(8,128)(2,1)S(1)} %multiply_convert_fusion, bf16[1024,1,400]{0,2,1:T(8,128)(2,1)S(1)} %copy-done.10, f32[1024]{0:T(1024)S(1)} %divide_add_fusion, bf16[1024,400]{0,1:T(8,128)(2,1)} %collective-permute-done.2, bf16[1024,400]{0,1:T(8,128)(2,1)} %collective-permute-done.1, ...), kind=kOutput, calls=%fused_computation.24 | convolution fusion | flops 3369779200 | bytes 14127104 | tf_op jit(solution)/shard_map/dot_general | solution.py:71
  207.5 1.8 multiply_add_fusion.1
  209.4 1.8 copy.38
  211.2 8.2 %scatter_custom_fusion.2 = f32[1536,400]{1,0:T(8,128)S(1)} fusion(s32[1024]{0:T(1024)S(1)} %get-tuple-element.24, f32[1024,400]{1,0:T(8,128)} %copy.38, f32[]{:T(128)} %constant.79.clone.1), kind=kCustom, calls=%fused_computation.33 | custom fusion | flops 409600 | bytes 2458112 | tf_op jit(solution)/shard_map/scatter-add | solution.py:89
  219.4 1.8 constant_dynamic-slice_fusion.4
  221.2 2.3 copy.52
  223.5 2.3 copy.51
  225.8 2.2 copy.53
  228.1 2.5 collective-permute-start.5
  230.5 1.7 collective-permute-start.4
  233.1 4.6 copy.37
  237.7 6.3 %reshape.312 = f32[2048,400]{1,0:T(8,128)} reshape(f32[1024,2,400]{2,1,0:T(2,128)} %copy.37) | data formatting | bytes 6553600 | tf_op jit(solution)/shard_map/reshape | solution.py:97
  244.2 13.6 %scatter_custom_fusion.1 = f32[4096,400]{1,0:T(8,128)} fusion(s32[2048]{0:T(1024)S(1)} %bitcast.62, f32[2048,400]{1,0:T(8,128)} %reshape.312, f32[]{:T(128)} %constant.79.clone.1), kind=kCustom, calls=%fused_computation.12 | custom fusion | bytes 6554112 | tf_op jit(solution)/shard_map/scatter | solution.py:98
  259.1 1.6 fusion.16
  261.0 8.7 %pad_maximum_fusion = f32[64,70,400]{2,1,0:T(8,128)} fusion(f32[64,6,400]{2,1,0:T(8,128)S(1)} %reshape.263, f32[64,64,400]{2,1,0:T(8,128)} %bitcast.48), kind=kLoop, calls=%fused_computation.11 | loop fusion | flops 1792000 | bytes 14336000 | tf_op jit(solution)/shard_map/concatenate | solution.py:99
  269.7 8.3 %all-to-all-start.2 = ((f32[64,70,400]{2,1,0:T(8,128)}), f32[64,70,400]{2,1,0:T(8,128)}, u32[]{:S(2)}, u32[]{:S(2)}) async-start(f32[64,70,400]{2,1,0:T(8,128)} %pad_maximum_fusion), calls=%async_computation.2 | async-start | bytes 18874368 | tf_op jit(solution)/shard_map/all_to_all | solution.py:102
  278.0 5.9 %fusion.18 = f32[4096,400]{0,1:T(8,128)S(1)} fusion(bf16[1024,4096]{1,0:T(8,128)(2,1)} %copy-done.16, f32[1024,200]{0,1:T(8,128)S(1)} %copy-done.6, f32[1024,200]{0,1:T(8,128)S(1)} %copy-done.3), kind=kOutput, calls=%fused_computation.50 | convolution fusion | flops 3357081600 | bytes 16580608 | tf_op jit(solution)/shard_map/dot_general | solution.py:74
  283.9 2.4 fusion.31
  286.4 1.8 copy-done.8
  289.6 196.6 %all-to-all-done.2 = f32[64,70,400]{2,1,0:T(8,128)} async-done(((f32[64,70,400]{2,1,0:T(8,128)}), f32[64,70,400]{2,1,0:T(8,128)}, u32[]{:S(2)}, u32[]{:S(2)}) %all-to-all-start.2) | async-done | bytes 7168032 | tf_op jit(solution)/shard_map/all_to_all | solution.py:102
  488.6 6.0 %all-to-all-start.3 = ((f32[64,6,400]{2,1,0:T(8,128)}), f32[64,6,400]{2,1,0:T(8,128)S(1)}, u32[]{:S(2)}, u32[]{:S(2)}) async-start(f32[64,6,400]{2,1,0:T(8,128)} %broadcast_in_dim.58), calls=%async_computation.3 | async-start | bytes 2097152 | tf_op jit(solution)/shard_map/all_to_all | solution.py:18
  496.1 8.5 %slice.80 = f32[64,64,400]{2,1,0:T(8,128)} slice(f32[64,70,400]{2,1,0:T(8,128)} %all-to-all-done.2), slice={[0:64], [0:64], [0:400]} | slice | bytes 13107200 | tf_op jit(solution)/shard_map/slice | solution.py:103
  504.6 27.7 %scatter_custom_fusion.3 = f32[2048,400]{1,0:T(8,128)} fusion(s32[4096]{0:T(1024)S(1)} %bitcast.64, f32[4096,400]{1,0:T(8,128)} %bitcast.53, f32[]{:T(128)} %constant.79.clone.1), kind=kCustom, calls=%fused_computation.19 | custom fusion | flops 1638400 | bytes 3277312 | tf_op jit(solution)/shard_map/scatter-add | solution.py:114
  532.3 1.8 constant_dynamic-slice_fusion
  534.1 1.7 copy.60
  538.4 5.0 fusion.10
  543.4 1.8 copy.42
  546.7 5.2 copy.48
  552.3 15.4 %collective-permute-done.9 = f32[384,400]{0,1:T(8,128)} collective-permute-done((f32[384,400]{0,1:T(8,128)}, f32[384,400]{0,1:T(8,128)}, u32[]{:S(2)}, u32[]{:S(2)}) %collective-permute-start.9) | collective-permute-done | bytes 614432 | tf_op jit(solution)/shard_map/ppermute | solution.py:13
  567.7 1.6 pad_maximum_fusion.3
  569.3 2.2 gather_fusion.3
  571.5 2.0 copy.69
  (101 shorter events, 26.9 us)
Async XLA Ops:
  14.7 22.4 %all-to-all-start = ((s32[64,1,64]{2,1,0:T(1,128)}), s32[64,1,64]{2,1,0:T(1,128)S(1)}, u32[]{:S(2)}, u32[]{:S(2)}) async-start(s32[64,1,64]{2,1,0:T(1,128)} %all_to_all.17), calls=%async_computation | async-start | bytes 65536 | tf_op jit(solution)/shard_map/all_to_all | solution.py:55
  54.5 6.6 %copy-start.9 = (bf16[2048,400]{0,1:T(8,128)(2,1)S(1)}, bf16[2048,400]{0,1:T(8,128)(2,1)}, u32[]{:S(2)}) copy-start(bf16[2048,400]{0,1:T(8,128)(2,1)} %param.6) | copy-start | bytes 4915204
  54.5 11.7 %copy-start.14 = (bf16[1345,400]{0,1:T(8,128)(2,1)S(1)}, bf16[1345,400]{0,1:T(8,128)(2,1)}, u32[]{:S(2)}) copy-start(bf16[1345,400]{0,1:T(8,128)(2,1)} %param.7) | copy-start | bytes 3228004
  54.5 101.9 %all-to-all-start.1 = ((bf16[64,64,400]{2,1,0:T(8,128)(2,1)}), bf16[64,64,400]{2,1,0:T(8,128)(2,1)}, u32[]{:S(2)}, u32[]{:S(2)}) async-start(bf16[64,64,400]{2,1,0:T(8,128)(2,1)} %bitcast.49), calls=%async_computation.1 | async-start | bytes 8388608 | tf_op jit(solution)/shard_map/all_to_all | solution.py:56
  60.5 6.6 %copy-start.15 = (s32[1024]{0:T(1024)S(1)}, s32[1024]{0:T(1024)}, u32[]{:S(2)}) copy-start(s32[1024]{0:T(1024)} %param.10) | copy-start | bytes 12292
  62.2 127.7 %collective-permute-start.2 = (bf16[1024,400]{0,1:T(8,128)(2,1)}, bf16[1024,400]{0,1:T(8,128)(2,1)}, u32[]{:S(2)}, u32[]{:S(2)}) collective-permute-start(bf16[1024,400]{0,1:T(8,128)(2,1)} %constant_dynamic-slice_fusion.5), channel_id=1, source_target_pairs={{0,192},{64,0},{128,64},{192,128},{1,193},{65,1},{129,65},{193,129... | collective-permute-start | bytes 2457608 | tf_op jit(solution)/shard_map/ppermute | solution.py:13
  64.7 125.2 %collective-permute-start.1 = (bf16[1024,400]{0,1:T(8,128)(2,1)}, bf16[1024,400]{0,1:T(8,128)(2,1)}, u32[]{:S(2)}, u32[]{:S(2)}) collective-permute-start(bf16[1024,400]{0,1:T(8,128)(2,1)} %constant_dynamic-slice_fusion.5), channel_id=1, source_target_pairs={{0,128},{64,192},{128,0},{192,64},{1,129},{65,193},{129,1},{193,65... | collective-permute-start | bytes 2457608 | tf_op jit(solution)/shard_map/ppermute | solution.py:13
  65.2 124.7 %collective-permute-start = (bf16[1024,400]{0,1:T(8,128)(2,1)}, bf16[1024,400]{0,1:T(8,128)(2,1)}, u32[]{:S(2)}, u32[]{:S(2)}) collective-permute-start(bf16[1024,400]{0,1:T(8,128)(2,1)} %constant_dynamic-slice_fusion.5), channel_id=1, source_target_pairs={{0,64},{64,128},{128,192},{192,0},{1,65},{65,129},{129,193},{193,1... | collective-permute-start | bytes 2457608 | tf_op jit(solution)/shard_map/ppermute | solution.py:13
  181.2 7.2 %copy-start = (f32[1024,400]{0,1:T(8,128)S(1)}, f32[1024,400]{0,1:T(8,128)}, u32[]{:S(2)}) copy-start(f32[1024,400]{0,1:T(8,128)} %convert_element_type.40) | copy-start | bytes 4915204
  188.4 1.1 copy-start.10
  188.9 10.2 %copy-start.1 = (f32[1024,200]{0,1:T(8,128)}, f32[1024,200]{0,1:T(8,128)S(1)}, u32[]{:S(2)}) copy-start(f32[1024,200]{0,1:T(8,128)S(1)} %get-tuple-element.13) | copy-start | bytes 2457604
  188.9 10.2 %copy-start.4 = (f32[1024,200]{0,1:T(8,128)}, f32[1024,200]{0,1:T(8,128)S(1)}, u32[]{:S(2)}) copy-start(f32[1024,200]{0,1:T(8,128)S(1)} %get-tuple-element.14) | copy-start | bytes 2457604
  199.1 8.4 %copy-start.16 = (bf16[1024,4096]{1,0:T(8,128)(2,1)}, bf16[1024,4096]{1,0:T(8,128)(2,1)S(1)}, u32[]{:S(2)}) copy-start(bf16[1024,4096]{1,0:T(8,128)(2,1)S(1)} %multiply_convert_fusion) | copy-start | bytes 25165828
  221.2 11.1 %copy-start.11 = (f32[1024,200]{0,1:T(8,128)S(1)}, f32[1024,200]{0,1:T(8,128)}, u32[]{:S(2)}) copy-start(f32[1024,200]{0,1:T(8,128)} %get-tuple-element.9) | copy-start | bytes 2457604
  221.2 11.1 %copy-start.12 = (f32[1024,200]{0,1:T(8,128)S(1)}, f32[1024,200]{0,1:T(8,128)}, u32[]{:S(2)}) copy-start(f32[1024,200]{0,1:T(8,128)} %get-tuple-element.10) | copy-start | bytes 2457604
  223.5 9.0 %copy-start.2 = (f32[1024,200]{0,1:T(8,128)S(1)}, f32[1024,200]{0,1:T(8,128)}, u32[]{:S(2)}) copy-start(f32[1024,200]{0,1:T(8,128)} %copy-done.1) | copy-start | bytes 2457604
  223.5 9.0 %copy-start.5 = (f32[1024,200]{0,1:T(8,128)S(1)}, f32[1024,200]{0,1:T(8,128)}, u32[]{:S(2)}) copy-start(f32[1024,200]{0,1:T(8,128)} %copy-done.4) | copy-start | bytes 2457604
  228.1 29.8 %collective-permute-start.5 = (f32[384,400]{0,1:T(8,128)}, f32[384,400]{0,1:T(8,128)}, u32[]{:S(2)}, u32[]{:S(2)}) collective-permute-start(f32[384,400]{0,1:T(8,128)} %bitcast.58), channel_id=1, source_target_pairs={{0,192},{64,0},{128,64},{192,128},{1,193},{65,1},{129,65},{193,129... | collective-permute-start | bytes 1843208 | tf_op jit(solution)/shard_map/ppermute | solution.py:13
  230.5 27.3 %collective-permute-start.3 = (f32[384,400]{0,1:T(8,128)}, f32[384,400]{0,1:T(8,128)}, u32[]{:S(2)}, u32[]{:S(2)}) collective-permute-start(f32[384,400]{0,1:T(8,128)} %bitcast.57), channel_id=1, source_target_pairs={{0,64},{64,128},{128,192},{192,0},{1,65},{65,129},{129,193},{193,1... | collective-permute-start | bytes 1843208 | tf_op jit(solution)/shard_map/ppermute | solution.py:13
  230.5 28.5 %collective-permute-start.4 = (f32[384,400]{0,1:T(8,128)}, f32[384,400]{0,1:T(8,128)}, u32[]{:S(2)}, u32[]{:S(2)}) collective-permute-start(f32[384,400]{0,1:T(8,128)} %bitcast.56), channel_id=1, source_target_pairs={{0,128},{64,192},{128,0},{192,64},{1,129},{65,193},{129,1},{193,65... | collective-permute-start | bytes 1843208 | tf_op jit(solution)/shard_map/ppermute | solution.py:13
  237.7 6.3 %copy-start.13 = (f32[1,384,400]{2,1,0:T(8,128)S(1)}, f32[1,384,400]{2,1,0:T(8,128)}, u32[]{:S(2)}) copy-start(f32[1,384,400]{2,1,0:T(8,128)} %get-tuple-element.15) | copy-start | bytes 1843204
  269.7 8.3 %copy-start.3 = (f32[1024,200]{0,1:T(8,128)S(1)}, f32[1024,200]{0,1:T(8,128)}, u32[]{:S(2)}) copy-start(f32[1024,200]{0,1:T(8,128)} %copy-done.1) | copy-start | bytes 2457604
  269.7 8.3 %copy-start.6 = (f32[1024,200]{0,1:T(8,128)S(1)}, f32[1024,200]{0,1:T(8,128)}, u32[]{:S(2)}) copy-start(f32[1024,200]{0,1:T(8,128)} %copy-done.4) | copy-start | bytes 2457604
  269.7 216.5 %all-to-all-start.2 = ((f32[64,70,400]{2,1,0:T(8,128)}), f32[64,70,400]{2,1,0:T(8,128)}, u32[]{:S(2)}, u32[]{:S(2)}) async-start(f32[64,70,400]{2,1,0:T(8,128)} %pad_maximum_fusion), calls=%async_computation.2 | async-start | bytes 18874368 | tf_op jit(solution)/shard_map/all_to_all | solution.py:102
  283.9 4.2 copy-start.8
  288.1 249.4 %collective-permute-start.6 = (f32[1024,400]{0,1:T(8,128)}, f32[1024,400]{0,1:T(8,128)}, u32[]{:S(2)}, u32[]{:S(2)}) collective-permute-start(f32[1024,400]{0,1:T(8,128)} %get-tuple-element.6), channel_id=1, source_target_pairs={{0,192},{64,0},{128,64},{192,128},{1,193},{65,1},{129,65},{193,129... | collective-permute-start | bytes 4915208 | tf_op jit(solution)/shard_map/ppermute | solution.py:13
  288.1 250.3 %collective-permute-start.8 = (f32[1024,400]{0,1:T(8,128)}, f32[1024,400]{0,1:T(8,128)}, u32[]{:S(2)}, u32[]{:S(2)}) collective-permute-start(f32[1024,400]{0,1:T(8,128)} %get-tuple-element.7), channel_id=1, source_target_pairs={{0,64},{64,128},{128,192},{192,0},{1,65},{65,129},{129,193},{193,1... | collective-permute-start | bytes 4915208 | tf_op jit(solution)/shard_map/ppermute | solution.py:13
  289.6 248.8 %collective-permute-start.7 = (f32[1024,400]{0,1:T(8,128)}, f32[1024,400]{0,1:T(8,128)}, u32[]{:S(2)}, u32[]{:S(2)}) collective-permute-start(f32[1024,400]{0,1:T(8,128)} %get-tuple-element.8), channel_id=1, source_target_pairs={{0,128},{64,192},{128,0},{192,64},{1,129},{65,193},{129,1},{193,65... | collective-permute-start | bytes 4915208 | tf_op jit(solution)/shard_map/ppermute | solution.py:13
  488.6 47.1 %all-to-all-start.3 = ((f32[64,6,400]{2,1,0:T(8,128)}), f32[64,6,400]{2,1,0:T(8,128)S(1)}, u32[]{:S(2)}, u32[]{:S(2)}) async-start(f32[64,6,400]{2,1,0:T(8,128)} %broadcast_in_dim.58), calls=%async_computation.3 | async-start | bytes 2097152 | tf_op jit(solution)/shard_map/all_to_all | solution.py:18
  535.7 2.7 copy-start.7
  536.9 15.3 %collective-permute-start.11 = (f32[384,400]{0,1:T(8,128)}, f32[384,400]{0,1:T(8,128)}, u32[]{:S(2)}, u32[]{:S(2)}) collective-permute-start(f32[384,400]{0,1:T(8,128)} %copy.43), channel_id=1, source_target_pairs={{0,192},{64,0},{128,64},{192,128},{1,193},{65,1},{129,65},{193,129... | collective-permute-start | bytes 1843208 | tf_op jit(solution)/shard_map/ppermute | solution.py:13
  536.9 15.4 %collective-permute-start.10 = (f32[384,400]{0,1:T(8,128)}, f32[384,400]{0,1:T(8,128)}, u32[]{:S(2)}, u32[]{:S(2)}) collective-permute-start(f32[384,400]{0,1:T(8,128)} %copy.43), channel_id=1, source_target_pairs={{0,128},{64,192},{128,0},{192,64},{1,129},{65,193},{129,1},{193,65... | collective-permute-start | bytes 1843208 | tf_op jit(solution)/shard_map/ppermute | solution.py:13
  537.5 30.2 %collective-permute-start.9 = (f32[384,400]{0,1:T(8,128)}, f32[384,400]{0,1:T(8,128)}, u32[]{:S(2)}, u32[]{:S(2)}) collective-permute-start(f32[384,400]{0,1:T(8,128)} %copy.43), channel_id=1, source_target_pairs={{0,64},{64,128},{128,192},{192,0},{1,65},{65,129},{129,193},{193,1... | collective-permute-start | bytes 1843208 | tf_op jit(solution)/shard_map/ppermute | solution.py:13

commit v5 on v4

--- a/solution.py
+++ b/solution.py
@@ -16,6 +16,39 @@
 def spread(value, axis, n):
     copies = jnp.broadcast_to(value[None], (n,) + value.shape)
     return lax.all_to_all(copies, axis, 0, 0, tiled=False)
+
+
+SHARD_DIMS = (4, 8, 2)
+
+
+def shard_moves(sizes, dim, by):
+    n = sizes[0] * sizes[1] * sizes[2]
+    pairs = []
+    for s in range(n):
+        coords = [s // (sizes[1] * sizes[2]), (s // sizes[2]) % sizes[1], s % sizes[2]]
+        coords[dim] = (coords[dim] + by) % sizes[dim]
+        pairs.append((s, (coords[0] * sizes[1] + coords[1]) * sizes[2] + coords[2]))
+    return pairs
+
+
+def reduce_over_shard(block, n_shard, width):
+    sizes = SHARD_DIMS
+    me = lax.axis_index("shard")
+    mine_at = [me // (sizes[1] * sizes[2]), (me // sizes[2]) % sizes[1], me % sizes[2]]
+    levels = (2, 0, 1)
+    for dim in levels:
+        n = sizes[dim]
+        parts = block.reshape(n, -1, width)
+        block = lax.dynamic_index_in_dim(parts, mine_at[dim], 0, keepdims=False)
+        for d in range(1, n):
+            going = lax.dynamic_index_in_dim(parts, (mine_at[dim] + d) % n, 0, keepdims=False)
+            block = block + lax.ppermute(going, "shard", shard_moves(sizes, dim, d))
+    for dim in reversed(levels):
+        n = sizes[dim]
+        held = [block] + [lax.ppermute(block, "shard", shard_moves(sizes, dim, d)) for d in range(1, n)]
+        order = (mine_at[dim] - jnp.arange(n, dtype=jnp.int32)) % n
+        block = jnp.take(jnp.stack(held), order, axis=0).reshape(-1, width)
+    return block
 
 
 def owner_rank(flat_owner, n_shard):
@@ -53,7 +86,9 @@
         .reshape(n_shard, capacity)
     )
     asked_rows = lax.all_to_all(requests, "shard", split_axis=0, concat_axis=0, tiled=True)
-    fetched = lax.all_to_all(table[asked_rows], "shard", split_axis=0, concat_axis=0, tiled=True)
+    fetch_rows = capacity * width // LANE
+    sending = table[asked_rows].reshape(n_shard, fetch_rows, LANE)
+    fetched = lax.all_to_all(sending, "shard", split_axis=0, concat_axis=0, tiled=True)
     gotten = fetched.reshape(n_shard * capacity, width)[slots].reshape(edges, 2, width)
     source = gotten[:, 0].astype(jnp.float32)
     target = gotten[:, 1].astype(jnp.float32)
@@ -93,20 +128,18 @@
     for d in range(1, n_blk):
         outgoing_quarter = lax.dynamic_index_in_dim(quarters, (me_blk + d) % n_blk, 0, keepdims=False)
         mine = mine + shifted(outgoing_quarter, "blk", n_blk, d)
+    relation_grad = reduce_over_shard(mine, n_shard, width)
+    held = jnp.stack([relation_grad] + [shifted(relation_grad, "blk", n_blk, d) for d in range(1, n_blk)])
+    order = (me_blk - jnp.arange(n_blk, dtype=jnp.int32)) % n_blk
+    relation_grad = jnp.take(held, order, axis=0).reshape(n_blk * quarter_rows, width)[:rel_rows_n]
 
+    sub = 8
+    grad_lanes = capacity * width // sub
     end_grads = jnp.stack([source_grad, target_grad], axis=1).reshape(2 * edges, width)
     outgoing = jnp.zeros((n_shard * capacity, width), jnp.float32).at[slots].set(end_grads)
-    payload = jnp.concatenate(
-        [outgoing.reshape(n_shard, capacity, width), mine.reshape(n_shard, chunk, width)], axis=1
-    )
+    payload = outgoing.reshape(n_shard, sub, grad_lanes)
     arrived = lax.all_to_all(payload, "shard", split_axis=0, concat_axis=0, tiled=True)
-    arrived_grads = arrived[:, :capacity].reshape(n_shard * capacity, width)
-    piece = arrived[:, capacity:].sum(axis=0)
-
-    quarter = spread(piece, "shard", n_shard).reshape(quarter_rows, width)
-    held = jnp.stack([quarter] + [shifted(quarter, "blk", n_blk, d) for d in range(1, n_blk)])
-    order = (me_blk - jnp.arange(n_blk, dtype=jnp.int32)) % n_blk
-    relation_grad = jnp.take(held, order, axis=0).reshape(n_blk * quarter_rows, width)[:rel_rows_n]
+    arrived_grads = arrived.reshape(n_shard * capacity, width)
 
     entity_grad = (
         jnp.zeros((rows_own, width), jnp.float32)

time: 585 us -> 630 us (1.077)
  starting transfers between devices: 44.6 us -> 92.2 us
  local copies, waits for them, and re-layouts: 137 us -> 171 us
  waiting for transfers between devices: 303 us -> 272 us
    all_to_all x1, waiting for transfers between devices: 197 us -> 0.01 us  [shards(): lax.all_to_all(payload, 'shard', split_axis=0, concat_axis=0, tiled=True)]
    ppermute x12, waiting for transfers between devices: 16.7 us -> 121 us  [shifted(): return lax.ppermute(value, axis, [(i, (i + by) % n) for i in range(n)])]
    ppermute x0 -> x22, waiting for transfers between devices: none -> 81.3 us  [the longest x11 70.5 us: reduce_over_shard(): block = block + lax.ppermute(going, 'shard', shard_moves(sizes, dim, d))]
    ppermute x0 -> x22, starting transfers between devices: none -> 51 us  [the longest x11 28.8 us: reduce_over_shard(): block = block + lax.ppermute(going, 'shard', shard_moves(sizes, dim, d))]
    reshape x3 -> x5, local copies, waits for them, and re-layouts: 1.31 us -> 32.7 us  [the longest x1 11.9 us: shards(): arrived_grads = arrived.reshape(n_shard * capacity, width)]
    all_to_all x2 -> x1, waiting for transfers between devices: 83.4 us -> 64 us  [shards(): lax.all_to_all(sending, 'shard', split_axis=0, concat_axis=0, tiled=True)]
    reshape x1 -> x2, local copies, waits for them, and re-layouts: 2.82 us -> 14 us  [shards(): fetched.reshape(n_shard * capacity, width)[slots].reshape(edges, 2, width)]
    concatenate x1 -> x0, other arithmetic: 8.67 us -> none  [shards(): jnp.concatenate([outgoing.reshape(n_shard, capacity, width), mine.reshape...]
  transfers between devices with their start and end apart: 16 -> 37, of which waited for: 5 -> 17; matrix products, arithmetic and copies ran while one was open for 24% -> 23% of each run, Pallas kernels for 0% -> 0%
where the time goes in v5:
time: 630 us; the launch traced here: 621 us
  waiting for transfers between devices  272 us (43%)
  local copies, waits for them, and re-layouts  171 us (27%)
  starting transfers between devices  92.2 us (15%)
  other arithmetic  57.2 us (9%)
  matrix products  25.6 us (4%)
    ppermute x12, waiting for transfers between devices, shifted(): return lax.ppermute(value, axis, [(i, (i + by) % n) for i in range(n)])  121 us
    ppermute x11, waiting for transfers between devices, reduce_over_shard(): block = block + lax.ppermute(going, 'shard', shard_moves(sizes, dim, d))  70.5 us
    all_to_all x1, waiting for transfers between devices, shards(): lax.all_to_all(sending, 'shard', split_axis=0, concat_axis=0, tiled=True)  64 us
    scatter-add x1, other arithmetic, shards(): entity_grad = jnp.zeros((rows_own, width), jnp.float32).at[asked_rows.res...  29.8 us
    ppermute x11, starting transfers between devices, reduce_over_shard(): block = block + lax.ppermute(going, 'shard', shard_moves(sizes, dim, d))  28.8 us
    unnamed x46, local copies, waits for them, and re-layouts  26.4 us
    ppermute x11, starting transfers between devices, reduce_over_shard(): lax.ppermute(block, 'shard', shard_moves(sizes, dim, d))  22.1 us
    gather x1, local copies, waits for them, and re-layouts, shards(): sending = table[asked_rows].reshape(n_shard, fetch_rows, LANE)  17.4 us
  transfers between devices with their start and end apart: 37, of which 17 were waited for; matrix products, arithmetic and copies ran while one was open for 23% of the time, Pallas kernels for 0%

profile of v5, /device:TPU:1, one launch (start us, length us, event | category | flops | bytes accessed | tf_op | source)
XLA Modules:
  0.0 620.9 jit_solution(12721177329077818757)
XLA Ops:
  6.0 8.1 %scatter_custom_fusion = s32[4096]{0:T(1024)S(1)} fusion(s32[2048]{0:T(1024)S(1)} %bitcast.141, s32[2048]{0:T(1024)S(1)} %reshape.602, s32[]{:T(128)} %constant.260.clone.1), kind=kCustom, calls=%fused_computation.95 | custom fusion | bytes 16388 | tf_op jit(solution)/shard_map/scatter | solution.py:85
  14.7 13.2 %all-to-all-start = ((s32[64,1,64]{2,1,0:T(1,128)}), s32[64,1,64]{2,1,0:T(1,128)S(1)}, u32[]{:S(2)}, u32[]{:S(2)}) async-start(s32[64,1,64]{2,1,0:T(1,128)} %all_to_all.14), calls=%async_computation | async-start | bytes 65536 | tf_op jit(solution)/shard_map/all_to_all | solution.py:88
  27.9 2.8 copy.63
  30.7 6.4 %all-to-all-done = s32[64,1,64]{2,1,0:T(1,128)S(1)} async-done(((s32[64,1,64]{2,1,0:T(1,128)}), s32[64,1,64]{2,1,0:T(1,128)S(1)}, u32[]{:S(2)}, u32[]{:S(2)}) %all-to-all-start) | async-done | bytes 16416 | tf_op jit(solution)/shard_map/all_to_all | solution.py:88
  37.2 17.4 %gather_fusion = bf16[4096,400]{1,0:T(8,128)(2,1)} fusion(bf16[2048,400]{1,0:T(8,128)(2,1)S(1)} %copy.63, s32[4096]{0:T(1024)S(1)} %broadcast_clamp_fusion), kind=kCustom, calls=%fused_computation | custom fusion | bytes 6569984 | tf_op jit(solution)/shard_map/gather | solution.py:90
  54.6 10.2 %reshape.530 = bf16[64,200,128]{2,1,0:T(8,128)(2,1)} reshape(bf16[4096,400]{1,0:T(8,128)(2,1)} %gather_fusion) | data formatting | bytes 6553600 | tf_op jit(solution)/shard_map/reshape | solution.py:90
  64.7 5.9 all-to-all-start.1
  72.3 2.5 collective-permute-start.2
  77.0 4.0 gather_fusion.2
  82.9 64.0 %all-to-all-done.1 = bf16[64,200,128]{2,1,0:T(8,128)(2,1)} async-done(((bf16[64,200,128]{2,1,0:T(8,128)(2,1)}), bf16[64,200,128]{2,1,0:T(8,128)(2,1)}, u32[]{:S(2)}, u32[]{:S(2)}) %all-to-all-start.1) | async-done | bytes 3276832 | tf_op jit(solution)/shard_map/all_to_all | solution.py:91
  146.9 11.1 %reshape.531 = bf16[4096,400]{1,0:T(8,128)(2,1)} reshape(bf16[64,200,128]{2,1,0:T(8,128)(2,1)} %all-to-all-done.1) | data formatting | bytes 6553600 | tf_op jit(solution)/shard_map/reshape | solution.py:92
  158.1 12.0 %gather_fusion.1 = bf16[2048,400]{1,0:T(8,128)(2,1)} fusion(bf16[4096,400]{1,0:T(8,128)(2,1)} %reshape.531, s32[2048]{0:T(1024)S(1)} %broadcast_clamp_fusion.1), kind=kCustom, calls=%fused_computation.1 | custom fusion | bytes 3284992 | tf_op jit(solution)/shard_map/gather | solution.py:92
  170.1 2.8 reshape.532
  172.9 4.2 fusion.50
  177.0 5.8 copy.84
  184.3 5.8 copy.85
  191.5 9.2 %multiply_convert_fusion = bf16[1024,4096]{1,0:T(8,128)(2,1)S(1)} fusion(bf16[1024,400]{0,1:T(8,128)(2,1)} %collective-permute-done.2, bf16[1024,400]{0,1:T(8,128)(2,1)} %collective-permute-done.1, bf16[1024,400]{0,1:T(8,128)(2,1)} %collective-permute-done, bf16[1024,400]{0,1:T(8,128)(2,1)} %constant_dynamic-slice_fusion.7, ...), kind=kOutput, calls=%fused_computation.11 | convolution fusion | flops 3391160320 | bytes 13303808 | tf_op jit(solution)/shard_map/dot_general | solution.py:102
  200.7 8.8 %fusion.7 = f32[1024,400]{0,1:T(8,128)S(1)} fusion(bf16[1024,4096]{1,0:T(8,128)(2,1)S(1)} %multiply_convert_fusion, bf16[1024,1,400]{0,2,1:T(8,128)(2,1)S(1)} %copy-done.7, f32[1024]{0:T(1024)S(1)} %divide_add_fusion, bf16[1024,400]{0,1:T(8,128)(2,1)} %collective-permute-done.2, bf16[1024,400]{0,1:T(8,128)(2,1)} %collective-permute-done.1, ...), kind=kOutput, calls=%fused_computation.26 | convolution fusion | flops 3369779200 | bytes 14127104 | tf_op jit(solution)/shard_map/dot_general | solution.py:106
  212.2 4.6 copy.68
  216.8 6.2 reshape.610
  223.0 13.4 %scatter_custom_fusion.1 = f32[4096,400]{1,0:T(8,128)} fusion(s32[2048]{0:T(1024)S(1)} %bitcast.143, f32[2048,400]{1,0:T(8,128)} %reshape.610, f32[]{:T(128)} %constant.259.clone.1), kind=kCustom, calls=%fused_computation.14 | custom fusion | bytes 6554112 | tf_op jit(solution)/shard_map/scatter | solution.py:139
  236.4 10.1 %reshape.534 = f32[64,8,3200]{2,1,0:T(8,128)} reshape(f32[4096,400]{1,0:T(8,128)} %scatter_custom_fusion.1) | data formatting | bytes 13107200 | tf_op jit(solution)/shard_map/reshape | solution.py:140
  246.4 6.1 all-to-all-start.2
  254.6 8.0 %scatter_custom_fusion.3 = f32[1536,400]{1,0:T(8,128)S(1)} fusion(s32[1024]{0:T(1024)S(1)} %get-tuple-element.41, f32[1024,400]{1,0:T(8,128)} %copy.71, f32[]{:T(128)} %constant.259.clone.1), kind=kCustom, calls=%fused_computation.35 | custom fusion | flops 409600 | bytes 2458112 | tf_op jit(solution)/shard_map/scatter-add | solution.py:124
  269.7 2.5 collective-permute-start.7
  273.6 11.3 %collective-permute-done.6 = f32[384,400]{0,1:T(8,128)S(1)} collective-permute-done((f32[384,400]{0,1:T(8,128)}, f32[384,400]{0,1:T(8,128)S(1)}, u32[]{:S(2)}, u32[]{:S(2)}) %collective-permute-start.6) | collective-permute-done | bytes 614432 | tf_op jit(solution)/shard_map/ppermute | solution.py:13
  284.9 14.2 %collective-permute-done.7 = f32[384,400]{0,1:T(8,128)} collective-permute-done((f32[384,400]{0,1:T(8,128)S(1)}, f32[384,400]{0,1:T(8,128)}, u32[]{:S(2)}, u32[]{:S(2)}) %collective-permute-start.7) | collective-permute-done | bytes 614432 | tf_op jit(solution)/shard_map/ppermute | solution.py:13
  314.9 3.5 collective-permute-start.13
  320.7 7.6 %collective-permute-start.18 = (f32[6,400]{1,0:T(8,128)S(1)}, f32[6,400]{1,0:T(8,128)S(1)}, u32[]{:S(2)}, u32[]{:S(2)}) collective-permute-start(f32[6,400]{1,0:T(8,128)S(1)} %get-tuple-element.36), channel_id=1, source_target_pairs={{0,12},{1,13},{2,14},{3,15},{4,0},{5,1},{6,2},{7,3},{8,4},{9,5},{1... | collective-permute-start | bytes 28808 | tf_op jit(solution)/shard_map/ppermute | solution.py:45
  330.5 63.0 %collective-permute-done.13 = f32[6,400]{1,0:T(8,128)S(1)} collective-permute-done((f32[6,400]{1,0:T(8,128)S(1)}, f32[6,400]{1,0:T(8,128)S(1)}, u32[]{:S(2)}, u32[]{:S(2)}) %collective-permute-start.13) | collective-permute-done | bytes 9632 | tf_op jit(solution)/shard_map/ppermute | solution.py:45
  393.5 4.4 collective-permute-start.15
  397.9 2.8 collective-permute-start.14
  402.8 2.6 collective-permute-start.20
  406.1 3.5 collective-permute-start.24
  414.2 3.5 collective-permute-done.21
  422.0 2.6 collective-permute-start.29
  426.2 3.4 collective-permute-done.28
  431.3 6.6 %collective-permute-start.30 = (f32[192,400]{1,0:T(8,128)S(1)}, f32[192,400]{1,0:T(8,128)S(1)}, u32[]{:S(2)}, u32[]{:S(2)}) collective-permute-start(f32[192,400]{1,0:T(8,128)S(1)} %bitcast_select_fusion), channel_id=1, source_target_pairs={{0,1},{1,0},{2,3},{3,2},{4,5},{5,4},{6,7},{7,6},{8,9},{9,8},{10,11... | collective-permute-start | bytes 921608 | tf_op jit(solution)/shard_map/ppermute | solution.py:48
  441.1 2.5 collective-permute-start.33
  443.6 5.9 fusion.18
  449.6 2.5 fusion.49
  456.0 2.5 collective-permute-start.32
  458.9 80.7 %collective-permute-done.32 = f32[384,400]{0,1:T(8,128)S(1)} collective-permute-done((f32[384,400]{0,1:T(8,128)}, f32[384,400]{0,1:T(8,128)S(1)}, u32[]{:S(2)}, u32[]{:S(2)}) %collective-permute-start.32) | collective-permute-done | bytes 614432 | tf_op jit(solution)/shard_map/ppermute | solution.py:13
  539.6 14.5 %collective-permute-done.31 = f32[384,400]{0,1:T(8,128)} collective-permute-done((f32[384,400]{0,1:T(8,128)}, f32[384,400]{0,1:T(8,128)}, u32[]{:S(2)}, u32[]{:S(2)}) %collective-permute-start.31) | collective-permute-done | bytes 614432 | tf_op jit(solution)/shard_map/ppermute | solution.py:13
  561.2 11.9 %reshape.618 = f32[4096,400]{1,0:T(8,128)} reshape(f32[64,8,3200]{2,1,0:T(8,128)} %all-to-all-done.2) | data formatting | bytes 13107200 | tf_op jit(solution)/shard_map/reshape | solution.py:142
  573.1 29.8 %scatter_custom_fusion.2 = f32[2048,400]{1,0:T(8,128)} fusion(s32[4096]{0:T(1024)S(1)} %bitcast.145, f32[4096,400]{1,0:T(8,128)} %reshape.618, f32[]{:T(128)} %constant.259.clone.1), kind=kCustom, calls=%fused_computation.21 | custom fusion | flops 1638400 | bytes 3277312 | tf_op jit(solution)/shard_map/scatter-add | solution.py:147
  606.3 5.6 fusion.10
  615.3 5.2 copy.81
  (181 shorter events, 83.5 us)
Async XLA Ops:
  14.7 22.4 %all-to-all-start = ((s32[64,1,64]{2,1,0:T(1,128)}), s32[64,1,64]{2,1,0:T(1,128)S(1)}, u32[]{:S(2)}, u32[]{:S(2)}) async-start(s32[64,1,64]{2,1,0:T(1,128)} %all_to_all.14), calls=%async_computation | async-start | bytes 65536 | tf_op jit(solution)/shard_map/all_to_all | solution.py:88
  64.7 6.6 %copy-start.6 = (bf16[2048,400]{0,1:T(8,128)(2,1)S(1)}, bf16[2048,400]{0,1:T(8,128)(2,1)}, u32[]{:S(2)}) copy-start(bf16[2048,400]{0,1:T(8,128)(2,1)} %param.6) | copy-start | bytes 4915204
  64.7 11.4 %copy-start.12 = (bf16[1345,400]{0,1:T(8,128)(2,1)S(1)}, bf16[1345,400]{0,1:T(8,128)(2,1)}, u32[]{:S(2)}) copy-start(bf16[1345,400]{0,1:T(8,128)(2,1)} %param.7) | copy-start | bytes 3228004
  64.7 82.2 %all-to-all-start.1 = ((bf16[64,200,128]{2,1,0:T(8,128)(2,1)}), bf16[64,200,128]{2,1,0:T(8,128)(2,1)}, u32[]{:S(2)}, u32[]{:S(2)}) async-start(bf16[64,200,128]{2,1,0:T(8,128)(2,1)} %reshape.530), calls=%async_computation.1 | async-start | bytes 6553600 | tf_op jit(solution)/shard_map/all_to_all | solution.py:91
  70.7 6.3 %copy-start.14 = (s32[1024]{0:T(1024)S(1)}, s32[1024]{0:T(1024)}, u32[]{:S(2)}) copy-start(s32[1024]{0:T(1024)} %param.10) | copy-start | bytes 12292
  72.3 119.2 %collective-permute-start.2 = (bf16[1024,400]{0,1:T(8,128)(2,1)}, bf16[1024,400]{0,1:T(8,128)(2,1)}, u32[]{:S(2)}, u32[]{:S(2)}) collective-permute-start(bf16[1024,400]{0,1:T(8,128)(2,1)} %constant_dynamic-slice_fusion.7), channel_id=1, source_target_pairs={{0,192},{64,0},{128,64},{192,128},{1,193},{65,1},{129,65},{193,129... | collective-permute-start | bytes 2457608 | tf_op jit(solution)/shard_map/ppermute | solution.py:13
  74.8 116.7 %collective-permute-start.1 = (bf16[1024,400]{0,1:T(8,128)(2,1)}, bf16[1024,400]{0,1:T(8,128)(2,1)}, u32[]{:S(2)}, u32[]{:S(2)}) collective-permute-start(bf16[1024,400]{0,1:T(8,128)(2,1)} %constant_dynamic-slice_fusion.7), channel_id=1, source_target_pairs={{0,128},{64,192},{128,0},{192,64},{1,129},{65,193},{129,1},{193,65... | collective-permute-start | bytes 2457608 | tf_op jit(solution)/shard_map/ppermute | solution.py:13
  75.3 116.2 %collective-permute-start = (bf16[1024,400]{0,1:T(8,128)(2,1)}, bf16[1024,400]{0,1:T(8,128)(2,1)}, u32[]{:S(2)}, u32[]{:S(2)}) collective-permute-start(bf16[1024,400]{0,1:T(8,128)(2,1)} %constant_dynamic-slice_fusion.7), channel_id=1, source_target_pairs={{0,64},{64,128},{128,192},{192,0},{1,65},{65,129},{129,193},{193,1... | collective-permute-start | bytes 2457608 | tf_op jit(solution)/shard_map/ppermute | solution.py:13
  182.8 7.2 %copy-start = (f32[1024,400]{0,1:T(8,128)S(1)}, f32[1024,400]{0,1:T(8,128)}, u32[]{:S(2)}) copy-start(f32[1024,400]{0,1:T(8,128)} %convert_element_type.40) | copy-start | bytes 4915204
  190.5 20.8 %copy-start.1 = (f32[1024,200]{0,1:T(8,128)}, f32[1024,200]{0,1:T(8,128)S(1)}, u32[]{:S(2)}) copy-start(f32[1024,200]{0,1:T(8,128)S(1)} %get-tuple-element.19) | copy-start | bytes 2457604
  190.5 20.8 %copy-start.3 = (f32[1024,200]{0,1:T(8,128)}, f32[1024,200]{0,1:T(8,128)S(1)}, u32[]{:S(2)}) copy-start(f32[1024,200]{0,1:T(8,128)S(1)} %get-tuple-element.20) | copy-start | bytes 2457604
  200.7 8.9 %copy-start.15 = (bf16[1024,4096]{1,0:T(8,128)(2,1)}, bf16[1024,4096]{1,0:T(8,128)(2,1)S(1)}, u32[]{:S(2)}) copy-start(bf16[1024,4096]{1,0:T(8,128)(2,1)S(1)} %multiply_convert_fusion) | copy-start | bytes 25165828
  246.4 6.2 copy-start.8
  246.4 6.2 copy-start.9
  246.4 314.8 %all-to-all-start.2 = ((f32[64,8,3200]{2,1,0:T(8,128)}), f32[64,8,3200]{2,1,0:T(8,128)}, u32[]{:S(2)}, u32[]{:S(2)}) async-start(f32[64,8,3200]{2,1,0:T(8,128)} %reshape.534), calls=%async_computation.2 | async-start | bytes 13107200 | tf_op jit(solution)/shard_map/all_to_all | solution.py:141
  264.4 8.9 %copy-start.10 = (f32[1,384,400]{2,1,0:T(8,128)S(1)}, f32[1,384,400]{2,1,0:T(8,128)}, u32[]{:S(2)}) copy-start(f32[1,384,400]{2,1,0:T(8,128)} %get-tuple-element.21) | copy-start | bytes 1843204
  268.3 16.6 %collective-permute-start.6 = (f32[384,400]{0,1:T(8,128)}, f32[384,400]{0,1:T(8,128)S(1)}, u32[]{:S(2)}, u32[]{:S(2)}) collective-permute-start(f32[384,400]{0,1:T(8,128)} %bitcast.132), channel_id=1, source_target_pairs={{0,64},{64,128},{128,192},{192,0},{1,65},{65,129},{129,193},{193,1... | collective-permute-start | bytes 1843208 | tf_op jit(solution)/shard_map/ppermute | solution.py:13
  269.7 29.4 %collective-permute-start.7 = (f32[384,400]{0,1:T(8,128)S(1)}, f32[384,400]{0,1:T(8,128)}, u32[]{:S(2)}, u32[]{:S(2)}) collective-permute-start(f32[384,400]{0,1:T(8,128)S(1)} %bitcast.131), channel_id=1, source_target_pairs={{0,128},{64,192},{128,0},{192,64},{1,129},{65,193},{129,1},{193,65... | collective-permute-start | bytes 1843208 | tf_op jit(solution)/shard_map/ppermute | solution.py:13
  272.1 26.9 %collective-permute-start.8 = (f32[384,400]{0,1:T(8,128)S(1)}, f32[384,400]{0,1:T(8,128)}, u32[]{:S(2)}, u32[]{:S(2)}) collective-permute-start(f32[384,400]{0,1:T(8,128)S(1)} %bitcast.130), channel_id=1, source_target_pairs={{0,192},{64,0},{128,64},{192,128},{1,193},{65,1},{129,65},{193,129... | collective-permute-start | bytes 1843208 | tf_op jit(solution)/shard_map/ppermute | solution.py:13
  302.4 2.8 collective-permute-start.9
  305.3 6.2 %collective-permute-start.10 = (f32[48,400]{1,0:T(8,128)S(1)}, f32[48,400]{1,0:T(8,128)S(1)}, u32[]{:S(2)}, u32[]{:S(2)}) collective-permute-start(f32[48,400]{1,0:T(8,128)S(1)} %get-tuple-element.31), channel_id=1, source_target_pairs={{0,16},{1,17},{2,18},{3,19},{4,20},{5,21},{6,22},{7,23},{8,24},{9,... | collective-permute-start | bytes 230408 | tf_op jit(solution)/shard_map/ppermute | solution.py:45
  306.8 5.5 collective-permute-start.12
  308.3 6.5 %collective-permute-start.11 = (f32[48,400]{1,0:T(8,128)S(1)}, f32[48,400]{1,0:T(8,128)S(1)}, u32[]{:S(2)}, u32[]{:S(2)}) collective-permute-start(f32[48,400]{1,0:T(8,128)S(1)} %get-tuple-element.33), channel_id=1, source_target_pairs={{0,32},{1,33},{2,34},{3,35},{4,36},{5,37},{6,38},{7,39},{8,40},{9,... | collective-permute-start | bytes 230408 | tf_op jit(solution)/shard_map/ppermute | solution.py:45
  314.9 78.7 %collective-permute-start.13 = (f32[6,400]{1,0:T(8,128)S(1)}, f32[6,400]{1,0:T(8,128)S(1)}, u32[]{:S(2)}, u32[]{:S(2)}) collective-permute-start(f32[6,400]{1,0:T(8,128)S(1)} %get-tuple-element.34), channel_id=1, source_target_pairs={{0,2},{1,3},{2,4},{3,5},{4,6},{5,7},{6,8},{7,9},{8,10},{9,11},{10,... | collective-permute-start | bytes 28808 | tf_op jit(solution)/shard_map/ppermute | solution.py:45
  318.4 79.6 %collective-permute-start.19 = (f32[6,400]{1,0:T(8,128)S(1)}, f32[6,400]{1,0:T(8,128)S(1)}, u32[]{:S(2)}, u32[]{:S(2)}) collective-permute-start(f32[6,400]{1,0:T(8,128)S(1)} %get-tuple-element.35), channel_id=1, source_target_pairs={{0,14},{1,15},{2,0},{3,1},{4,2},{5,3},{6,4},{7,5},{8,6},{9,7},{10,... | collective-permute-start | bytes 28808 | tf_op jit(solution)/shard_map/ppermute | solution.py:45
  320.7 80.1 %collective-permute-start.18 = (f32[6,400]{1,0:T(8,128)S(1)}, f32[6,400]{1,0:T(8,128)S(1)}, u32[]{:S(2)}, u32[]{:S(2)}) collective-permute-start(f32[6,400]{1,0:T(8,128)S(1)} %get-tuple-element.36), channel_id=1, source_target_pairs={{0,12},{1,13},{2,14},{3,15},{4,0},{5,1},{6,2},{7,3},{8,4},{9,5},{1... | collective-permute-start | bytes 28808 | tf_op jit(solution)/shard_map/ppermute | solution.py:45
  328.3 72.5 %collective-permute-start.17 = (f32[6,400]{1,0:T(8,128)S(1)}, f32[6,400]{1,0:T(8,128)S(1)}, u32[]{:S(2)}, u32[]{:S(2)}) collective-permute-start(f32[6,400]{1,0:T(8,128)S(1)} %get-tuple-element.37), channel_id=1, source_target_pairs={{0,10},{1,11},{2,12},{3,13},{4,14},{5,15},{6,0},{7,1},{8,2},{9,3},... | collective-permute-start | bytes 28808 | tf_op jit(solution)/shard_map/ppermute | solution.py:45
  330.5 70.4 %collective-permute-start.16 = (f32[6,400]{1,0:T(8,128)S(1)}, f32[6,400]{1,0:T(8,128)S(1)}, u32[]{:S(2)}, u32[]{:S(2)}) collective-permute-start(f32[6,400]{1,0:T(8,128)S(1)} %get-tuple-element.38), channel_id=1, source_target_pairs={{0,8},{1,9},{2,10},{3,11},{4,12},{5,13},{6,14},{7,15},{8,0},{9,1},... | collective-permute-start | bytes 28808 | tf_op jit(solution)/shard_map/ppermute | solution.py:45
  393.5 7.3 %collective-permute-start.15 = (f32[6,400]{1,0:T(8,128)S(1)}, f32[6,400]{1,0:T(8,128)S(1)}, u32[]{:S(2)}, u32[]{:S(2)}) collective-permute-start(f32[6,400]{1,0:T(8,128)S(1)} %get-tuple-element.39), channel_id=1, source_target_pairs={{0,6},{1,7},{2,8},{3,9},{4,10},{5,11},{6,12},{7,13},{8,14},{9,15},... | collective-permute-start | bytes 28808 | tf_op jit(solution)/shard_map/ppermute | solution.py:45
  397.9 4.9 collective-permute-start.14
  402.8 9.0 %collective-permute-start.20 = (f32[6,400]{1,0:T(8,128)S(1)}, f32[6,400]{1,0:T(8,128)S(1)}, u32[]{:S(2)}, u32[]{:S(2)}) collective-permute-start(f32[6,400]{1,0:T(8,128)S(1)} %get-tuple-element.11), channel_id=1, source_target_pairs={{0,2},{1,3},{2,4},{3,5},{4,6},{5,7},{6,8},{7,9},{8,10},{9,11},{10,... | collective-permute-start | bytes 28808 | tf_op jit(solution)/shard_map/ppermute | solution.py:48
  406.0 12.9 %collective-permute-start.25 = (f32[6,400]{1,0:T(8,128)S(1)}, f32[6,400]{1,0:T(8,128)S(1)}, u32[]{:S(2)}, u32[]{:S(2)}) collective-permute-start(f32[6,400]{1,0:T(8,128)S(1)} %get-tuple-element.11), channel_id=1, source_target_pairs={{0,12},{1,13},{2,14},{3,15},{4,0},{5,1},{6,2},{7,3},{8,4},{9,5},{1... | collective-permute-start | bytes 28808 | tf_op jit(solution)/shard_map/ppermute | solution.py:48
  406.1 12.8 %collective-permute-start.24 = (f32[6,400]{1,0:T(8,128)S(1)}, f32[6,400]{1,0:T(8,128)S(1)}, u32[]{:S(2)}, u32[]{:S(2)}) collective-permute-start(f32[6,400]{1,0:T(8,128)S(1)} %get-tuple-element.11), channel_id=1, source_target_pairs={{0,10},{1,11},{2,12},{3,13},{4,14},{5,15},{6,0},{7,1},{8,2},{9,3},... | collective-permute-start | bytes 28808 | tf_op jit(solution)/shard_map/ppermute | solution.py:48
  409.6 9.2 %collective-permute-start.23 = (f32[6,400]{1,0:T(8,128)S(1)}, f32[6,400]{1,0:T(8,128)S(1)}, u32[]{:S(2)}, u32[]{:S(2)}) collective-permute-start(f32[6,400]{1,0:T(8,128)S(1)} %get-tuple-element.11), channel_id=1, source_target_pairs={{0,8},{1,9},{2,10},{3,11},{4,12},{5,13},{6,14},{7,15},{8,0},{9,1},... | collective-permute-start | bytes 28808 | tf_op jit(solution)/shard_map/ppermute | solution.py:48
  411.8 7.0 %collective-permute-start.22 = (f32[6,400]{1,0:T(8,128)S(1)}, f32[6,400]{1,0:T(8,128)S(1)}, u32[]{:S(2)}, u32[]{:S(2)}) collective-permute-start(f32[6,400]{1,0:T(8,128)S(1)} %get-tuple-element.11), channel_id=1, source_target_pairs={{0,6},{1,7},{2,8},{3,9},{4,10},{5,11},{6,12},{7,13},{8,14},{9,15},... | collective-permute-start | bytes 28808 | tf_op jit(solution)/shard_map/ppermute | solution.py:48
  411.9 5.8 collective-permute-start.21
  417.7 3.6 collective-permute-start.26
  422.0 4.2 collective-permute-start.29
  424.6 5.1 collective-permute-start.28
  424.9 5.7 collective-permute-start.27
  431.3 8.0 %collective-permute-start.30 = (f32[192,400]{1,0:T(8,128)S(1)}, f32[192,400]{1,0:T(8,128)S(1)}, u32[]{:S(2)}, u32[]{:S(2)}) collective-permute-start(f32[192,400]{1,0:T(8,128)S(1)} %bitcast_select_fusion), channel_id=1, source_target_pairs={{0,1},{1,0},{2,3},{3,2},{4,5},{5,4},{6,7},{7,6},{8,9},{9,8},{10,11... | collective-permute-start | bytes 921608 | tf_op jit(solution)/shard_map/ppermute | solution.py:48
  441.1 17.4 %collective-permute-start.33 = (f32[384,400]{0,1:T(8,128)}, f32[384,400]{0,1:T(8,128)S(1)}, u32[]{:S(2)}, u32[]{:S(2)}) collective-permute-start(f32[384,400]{0,1:T(8,128)} %broadcast_select_fusion), channel_id=1, source_target_pairs={{0,192},{64,0},{128,64},{192,128},{1,193},{65,1},{129,65},{193,129... | collective-permute-start | bytes 1843208 | tf_op jit(solution)/shard_map/ppermute | solution.py:13
  453.8 152.4 %collective-permute-start.3 = (f32[1024,400]{0,1:T(8,128)}, f32[1024,400]{0,1:T(8,128)}, u32[]{:S(2)}, u32[]{:S(2)}) collective-permute-start(f32[1024,400]{0,1:T(8,128)} %get-tuple-element.12), channel_id=1, source_target_pairs={{0,192},{64,0},{128,64},{192,128},{1,193},{65,1},{129,65},{193,129... | collective-permute-start | bytes 4915208 | tf_op jit(solution)/shard_map/ppermute | solution.py:13
  454.4 151.9 %collective-permute-start.5 = (f32[1024,400]{0,1:T(8,128)}, f32[1024,400]{0,1:T(8,128)}, u32[]{:S(2)}, u32[]{:S(2)}) collective-permute-start(f32[1024,400]{0,1:T(8,128)} %get-tuple-element.13), channel_id=1, source_target_pairs={{0,64},{64,128},{128,192},{192,0},{1,65},{65,129},{129,193},{193,1... | collective-permute-start | bytes 4915208 | tf_op jit(solution)/shard_map/ppermute | solution.py:13
  455.5 150.7 %collective-permute-start.4 = (f32[1024,400]{0,1:T(8,128)}, f32[1024,400]{0,1:T(8,128)}, u32[]{:S(2)}, u32[]{:S(2)}) collective-permute-start(f32[1024,400]{0,1:T(8,128)} %get-tuple-element.14), channel_id=1, source_target_pairs={{0,128},{64,192},{128,0},{192,64},{1,129},{65,193},{129,1},{193,65... | collective-permute-start | bytes 4915208 | tf_op jit(solution)/shard_map/ppermute | solution.py:13
  456.0 83.6 %collective-permute-start.32 = (f32[384,400]{0,1:T(8,128)}, f32[384,400]{0,1:T(8,128)S(1)}, u32[]{:S(2)}, u32[]{:S(2)}) collective-permute-start(f32[384,400]{0,1:T(8,128)} %broadcast_select_fusion), channel_id=1, source_target_pairs={{0,128},{64,192},{128,0},{192,64},{1,129},{65,193},{129,1},{193,65... | collective-permute-start | bytes 1843208 | tf_op jit(solution)/shard_map/ppermute | solution.py:13
  458.5 95.6 %collective-permute-start.31 = (f32[384,400]{0,1:T(8,128)}, f32[384,400]{0,1:T(8,128)}, u32[]{:S(2)}, u32[]{:S(2)}) collective-permute-start(f32[384,400]{0,1:T(8,128)} %broadcast_select_fusion), channel_id=1, source_target_pairs={{0,64},{64,128},{128,192},{192,0},{1,65},{65,129},{129,193},{193,1... | collective-permute-start | bytes 1843208 | tf_op jit(solution)/shard_map/ppermute | solution.py:13
  539.6 14.5 %copy-start.13 = (f32[384,400]{0,1:T(8,128)}, f32[384,400]{0,1:T(8,128)S(1)}, u32[]{:S(2)}) copy-start(f32[384,400]{0,1:T(8,128)S(1)} %collective-permute-done.32) | copy-start | bytes 1843204
  (5 other events, 16.7 us)

commit v6 on v3

--- a/solution.py
+++ b/solution.py
@@ -93,21 +93,19 @@
         outgoing_quarter = lax.dynamic_index_in_dim(quarters, (me_blk + d) % n_blk, 0, keepdims=False)
         mine = mine + shifted(outgoing_quarter, "blk", n_blk, d)
 
-    sub = 8
-    grad_lanes = capacity * width // sub
-    rel_lanes = -(-per_peer // (sub * LANE)) * LANE
-    end_grads = jnp.stack([source_grad, target_grad], axis=1).reshape(2 * edges, width)
-    outgoing = jnp.zeros((n_shard * capacity, width), jnp.float32).at[slots].set(end_grads)
-    rel_out = jnp.pad(mine, ((0, 0), (0, sub * rel_lanes - per_peer))).reshape(n_shard, sub, rel_lanes)
-    payload = jnp.concatenate([outgoing.reshape(n_shard, sub, grad_lanes), rel_out], axis=2)
-    arrived = lax.all_to_all(payload, "shard", split_axis=0, concat_axis=0, tiled=True)
-    arrived_grads = arrived[:, :, :grad_lanes].reshape(n_shard * capacity, width)
-    piece = arrived[:, :, grad_lanes:].reshape(n_shard, sub * rel_lanes)[:, :per_peer].sum(axis=0)
-
-    quarter = spread(piece, "shard", n_shard)
+    small = lax.all_to_all(mine, "shard", 0, 0, tiled=False).sum(axis=0)
+    quarter = spread(small, "shard", n_shard)
     held = jnp.stack([quarter] + [shifted(quarter, "blk", n_blk, d) for d in range(1, n_blk)])
     order = (me_blk - jnp.arange(n_blk, dtype=jnp.int32)) % n_blk
     relation_grad = jnp.take(held, order, axis=0).reshape(-1)[:total].reshape(rel_rows_n, width)
+
+    sub = 8
+    grad_lanes = capacity * width // sub
+    end_grads = jnp.stack([source_grad, target_grad], axis=1).reshape(2 * edges, width)
+    outgoing = jnp.zeros((n_shard * capacity, width), jnp.float32).at[slots].set(end_grads)
+    payload = outgoing.reshape(n_shard, sub, grad_lanes)
+    arrived = lax.all_to_all(payload, "shard", split_axis=0, concat_axis=0, tiled=True)
+    arrived_grads = arrived.reshape(n_shard * capacity, width)
 
     entity_grad = (
         jnp.zeros((rows_own, width), jnp.float32)

time: 560 us -> 552 us (0.986)
  waiting for transfers between devices: 250 us -> 225 us
  blocking collectives: 0 us -> 24.2 us
  local copies, waits for them, and re-layouts: 166 us -> 159 us
  other arithmetic: 61.5 us -> 55 us
    all_to_all x1, waiting for transfers between devices: 150 us -> 30.5 us  [shards(): lax.all_to_all(payload, 'shard', split_axis=0, concat_axis=0, tiled=True)]
    ppermute x12, waiting for transfers between devices: 9.57 us -> 105 us  [shifted(): return lax.ppermute(value, axis, [(i, (i + by) % n) for i in range(n)])]
    all_to_all x0 -> x1, blocking collectives: none -> 24.2 us  [shards(): small = lax.all_to_all(mine, 'shard', 0, 0, tiled=False).sum(axis=0)]
    slice x2 -> x0, local copies, waits for them, and re-layouts: 7.27 us -> none  [the longest x1 6.08 us: shards(): arrived[:, :, :grad_lanes].reshape(n_shard * capacity, width)]
    concatenate x1 -> x0, other arithmetic: 6.77 us -> none  [shards(): jnp.concatenate([outgoing.reshape(n_shard, sub, grad_lanes), rel_out], ax...]
    unnamed x44 -> x40, local copies, waits for them, and re-layouts: 28.7 us -> 29.4 us
  transfers between devices with their start and end apart: 16 -> 16, of which waited for: 4 -> 6; matrix products, arithmetic and copies ran while one was open for 28% -> 27% of each run, Pallas kernels for 0% -> 0%
where the time goes in v6:
time: 552 us; the launch traced here: 543 us
  waiting for transfers between devices  225 us (41%)
  local copies, waits for them, and re-layouts  159 us (29%)
  other arithmetic  55 us (10%)
  starting transfers between devices  52.7 us (10%)
  matrix products  25.2 us (5%)
  blocking collectives  24.2 us (4%)
    ppermute x12, waiting for transfers between devices, shifted(): return lax.ppermute(value, axis, [(i, (i + by) % n) for i in range(n)])  105 us
    all_to_all x1, waiting for transfers between devices, shards(): lax.all_to_all(table[asked_rows], 'shard', split_axis=0, concat_axis=0, t...  83.3 us
    all_to_all x1, waiting for transfers between devices, shards(): lax.all_to_all(payload, 'shard', split_axis=0, concat_axis=0, tiled=True)  30.5 us
    scatter-add x1, other arithmetic, shards(): entity_grad = jnp.zeros((rows_own, width), jnp.float32).at[asked_rows.res...  29.7 us
    unnamed x40, local copies, waits for them, and re-layouts  29.4 us
    all_to_all x1, blocking collectives, shards(): small = lax.all_to_all(mine, 'shard', 0, 0, tiled=False).sum(axis=0)  24.2 us
    gather x1, local copies, waits for them, and re-layouts, shards(): table[asked_rows]  17.3 us
    ppermute x12, starting transfers between devices, shifted(): return lax.ppermute(value, axis, [(i, (i + by) % n) for i in range(n)])  16.2 us
  transfers between devices with their start and end apart: 16, of which 6 were waited for; matrix products, arithmetic and copies ran while one was open for 27% of the time, Pallas kernels for 0%

profile of v6, /device:TPU:1, one launch (start us, length us, event | category | flops | bytes accessed | tf_op | source)
XLA Modules:
  0.0 543.3 jit_solution(8698712687070107737)
XLA Ops:
  6.0 8.1 %scatter_custom_fusion = s32[4096]{0:T(1024)S(1)} fusion(s32[2048]{0:T(1024)S(1)} %bitcast.57, s32[2048]{0:T(1024)S(1)} %reshape.314, s32[]{:T(128)} %constant.80.clone.1), kind=kCustom, calls=%fused_computation.59 | custom fusion | bytes 16388 | tf_op jit(solution)/shard_map/scatter | solution.py:52
  14.7 13.2 %all-to-all-start = ((s32[64,1,64]{2,1,0:T(1,128)}), s32[64,1,64]{2,1,0:T(1,128)S(1)}, u32[]{:S(2)}, u32[]{:S(2)}) async-start(s32[64,1,64]{2,1,0:T(1,128)} %all_to_all.26), calls=%async_computation | async-start | bytes 65536 | tf_op jit(solution)/shard_map/all_to_all | solution.py:55
  27.9 2.8 copy.28
  30.7 6.4 %all-to-all-done = s32[64,1,64]{2,1,0:T(1,128)S(1)} async-done(((s32[64,1,64]{2,1,0:T(1,128)}), s32[64,1,64]{2,1,0:T(1,128)S(1)}, u32[]{:S(2)}, u32[]{:S(2)}) %all-to-all-start) | async-done | bytes 16416 | tf_op jit(solution)/shard_map/all_to_all | solution.py:55
  37.2 17.3 %gather_fusion = bf16[4096,400]{1,0:T(8,128)(2,1)} fusion(bf16[2048,400]{1,0:T(8,128)(2,1)S(1)} %copy.28, s32[4096]{0:T(1024)S(1)} %broadcast_clamp_fusion), kind=kCustom, calls=%fused_computation | custom fusion | bytes 6569984 | tf_op jit(solution)/shard_map/gather | solution.py:56
  54.5 5.8 %all-to-all-start.1 = ((bf16[64,64,400]{2,1,0:T(8,128)(2,1)}), bf16[64,64,400]{2,1,0:T(8,128)(2,1)}, u32[]{:S(2)}, u32[]{:S(2)}) async-start(bf16[64,64,400]{2,1,0:T(8,128)(2,1)} %bitcast.46), calls=%async_computation.1 | async-start | bytes 8388608 | tf_op jit(solution)/shard_map/all_to_all | solution.py:56
  62.1 2.5 collective-permute-start.2
  67.1 4.0 gather_fusion.2
  73.0 83.3 %all-to-all-done.1 = bf16[64,64,400]{2,1,0:T(8,128)(2,1)} async-done(((bf16[64,64,400]{2,1,0:T(8,128)(2,1)}), bf16[64,64,400]{2,1,0:T(8,128)(2,1)}, u32[]{:S(2)}, u32[]{:S(2)}) %all-to-all-start.1) | async-done | bytes 3276832 | tf_op jit(solution)/shard_map/all_to_all | solution.py:56
  156.3 12.0 %gather_fusion.1 = bf16[2048,400]{1,0:T(8,128)(2,1)} fusion(bf16[4096,400]{1,0:T(8,128)(2,1)} %bitcast.5, s32[2048]{0:T(1024)S(1)} %broadcast_clamp_fusion.1), kind=kCustom, calls=%fused_computation.1 | custom fusion | bytes 3284992 | tf_op jit(solution)/shard_map/gather | solution.py:57
  168.3 2.8 reshape.269
  171.1 4.2 fusion.31
  175.3 5.8 %copy.41 = bf16[1024,1,400]{0,2,1:T(8,128)(2,1)} copy(bf16[1024,1,400]{2,1,0:T(2,128)(2,1)} %get-tuple-element.19) | data formatting | bytes 1638400
  182.5 5.8 %copy.42 = bf16[1024,1,400]{0,2,1:T(8,128)(2,1)} copy(bf16[1024,1,400]{2,1,0:T(2,128)(2,1)} %get-tuple-element.18) | data formatting | bytes 1638400
  189.7 9.2 %multiply_convert_fusion = bf16[1024,4096]{1,0:T(8,128)(2,1)S(1)} fusion(bf16[1024,400]{0,1:T(8,128)(2,1)} %collective-permute-done.2, bf16[1024,400]{0,1:T(8,128)(2,1)} %collective-permute-done.1, bf16[1024,400]{0,1:T(8,128)(2,1)} %collective-permute-done, bf16[1024,400]{0,1:T(8,128)(2,1)} %constant_dynamic-slice_fusion.1, ...), kind=kOutput, calls=%fused_computation.8 | convolution fusion | flops 3391160320 | bytes 13303808 | tf_op jit(solution)/shard_map/dot_general | solution.py:67
  199.0 8.4 %fusion.7 = f32[1024,400]{0,1:T(8,128)S(1)} fusion(bf16[1024,4096]{1,0:T(8,128)(2,1)S(1)} %multiply_convert_fusion, bf16[1024,1,400]{0,2,1:T(8,128)(2,1)S(1)} %copy-done.9, f32[1024]{0:T(1024)S(1)} %divide_add_fusion, bf16[1024,400]{0,1:T(8,128)(2,1)} %collective-permute-done.2, bf16[1024,400]{0,1:T(8,128)(2,1)} %collective-permute-done.1, ...), kind=kOutput, calls=%fused_computation.22 | convolution fusion | flops 3369779200 | bytes 14127104 | tf_op jit(solution)/shard_map/dot_general | solution.py:71
  207.4 1.8 multiply_add_fusion
  209.4 1.8 copy.36
  211.2 8.1 %scatter_custom_fusion.3 = f32[1345,400]{1,0:T(8,128)S(1)} fusion(s32[1024]{0:T(1024)S(1)} %get-tuple-element.24, f32[1024,400]{1,0:T(8,128)} %copy.36, f32[]{:T(128)} %constant.79.clone.1), kind=kCustom, calls=%fused_computation.31 | custom fusion | flops 409600 | bytes 2152512 | tf_op jit(solution)/shard_map/scatter-add | solution.py:88
  219.2 3.7 reshape.273
  222.9 3.1 pad.4
  226.0 1.8 reshape.274
  233.2 11.0 %collective-permute-done.6 = f32[64,2176]{1,0:T(8,128)S(1)} collective-permute-done((f32[64,2176]{1,0:T(8,128)}, f32[64,2176]{1,0:T(8,128)S(1)}, u32[]{:S(2)}, u32[]{:S(2)}) %collective-permute-start.6) | collective-permute-done | bytes 557088 | tf_op jit(solution)/shard_map/ppermute | solution.py:13
  244.2 13.0 %collective-permute-done.7 = f32[64,2176]{1,0:T(8,128)} collective-permute-done((f32[64,2176]{1,0:T(8,128)S(1)}, f32[64,2176]{1,0:T(8,128)}, u32[]{:S(2)}, u32[]{:S(2)}) %collective-permute-start.7) | collective-permute-done | bytes 557088 | tf_op jit(solution)/shard_map/ppermute | solution.py:13
  259.0 24.2 %all_to_all.40 = f32[64,1,2176]{2,1,0:T(1,128)S(1)} all-to-all(f32[64,1,2176]{2,1,0:T(1,128)S(1)} %all_to_all.31), channel_id=1, replica_groups=mesh['blk'=4,'shard'=64] {'shard'}, dimensions={0} | all-to-all | bytes 1114112 | tf_op jit(solution)/shard_map/all_to_all | solution.py:96
  284.6 6.9 %all-to-all-start.4 = ((f32[64,1,2176]{2,1,0:T(1,128)}), f32[64,1,2176]{2,1,0:T(1,128)}, u32[]{:S(2)}, u32[]{:S(2)}) async-start(f32[64,1,2176]{2,1,0:T(1,128)} %broadcast_in_dim.49), calls=%async_computation.4 | async-start | bytes 1114112 | tf_op jit(solution)/shard_map/all_to_all | solution.py:18
  292.5 4.6 copy.33
  297.0 6.2 %reshape.322 = f32[2048,400]{1,0:T(8,128)} reshape(f32[1024,2,400]{2,1,0:T(2,128)} %copy.33) | data formatting | bytes 6553600 | tf_op jit(solution)/shard_map/reshape | solution.py:104
  303.2 13.4 %scatter_custom_fusion.1 = f32[4096,400]{1,0:T(8,128)} fusion(s32[2048]{0:T(1024)S(1)} %bitcast.59, f32[2048,400]{1,0:T(8,128)} %reshape.322, f32[]{:T(128)} %constant.79.clone.1), kind=kCustom, calls=%fused_computation.11 | custom fusion | bytes 6554112 | tf_op jit(solution)/shard_map/scatter | solution.py:105
  316.6 10.1 %reshape.271 = f32[64,8,3200]{2,1,0:T(8,128)} reshape(f32[4096,400]{1,0:T(8,128)} %scatter_custom_fusion.1) | data formatting | bytes 13107200 | tf_op jit(solution)/shard_map/reshape | solution.py:106
  326.7 10.6 %all-to-all-start.2 = ((f32[64,8,3200]{2,1,0:T(8,128)}), f32[64,8,3200]{2,1,0:T(8,128)}, u32[]{:S(2)}, u32[]{:S(2)}) async-start(f32[64,8,3200]{2,1,0:T(8,128)} %reshape.271), calls=%async_computation.2 | async-start | bytes 13107200 | tf_op jit(solution)/shard_map/all_to_all | solution.py:107
  340.4 5.9 %fusion.18 = f32[4096,400]{0,1:T(8,128)S(1)} fusion(bf16[1024,4096]{1,0:T(8,128)(2,1)} %copy-done.14, f32[1024,200]{0,1:T(8,128)S(1)} %copy-done.6, f32[1024,200]{0,1:T(8,128)S(1)} %copy-done.3), kind=kOutput, calls=%fused_computation.53 | convolution fusion | flops 3357081600 | bytes 16580608 | tf_op jit(solution)/shard_map/dot_general | solution.py:74
  346.4 2.6 fusion.30
  350.6 3.2 collective-permute-start.3
  354.9 2.1 collective-permute-start.9
  357.9 80.7 %collective-permute-done.9 = f32[64,2176]{1,0:T(8,128)S(1)} collective-permute-done((f32[64,2176]{1,0:T(8,128)S(1)}, f32[64,2176]{1,0:T(8,128)S(1)}, u32[]{:S(2)}, u32[]{:S(2)}) %collective-permute-start.9) | collective-permute-done | bytes 557088 | tf_op jit(solution)/shard_map/ppermute | solution.py:13
  438.7 2.1 gather_fusion.3
  440.7 1.8 broadcast_select_fusion
  444.1 3.1 slice.76
  447.2 4.0 reshape.275
  451.1 2.1 copy.38
  453.3 30.5 %all-to-all-done.2 = f32[64,8,3200]{2,1,0:T(8,128)} async-done(((f32[64,8,3200]{2,1,0:T(8,128)}), f32[64,8,3200]{2,1,0:T(8,128)}, u32[]{:S(2)}, u32[]{:S(2)}) %all-to-all-start.2) | async-done | bytes 6553632 | tf_op jit(solution)/shard_map/all_to_all | solution.py:107
  483.8 11.9 %reshape.330 = f32[4096,400]{1,0:T(8,128)} reshape(f32[64,8,3200]{2,1,0:T(8,128)} %all-to-all-done.2) | data formatting | bytes 13107200 | tf_op jit(solution)/shard_map/reshape | solution.py:108
  495.6 29.7 %scatter_custom_fusion.2 = f32[2048,400]{1,0:T(8,128)} fusion(s32[4096]{0:T(1024)S(1)} %bitcast.61, f32[4096,400]{1,0:T(8,128)} %reshape.330, f32[]{:T(128)} %constant.79.clone.1), kind=kCustom, calls=%fused_computation.17 | custom fusion | flops 1638400 | bytes 3277312 | tf_op jit(solution)/shard_map/scatter-add | solution.py:113
  525.3 1.8 constant_dynamic-slice_fusion
  528.7 5.6 %fusion.10 = f32[1024,400]{0,1:T(8,128)} fusion(f32[1024,400]{0,1:T(8,128)} %copy.43, f32[1024,400]{0,1:T(8,128)} %collective-permute-done.5, f32[1024,400]{0,1:T(8,128)} %collective-permute-done.4, f32[1024,400]{0,1:T(8,128)} %collective-permute-done.3, f32[4096,400]{0,1:T(8,128)} %copy-done.7), kind=kLoop, calls=%fused_computation.26 | loop fusion | flops 1638400 | bytes 9830400 | tf_op jit(solution)/shard_map/add | solution.py:116
  534.4 1.8 copy.35
  537.7 5.2 copy.37
  (94 shorter events, 35.4 us)
Async XLA Ops:
  14.7 22.4 %all-to-all-start = ((s32[64,1,64]{2,1,0:T(1,128)}), s32[64,1,64]{2,1,0:T(1,128)S(1)}, u32[]{:S(2)}, u32[]{:S(2)}) async-start(s32[64,1,64]{2,1,0:T(1,128)} %all_to_all.26), calls=%async_computation | async-start | bytes 65536 | tf_op jit(solution)/shard_map/all_to_all | solution.py:55
  54.5 6.6 %copy-start.8 = (bf16[2048,400]{0,1:T(8,128)(2,1)S(1)}, bf16[2048,400]{0,1:T(8,128)(2,1)}, u32[]{:S(2)}) copy-start(bf16[2048,400]{0,1:T(8,128)(2,1)} %param.6) | copy-start | bytes 4915204
  54.5 101.8 %all-to-all-start.1 = ((bf16[64,64,400]{2,1,0:T(8,128)(2,1)}), bf16[64,64,400]{2,1,0:T(8,128)(2,1)}, u32[]{:S(2)}, u32[]{:S(2)}) async-start(bf16[64,64,400]{2,1,0:T(8,128)(2,1)} %bitcast.46), calls=%async_computation.1 | async-start | bytes 8388608 | tf_op jit(solution)/shard_map/all_to_all | solution.py:56
  60.4 5.8 %copy-start.12 = (bf16[1345,400]{0,1:T(8,128)(2,1)S(1)}, bf16[1345,400]{0,1:T(8,128)(2,1)}, u32[]{:S(2)}) copy-start(bf16[1345,400]{0,1:T(8,128)(2,1)} %param.7) | copy-start | bytes 3228004
  60.4 6.7 %copy-start.13 = (s32[1024]{0:T(1024)S(1)}, s32[1024]{0:T(1024)}, u32[]{:S(2)}) copy-start(s32[1024]{0:T(1024)} %param.10) | copy-start | bytes 12292
  62.1 127.6 %collective-permute-start.2 = (bf16[1024,400]{0,1:T(8,128)(2,1)}, bf16[1024,400]{0,1:T(8,128)(2,1)}, u32[]{:S(2)}, u32[]{:S(2)}) collective-permute-start(bf16[1024,400]{0,1:T(8,128)(2,1)} %constant_dynamic-slice_fusion.1), channel_id=1, source_target_pairs={{0,192},{64,0},{128,64},{192,128},{1,193},{65,1},{129,65},{193,129... | collective-permute-start | bytes 2457608 | tf_op jit(solution)/shard_map/ppermute | solution.py:13
  64.6 125.1 %collective-permute-start.1 = (bf16[1024,400]{0,1:T(8,128)(2,1)}, bf16[1024,400]{0,1:T(8,128)(2,1)}, u32[]{:S(2)}, u32[]{:S(2)}) collective-permute-start(bf16[1024,400]{0,1:T(8,128)(2,1)} %constant_dynamic-slice_fusion.1), channel_id=1, source_target_pairs={{0,128},{64,192},{128,0},{192,64},{1,129},{65,193},{129,1},{193,65... | collective-permute-start | bytes 2457608 | tf_op jit(solution)/shard_map/ppermute | solution.py:13
  65.1 124.6 %collective-permute-start = (bf16[1024,400]{0,1:T(8,128)(2,1)}, bf16[1024,400]{0,1:T(8,128)(2,1)}, u32[]{:S(2)}, u32[]{:S(2)}) collective-permute-start(bf16[1024,400]{0,1:T(8,128)(2,1)} %constant_dynamic-slice_fusion.1), channel_id=1, source_target_pairs={{0,64},{64,128},{128,192},{192,0},{1,65},{65,129},{129,193},{193,1... | collective-permute-start | bytes 2457608 | tf_op jit(solution)/shard_map/ppermute | solution.py:13
  181.1 7.2 %copy-start = (f32[1024,400]{0,1:T(8,128)S(1)}, f32[1024,400]{0,1:T(8,128)}, u32[]{:S(2)}) copy-start(f32[1024,400]{0,1:T(8,128)} %convert_element_type.42) | copy-start | bytes 4915204
  188.3 1.1 copy-start.9
  188.8 10.2 %copy-start.1 = (f32[1024,200]{0,1:T(8,128)}, f32[1024,200]{0,1:T(8,128)S(1)}, u32[]{:S(2)}) copy-start(f32[1024,200]{0,1:T(8,128)S(1)} %get-tuple-element.13) | copy-start | bytes 2457604
  188.8 10.2 %copy-start.4 = (f32[1024,200]{0,1:T(8,128)}, f32[1024,200]{0,1:T(8,128)S(1)}, u32[]{:S(2)}) copy-start(f32[1024,200]{0,1:T(8,128)S(1)} %get-tuple-element.14) | copy-start | bytes 2457604
  199.0 8.4 %copy-start.14 = (bf16[1024,4096]{1,0:T(8,128)(2,1)}, bf16[1024,4096]{1,0:T(8,128)(2,1)S(1)}, u32[]{:S(2)}) copy-start(bf16[1024,4096]{1,0:T(8,128)(2,1)S(1)} %multiply_convert_fusion) | copy-start | bytes 25165828
  228.9 15.2 %collective-permute-start.6 = (f32[64,2176]{1,0:T(8,128)}, f32[64,2176]{1,0:T(8,128)S(1)}, u32[]{:S(2)}, u32[]{:S(2)}) collective-permute-start(f32[64,2176]{1,0:T(8,128)} %get-tuple-element.15), channel_id=1, source_target_pairs={{0,64},{64,128},{128,192},{192,0},{1,65},{65,129},{129,193},{193,1... | collective-permute-start | bytes 1671176 | tf_op jit(solution)/shard_map/ppermute | solution.py:13
  230.2 14.0 %collective-permute-start.8 = (f32[64,2176]{1,0:T(8,128)}, f32[64,2176]{1,0:T(8,128)}, u32[]{:S(2)}, u32[]{:S(2)}) collective-permute-start(f32[64,2176]{1,0:T(8,128)} %get-tuple-element.16), channel_id=1, source_target_pairs={{0,192},{64,0},{128,64},{192,128},{1,193},{65,1},{129,65},{193,129... | collective-permute-start | bytes 1671176 | tf_op jit(solution)/shard_map/ppermute | solution.py:13
  231.6 25.6 %collective-permute-start.7 = (f32[64,2176]{1,0:T(8,128)S(1)}, f32[64,2176]{1,0:T(8,128)}, u32[]{:S(2)}, u32[]{:S(2)}) collective-permute-start(f32[64,2176]{1,0:T(8,128)S(1)} %get-tuple-element.17), channel_id=1, source_target_pairs={{0,128},{64,192},{128,0},{192,64},{1,129},{65,193},{129,1},{193,65... | collective-permute-start | bytes 1671176 | tf_op jit(solution)/shard_map/ppermute | solution.py:13
  258.5 33.0 %copy-start.10 = (f32[1024,200]{0,1:T(8,128)S(1)}, f32[1024,200]{0,1:T(8,128)}, u32[]{:S(2)}) copy-start(f32[1024,200]{0,1:T(8,128)} %get-tuple-element.20) | copy-start | bytes 2457604
  258.6 33.0 %copy-start.11 = (f32[1024,200]{0,1:T(8,128)S(1)}, f32[1024,200]{0,1:T(8,128)}, u32[]{:S(2)}) copy-start(f32[1024,200]{0,1:T(8,128)} %get-tuple-element.21) | copy-start | bytes 2457604
  284.6 7.2 %copy-start.2 = (f32[1024,200]{0,1:T(8,128)S(1)}, f32[1024,200]{0,1:T(8,128)}, u32[]{:S(2)}) copy-start(f32[1024,200]{0,1:T(8,128)} %copy-done.1) | copy-start | bytes 2457604
  284.6 7.2 %copy-start.5 = (f32[1024,200]{0,1:T(8,128)S(1)}, f32[1024,200]{0,1:T(8,128)}, u32[]{:S(2)}) copy-start(f32[1024,200]{0,1:T(8,128)} %copy-done.4) | copy-start | bytes 2457604
  284.6 42.0 %all-to-all-start.4 = ((f32[64,1,2176]{2,1,0:T(1,128)}), f32[64,1,2176]{2,1,0:T(1,128)}, u32[]{:S(2)}, u32[]{:S(2)}) async-start(f32[64,1,2176]{2,1,0:T(1,128)} %broadcast_in_dim.49), calls=%async_computation.4 | async-start | bytes 1114112 | tf_op jit(solution)/shard_map/all_to_all | solution.py:18
  326.6 13.8 %copy-start.3 = (f32[1024,200]{0,1:T(8,128)S(1)}, f32[1024,200]{0,1:T(8,128)}, u32[]{:S(2)}) copy-start(f32[1024,200]{0,1:T(8,128)} %copy-done.1) | copy-start | bytes 2457604
  326.6 13.8 %copy-start.6 = (f32[1024,200]{0,1:T(8,128)S(1)}, f32[1024,200]{0,1:T(8,128)}, u32[]{:S(2)}) copy-start(f32[1024,200]{0,1:T(8,128)} %copy-done.4) | copy-start | bytes 2457604
  326.7 157.1 %all-to-all-start.2 = ((f32[64,8,3200]{2,1,0:T(8,128)}), f32[64,8,3200]{2,1,0:T(8,128)}, u32[]{:S(2)}, u32[]{:S(2)}) async-start(f32[64,8,3200]{2,1,0:T(8,128)} %reshape.271), calls=%async_computation.2 | async-start | bytes 13107200 | tf_op jit(solution)/shard_map/all_to_all | solution.py:107
  339.8 17.2 %collective-permute-start.10 = (f32[64,2176]{1,0:T(8,128)S(1)}, f32[64,2176]{1,0:T(8,128)S(1)}, u32[]{:S(2)}, u32[]{:S(2)}) collective-permute-start(f32[64,2176]{1,0:T(8,128)S(1)} %bitcast.49), channel_id=1, source_target_pairs={{0,128},{64,192},{128,0},{192,64},{1,129},{65,193},{129,1},{193,65... | collective-permute-start | bytes 1671176 | tf_op jit(solution)/shard_map/ppermute | solution.py:13
  346.4 4.2 copy-start.7
  350.6 178.2 %collective-permute-start.3 = (f32[1024,400]{0,1:T(8,128)}, f32[1024,400]{0,1:T(8,128)}, u32[]{:S(2)}, u32[]{:S(2)}) collective-permute-start(f32[1024,400]{0,1:T(8,128)} %get-tuple-element.6), channel_id=1, source_target_pairs={{0,192},{64,0},{128,64},{192,128},{1,193},{65,1},{129,65},{193,129... | collective-permute-start | bytes 4915208 | tf_op jit(solution)/shard_map/ppermute | solution.py:13
  353.8 175.0 %collective-permute-start.5 = (f32[1024,400]{0,1:T(8,128)}, f32[1024,400]{0,1:T(8,128)}, u32[]{:S(2)}, u32[]{:S(2)}) collective-permute-start(f32[1024,400]{0,1:T(8,128)} %get-tuple-element.7), channel_id=1, source_target_pairs={{0,64},{64,128},{128,192},{192,0},{1,65},{65,129},{129,193},{193,1... | collective-permute-start | bytes 4915208 | tf_op jit(solution)/shard_map/ppermute | solution.py:13
  353.8 175.0 %collective-permute-start.4 = (f32[1024,400]{0,1:T(8,128)}, f32[1024,400]{0,1:T(8,128)}, u32[]{:S(2)}, u32[]{:S(2)}) collective-permute-start(f32[1024,400]{0,1:T(8,128)} %get-tuple-element.8), channel_id=1, source_target_pairs={{0,128},{64,192},{128,0},{192,64},{1,129},{65,193},{129,1},{193,65... | collective-permute-start | bytes 4915208 | tf_op jit(solution)/shard_map/ppermute | solution.py:13
  354.9 83.6 %collective-permute-start.9 = (f32[64,2176]{1,0:T(8,128)S(1)}, f32[64,2176]{1,0:T(8,128)S(1)}, u32[]{:S(2)}, u32[]{:S(2)}) collective-permute-start(f32[64,2176]{1,0:T(8,128)S(1)} %bitcast.50), channel_id=1, source_target_pairs={{0,64},{64,128},{128,192},{192,0},{1,65},{65,129},{129,193},{193,1... | collective-permute-start | bytes 1671176 | tf_op jit(solution)/shard_map/ppermute | solution.py:13
  357.0 81.5 %collective-permute-start.11 = (f32[64,2176]{1,0:T(8,128)S(1)}, f32[64,2176]{1,0:T(8,128)S(1)}, u32[]{:S(2)}, u32[]{:S(2)}) collective-permute-start(f32[64,2176]{1,0:T(8,128)S(1)} %bitcast.51), channel_id=1, source_target_pairs={{0,192},{64,0},{128,64},{192,128},{1,193},{65,1},{129,65},{193,129... | collective-permute-start | bytes 1671176 | tf_op jit(solution)/shard_map/ppermute | solution.py:13

commit v7 on v6

--- a/solution.py
+++ b/solution.py
@@ -54,9 +54,12 @@
     )
     asked_rows = lax.all_to_all(requests, "shard", split_axis=0, concat_axis=0, tiled=True)
     fetched = lax.all_to_all(table[asked_rows], "shard", split_axis=0, concat_axis=0, tiled=True)
-    gotten = fetched.reshape(n_shard * capacity, width)[slots].reshape(edges, 2, width)
-    source = gotten[:, 0].astype(jnp.float32)
-    target = gotten[:, 1].astype(jnp.float32)
+    fetched = fetched.reshape(n_shard * capacity, width)
+    end_slots = slots.reshape(edges, 2)
+    source_slots = end_slots[:, 0]
+    target_slots = end_slots[:, 1]
+    source = fetched[source_slots].astype(jnp.float32)
+    target = fetched[target_slots].astype(jnp.float32)
     rel_rows = relation[rel_ids].astype(jnp.float32)
     s_re, s_im = (source[:, :half], source[:, half:])
     r_re, r_im = (rel_rows[:, :half], rel_rows[:, half:])
@@ -93,7 +96,9 @@
         outgoing_quarter = lax.dynamic_index_in_dim(quarters, (me_blk + d) % n_blk, 0, keepdims=False)
         mine = mine + shifted(outgoing_quarter, "blk", n_blk, d)
 
-    small = lax.all_to_all(mine, "shard", 0, 0, tiled=False).sum(axis=0)
+    small = lax.all_to_all(
+        mine.reshape(n_shard, 1, per_peer), "shard", 0, 0, tiled=True
+    ).sum(axis=(0, 1))
     quarter = spread(small, "shard", n_shard)
     held = jnp.stack([quarter] + [shifted(quarter, "blk", n_blk, d) for d in range(1, n_blk)])
     order = (me_blk - jnp.arange(n_blk, dtype=jnp.int32)) % n_blk
@@ -101,8 +106,13 @@
 
     sub = 8
     grad_lanes = capacity * width // sub
-    end_grads = jnp.stack([source_grad, target_grad], axis=1).reshape(2 * edges, width)
-    outgoing = jnp.zeros((n_shard * capacity, width), jnp.float32).at[slots].set(end_grads)
+    outgoing = (
+        jnp.zeros((n_shard * capacity, width), jnp.float32)
+        .at[source_slots]
+        .set(source_grad)
+        .at[target_slots]
+        .set(target_grad)
+    )
     payload = outgoing.reshape(n_shard, sub, grad_lanes)
     arrived = lax.all_to_all(payload, "shard", split_axis=0, concat_axis=0, tiled=True)
     arrived_grads = arrived.reshape(n_shard * capacity, width)

time: 552 us -> 537 us (0.973)
  local copies, waits for them, and re-layouts: 159 us -> 144 us
    ppermute x12, waiting for transfers between devices: 105 us -> 119 us  [shifted(): return lax.ppermute(value, axis, [(i, (i + by) % n) for i in range(n)])]
    unnamed x40 -> x32, local copies, waits for them, and re-layouts: 29.4 us -> 17.9 us
    all_to_all x1, waiting for transfers between devices: 30.5 us -> 21.7 us  [shards(): lax.all_to_all(payload, 'shard', split_axis=0, concat_axis=0, tiled=True)]
    reshape x2 -> x1, local copies, waits for them, and re-layouts: 9.01 us -> 0.38 us  [shards(): mine.reshape(n_shard, 1, per_peer)]
    scatter x1 -> x2, local copies, waits for them, and re-layouts: 13.4 us -> 20.6 us  [shards(): outgoing = jnp.zeros((n_shard * capacity, width), jnp.float32).at[source_...]
    gather x1 -> x4, local copies, waits for them, and re-layouts: 12 us -> 15.1 us  [the longest x2 7.94 us: shards(): source = fetched[source_slots].astype(jnp.float32)]
  transfers between devices with their start and end apart: 16 -> 16, of which waited for: 6 -> 7; matrix products, arithmetic and copies ran while one was open for 27% -> 25% of each run, Pallas kernels for 0% -> 0%
where the time goes in v7:
time: 537 us; the launch traced here: 529 us
  waiting for transfers between devices  230 us (43%)
  local copies, waits for them, and re-layouts  144 us (27%)
  other arithmetic  54.1 us (10%)
  starting transfers between devices  49.2 us (9%)
  matrix products  25.4 us (5%)
  blocking collectives  24.1 us (4%)
    ppermute x12, waiting for transfers between devices, shifted(): return lax.ppermute(value, axis, [(i, (i + by) % n) for i in range(n)])  119 us
    all_to_all x1, waiting for transfers between devices, shards(): lax.all_to_all(table[asked_rows], 'shard', split_axis=0, concat_axis=0, t...  83.2 us
    scatter-add x1, other arithmetic, shards(): entity_grad = jnp.zeros((rows_own, width), jnp.float32).at[asked_rows.res...  29.6 us
    all_to_all x1, blocking collectives, shards(): lax.all_to_all(mine.reshape(n_shard, 1, per_peer), 'shard', 0, 0, tiled=T...  24.1 us
    all_to_all x1, waiting for transfers between devices, shards(): lax.all_to_all(payload, 'shard', split_axis=0, concat_axis=0, tiled=True)  21.7 us
    scatter x2, local copies, waits for them, and re-layouts, shards(): outgoing = jnp.zeros((n_shard * capacity, width), jnp.float32).at[source_...  20.6 us
    unnamed x32, local copies, waits for them, and re-layouts  17.9 us
    gather x1, local copies, waits for them, and re-layouts, shards(): table[asked_rows]  17.4 us
  transfers between devices with their start and end apart: 16, of which 7 were waited for; matrix products, arithmetic and copies ran while one was open for 25% of the time, Pallas kernels for 0%

profile of v7, /device:TPU:1, one launch (start us, length us, event | category | flops | bytes accessed | tf_op | source)
XLA Modules:
  0.0 529.2 jit_solution(13891447126065281934)
XLA Ops:
  4.9 8.1 %scatter_custom_fusion = s32[4096]{0:T(1024)S(1)} fusion(s32[2048]{0:T(1024)S(1)} %bitcast.44, s32[2048]{0:T(1024)S(1)} %reshape.266, s32[]{:T(128)} %constant.81.clone.1), kind=kCustom, calls=%fused_computation.64 | custom fusion | bytes 16388 | tf_op jit(solution)/shard_map/scatter | solution.py:52
  13.7 13.2 %all-to-all-start = ((s32[64,1,64]{2,1,0:T(1,128)}), s32[64,1,64]{2,1,0:T(1,128)S(1)}, u32[]{:S(2)}, u32[]{:S(2)}) async-start(s32[64,1,64]{2,1,0:T(1,128)} %all_to_all.23), calls=%async_computation | async-start | bytes 65536 | tf_op jit(solution)/shard_map/all_to_all | solution.py:55
  26.8 2.8 copy.46
  29.6 6.4 %all-to-all-done = s32[64,1,64]{2,1,0:T(1,128)S(1)} async-done(((s32[64,1,64]{2,1,0:T(1,128)}), s32[64,1,64]{2,1,0:T(1,128)S(1)}, u32[]{:S(2)}, u32[]{:S(2)}) %all-to-all-start) | async-done | bytes 16416 | tf_op jit(solution)/shard_map/all_to_all | solution.py:55
  36.2 17.4 %gather_fusion = bf16[4096,400]{1,0:T(8,128)(2,1)} fusion(bf16[2048,400]{1,0:T(8,128)(2,1)S(1)} %copy.46, s32[4096]{0:T(1024)S(1)} %broadcast_clamp_fusion), kind=kCustom, calls=%fused_computation | custom fusion | bytes 6569984 | tf_op jit(solution)/shard_map/gather | solution.py:56
  53.5 5.8 %all-to-all-start.1 = ((bf16[64,64,400]{2,1,0:T(8,128)(2,1)}), bf16[64,64,400]{2,1,0:T(8,128)(2,1)}, u32[]{:S(2)}, u32[]{:S(2)}) async-start(bf16[64,64,400]{2,1,0:T(8,128)(2,1)} %bitcast.33), calls=%async_computation.1 | async-start | bytes 8388608 | tf_op jit(solution)/shard_map/all_to_all | solution.py:56
  61.0 2.5 collective-permute-start.2
  65.2 2.3 copy.48
  67.5 4.0 gather_fusion.2
  72.2 83.2 %all-to-all-done.1 = bf16[64,64,400]{2,1,0:T(8,128)(2,1)} async-done(((bf16[64,64,400]{2,1,0:T(8,128)(2,1)}), bf16[64,64,400]{2,1,0:T(8,128)(2,1)}, u32[]{:S(2)}, u32[]{:S(2)}) %all-to-all-start.1) | async-done | bytes 3276832 | tf_op jit(solution)/shard_map/all_to_all | solution.py:56
  155.3 6.7 %gather_fusion.3 = bf16[1024,400]{1,0:T(8,128)(2,1)S(1)} fusion(bf16[4096,400]{1,0:T(8,128)(2,1)} %bitcast.5, s32[1024]{0:T(1024)S(1)} %get-tuple-element.30), kind=kCustom, calls=%fused_computation.3 | custom fusion | bytes 1642496 | tf_op jit(solution)/shard_map/gather | solution.py:62
  162.5 6.7 %gather_fusion.1 = bf16[1024,400]{1,0:T(8,128)(2,1)S(1)} fusion(bf16[4096,400]{1,0:T(8,128)(2,1)} %bitcast.5, s32[1024]{0:T(1024)S(1)} %get-tuple-element.31), kind=kCustom, calls=%fused_computation.1 | custom fusion | bytes 1642496 | tf_op jit(solution)/shard_map/gather | solution.py:61
  172.6 9.4 %multiply_convert_fusion = bf16[1024,4096]{1,0:T(8,128)(2,1)S(1)} fusion(bf16[1024,400]{0,1:T(8,128)(2,1)} %collective-permute-done.2, bf16[1024,400]{0,1:T(8,128)(2,1)} %collective-permute-done.1, bf16[1024,400]{0,1:T(8,128)(2,1)} %collective-permute-done, bf16[1024,400]{0,1:T(8,128)(2,1)} %constant_dynamic-slice_fusion.1, ...), kind=kOutput, calls=%fused_computation.10 | convolution fusion | flops 3391160320 | bytes 13303808 | tf_op jit(solution)/shard_map/dot_general | solution.py:70
  182.0 8.4 %fusion.7 = f32[1024,400]{0,1:T(8,128)S(1)} fusion(bf16[1024,400]{0,1:T(8,128)(2,1)S(1)} %copy.50, bf16[1024,4096]{1,0:T(8,128)(2,1)S(1)} %multiply_convert_fusion, f32[1024]{0:T(1024)S(1)} %divide_add_fusion, bf16[1024,400]{0,1:T(8,128)(2,1)} %collective-permute-done.2, bf16[1024,400]{0,1:T(8,128)(2,1)} %collective-permute-done.1, ...), kind=kOutput, calls=%fused_computation.23 | convolution fusion | flops 3369779200 | bytes 14127104 | tf_op jit(solution)/shard_map/dot_general | solution.py:74
  190.4 1.8 multiply_add_fusion
  192.4 1.8 copy.55
  194.2 8.1 %scatter_custom_fusion.4 = f32[1345,400]{1,0:T(8,128)S(1)} fusion(s32[1024]{0:T(1024)S(1)} %get-tuple-element.28, f32[1024,400]{1,0:T(8,128)} %copy.55, f32[]{:T(128)} %constant.80.clone.1), kind=kCustom, calls=%fused_computation.33 | custom fusion | flops 409600 | bytes 2152512 | tf_op jit(solution)/shard_map/scatter-add | solution.py:91
  202.3 3.7 reshape.218
  206.0 3.1 pad.4
  209.1 1.8 reshape.219
  212.0 2.5 collective-permute-start.8
  215.6 22.6 %collective-permute-done.8 = f32[64,2176]{1,0:T(8,128)S(1)} collective-permute-done((f32[64,2176]{1,0:T(8,128)}, f32[64,2176]{1,0:T(8,128)S(1)}, u32[]{:S(2)}, u32[]{:S(2)}) %collective-permute-start.8) | collective-permute-done | bytes 557088 | tf_op jit(solution)/shard_map/ppermute | solution.py:13
  238.2 4.6 collective-permute-done.6
  244.5 24.1 %all_to_all.36 = f32[64,1,2176]{2,1,0:T(1,128)S(1)} all-to-all(f32[64,1,2176]{2,1,0:T(1,128)S(1)} %reshape.220), channel_id=1, replica_groups=mesh['blk'=4,'shard'=64] {'shard'}, dimensions={0} | all-to-all | bytes 1114112 | tf_op jit(solution)/shard_map/all_to_all | solution.py:99
  270.0 6.8 %all-to-all-start.4 = ((f32[64,1,2176]{2,1,0:T(1,128)}), f32[64,1,2176]{2,1,0:T(1,128)}, u32[]{:S(2)}, u32[]{:S(2)}) async-start(f32[64,1,2176]{2,1,0:T(1,128)} %broadcast_in_dim.51), calls=%async_computation.4 | async-start | bytes 1114112 | tf_op jit(solution)/shard_map/all_to_all | solution.py:18
  277.1 1.8 copy.51
  278.9 9.2 %scatter_custom_fusion.1 = f32[4096,400]{1,0:T(8,128)} fusion(s32[1024]{0:T(1024)S(1)} %get-tuple-element.9, f32[1024,400]{1,0:T(8,128)} %copy.51, f32[]{:T(128)} %constant.80.clone.1), kind=kCustom, calls=%fused_computation.13 | custom fusion | bytes 6554112 | tf_op jit(solution)/shard_map/scatter | solution.py:112
  289.4 1.8 copy.52
  291.2 11.4 %scatter_fusion = f32[4096,400]{1,0:T(8,128)} fusion(f32[4096,400]{1,0:T(8,128)} %scatter_custom_fusion.1, s32[1024]{0:T(1024)S(1)} %get-tuple-element.8, f32[1024,400]{1,0:T(8,128)S(1)} %copy.52), kind=kCustom, calls=%fused_computation.7 | custom fusion | bytes 4919296 | tf_op jit(solution)/shard_map/scatter | solution.py:114
  302.6 10.1 %reshape.216 = f32[64,8,3200]{2,1,0:T(8,128)} reshape(f32[4096,400]{1,0:T(8,128)} %scatter_fusion) | data formatting | bytes 13107200 | tf_op jit(solution)/shard_map/reshape | solution.py:116
  312.7 10.6 %all-to-all-start.2 = ((f32[64,8,3200]{2,1,0:T(8,128)}), f32[64,8,3200]{2,1,0:T(8,128)}, u32[]{:S(2)}, u32[]{:S(2)}) async-start(f32[64,8,3200]{2,1,0:T(8,128)} %reshape.216), calls=%async_computation.2 | async-start | bytes 13107200 | tf_op jit(solution)/shard_map/all_to_all | solution.py:117
  326.1 5.9 %fusion.21 = f32[4096,400]{0,1:T(8,128)S(1)} fusion(bf16[1024,4096]{1,0:T(8,128)(2,1)} %copy-done.11, f32[1024,200]{0,1:T(8,128)S(1)} %copy-done.4, f32[1024,200]{0,1:T(8,128)S(1)} %copy-done.1), kind=kOutput, calls=%fused_computation.58 | convolution fusion | flops 3357081600 | bytes 16580608 | tf_op jit(solution)/shard_map/dot_general | solution.py:77
  332.0 2.6 fusion.34
  338.3 1.9 collective-permute-start.3
  341.6 78.8 %collective-permute-done.10 = f32[64,2176]{1,0:T(8,128)S(1)} collective-permute-done((f32[64,2176]{1,0:T(8,128)S(1)}, f32[64,2176]{1,0:T(8,128)S(1)}, u32[]{:S(2)}, u32[]{:S(2)}) %collective-permute-start.10) | collective-permute-done | bytes 557088 | tf_op jit(solution)/shard_map/ppermute | solution.py:13
  420.4 12.9 %collective-permute-done.9 = f32[64,2176]{1,0:T(8,128)S(1)} collective-permute-done((f32[64,2176]{1,0:T(8,128)S(1)}, f32[64,2176]{1,0:T(8,128)S(1)}, u32[]{:S(2)}, u32[]{:S(2)}) %collective-permute-start.9) | collective-permute-done | bytes 557088 | tf_op jit(solution)/shard_map/ppermute | solution.py:13
  433.5 2.1 gather_fusion.4
  435.5 1.8 broadcast_select_fusion
  438.9 3.1 slice.78
  442.0 4.0 reshape.221
  445.9 2.1 copy.57
  448.0 21.7 %all-to-all-done.2 = f32[64,8,3200]{2,1,0:T(8,128)} async-done(((f32[64,8,3200]{2,1,0:T(8,128)}), f32[64,8,3200]{2,1,0:T(8,128)}, u32[]{:S(2)}, u32[]{:S(2)}) %all-to-all-start.2) | async-done | bytes 6553632 | tf_op jit(solution)/shard_map/all_to_all | solution.py:117
  469.8 11.8 %reshape.290 = f32[4096,400]{1,0:T(8,128)} reshape(f32[64,8,3200]{2,1,0:T(8,128)} %all-to-all-done.2) | data formatting | bytes 13107200 | tf_op jit(solution)/shard_map/reshape | solution.py:118
  481.6 29.6 %scatter_custom_fusion.3 = f32[2048,400]{1,0:T(8,128)} fusion(s32[4096]{0:T(1024)S(1)} %bitcast.43, f32[4096,400]{1,0:T(8,128)} %reshape.290, f32[]{:T(128)} %constant.80.clone.1), kind=kCustom, calls=%fused_computation.18 | custom fusion | flops 1638400 | bytes 3277312 | tf_op jit(solution)/shard_map/scatter-add | solution.py:123
  511.2 1.8 constant_dynamic-slice_fusion
  514.7 5.6 %fusion.10 = f32[1024,400]{0,1:T(8,128)} fusion(f32[1024,400]{0,1:T(8,128)} %copy.60, f32[1024,400]{0,1:T(8,128)} %collective-permute-done.5, f32[1024,400]{0,1:T(8,128)} %collective-permute-done.4, f32[1024,400]{0,1:T(8,128)} %collective-permute-done.3, f32[4096,400]{0,1:T(8,128)} %copy-done.5), kind=kLoop, calls=%fused_computation.27 | loop fusion | flops 1638400 | bytes 9830400 | tf_op jit(solution)/shard_map/add | solution.py:126
  520.3 1.8 copy.54
  523.6 5.2 copy.56
  (88 shorter events, 31.8 us)
Async XLA Ops:
  3.5 0.9 copy-start.9
  13.7 22.4 %all-to-all-start = ((s32[64,1,64]{2,1,0:T(1,128)}), s32[64,1,64]{2,1,0:T(1,128)S(1)}, u32[]{:S(2)}, u32[]{:S(2)}) async-start(s32[64,1,64]{2,1,0:T(1,128)} %all_to_all.23), calls=%async_computation | async-start | bytes 65536 | tf_op jit(solution)/shard_map/all_to_all | solution.py:55
  53.5 6.5 %copy-start.6 = (bf16[2048,400]{0,1:T(8,128)(2,1)S(1)}, bf16[2048,400]{0,1:T(8,128)(2,1)}, u32[]{:S(2)}) copy-start(bf16[2048,400]{0,1:T(8,128)(2,1)} %param.6) | copy-start | bytes 4915204
  53.5 101.8 %all-to-all-start.1 = ((bf16[64,64,400]{2,1,0:T(8,128)(2,1)}), bf16[64,64,400]{2,1,0:T(8,128)(2,1)}, u32[]{:S(2)}, u32[]{:S(2)}) async-start(bf16[64,64,400]{2,1,0:T(8,128)(2,1)} %bitcast.33), calls=%async_computation.1 | async-start | bytes 8388608 | tf_op jit(solution)/shard_map/all_to_all | solution.py:56
  59.4 5.8 %copy-start.10 = (s32[1024]{0:T(1024)S(1)}, s32[1024]{0:T(1024)}, u32[]{:S(2)}) copy-start(s32[1024]{0:T(1024)} %param.10) | copy-start | bytes 12292
  61.0 111.6 %collective-permute-start.2 = (bf16[1024,400]{0,1:T(8,128)(2,1)}, bf16[1024,400]{0,1:T(8,128)(2,1)}, u32[]{:S(2)}, u32[]{:S(2)}) collective-permute-start(bf16[1024,400]{0,1:T(8,128)(2,1)} %constant_dynamic-slice_fusion.1), channel_id=1, source_target_pairs={{0,192},{64,0},{128,64},{192,128},{1,193},{65,1},{129,65},{193,129... | collective-permute-start | bytes 2457608 | tf_op jit(solution)/shard_map/ppermute | solution.py:13
  63.5 109.1 %collective-permute-start.1 = (bf16[1024,400]{0,1:T(8,128)(2,1)}, bf16[1024,400]{0,1:T(8,128)(2,1)}, u32[]{:S(2)}, u32[]{:S(2)}) collective-permute-start(bf16[1024,400]{0,1:T(8,128)(2,1)} %constant_dynamic-slice_fusion.1), channel_id=1, source_target_pairs={{0,128},{64,192},{128,0},{192,64},{1,129},{65,193},{129,1},{193,65... | collective-permute-start | bytes 2457608 | tf_op jit(solution)/shard_map/ppermute | solution.py:13
  64.0 108.6 %collective-permute-start = (bf16[1024,400]{0,1:T(8,128)(2,1)}, bf16[1024,400]{0,1:T(8,128)(2,1)}, u32[]{:S(2)}, u32[]{:S(2)}) collective-permute-start(bf16[1024,400]{0,1:T(8,128)(2,1)} %constant_dynamic-slice_fusion.1), channel_id=1, source_target_pairs={{0,64},{64,128},{128,192},{192,0},{1,65},{65,129},{129,193},{193,1... | collective-permute-start | bytes 2457608 | tf_op jit(solution)/shard_map/ppermute | solution.py:13
  172.3 9.7 %copy-start = (f32[1024,200]{0,1:T(8,128)}, f32[1024,200]{0,1:T(8,128)S(1)}, u32[]{:S(2)}) copy-start(f32[1024,200]{0,1:T(8,128)S(1)} %get-tuple-element.17) | copy-start | bytes 2457604
  172.3 9.7 %copy-start.2 = (f32[1024,200]{0,1:T(8,128)}, f32[1024,200]{0,1:T(8,128)S(1)}, u32[]{:S(2)}) copy-start(f32[1024,200]{0,1:T(8,128)S(1)} %get-tuple-element.18) | copy-start | bytes 2457604
  182.0 8.4 %copy-start.11 = (bf16[1024,4096]{1,0:T(8,128)(2,1)}, bf16[1024,4096]{1,0:T(8,128)(2,1)S(1)}, u32[]{:S(2)}) copy-start(bf16[1024,4096]{1,0:T(8,128)(2,1)S(1)} %multiply_convert_fusion) | copy-start | bytes 25165828
  212.0 26.2 %collective-permute-start.8 = (f32[64,2176]{1,0:T(8,128)}, f32[64,2176]{1,0:T(8,128)S(1)}, u32[]{:S(2)}, u32[]{:S(2)}) collective-permute-start(f32[64,2176]{1,0:T(8,128)} %get-tuple-element.20), channel_id=1, source_target_pairs={{0,192},{64,0},{128,64},{192,128},{1,193},{65,1},{129,65},{193,129... | collective-permute-start | bytes 1671176 | tf_op jit(solution)/shard_map/ppermute | solution.py:13
  214.5 23.7 %collective-permute-start.7 = (f32[64,2176]{1,0:T(8,128)}, f32[64,2176]{1,0:T(8,128)}, u32[]{:S(2)}, u32[]{:S(2)}) collective-permute-start(f32[64,2176]{1,0:T(8,128)} %get-tuple-element.21), channel_id=1, source_target_pairs={{0,128},{64,192},{128,0},{192,64},{1,129},{65,193},{129,1},{193,65... | collective-permute-start | bytes 1671176 | tf_op jit(solution)/shard_map/ppermute | solution.py:13
  215.0 27.8 %collective-permute-start.6 = (f32[64,2176]{1,0:T(8,128)S(1)}, f32[64,2176]{1,0:T(8,128)}, u32[]{:S(2)}, u32[]{:S(2)}) collective-permute-start(f32[64,2176]{1,0:T(8,128)S(1)} %get-tuple-element.19), channel_id=1, source_target_pairs={{0,64},{64,128},{128,192},{192,0},{1,65},{65,129},{129,193},{193,1... | collective-permute-start | bytes 1671176 | tf_op jit(solution)/shard_map/ppermute | solution.py:13
  244.1 32.7 %copy-start.7 = (f32[1024,200]{0,1:T(8,128)S(1)}, f32[1024,200]{0,1:T(8,128)}, u32[]{:S(2)}) copy-start(f32[1024,200]{0,1:T(8,128)} %get-tuple-element.22) | copy-start | bytes 2457604
  244.1 32.7 %copy-start.8 = (f32[1024,200]{0,1:T(8,128)S(1)}, f32[1024,200]{0,1:T(8,128)}, u32[]{:S(2)}) copy-start(f32[1024,200]{0,1:T(8,128)} %get-tuple-element.23) | copy-start | bytes 2457604
  270.0 42.6 %all-to-all-start.4 = ((f32[64,1,2176]{2,1,0:T(1,128)}), f32[64,1,2176]{2,1,0:T(1,128)}, u32[]{:S(2)}, u32[]{:S(2)}) async-start(f32[64,1,2176]{2,1,0:T(1,128)} %broadcast_in_dim.51), calls=%async_computation.4 | async-start | bytes 1114112 | tf_op jit(solution)/shard_map/all_to_all | solution.py:18
  278.8 9.2 %copy-start.1 = (f32[1024,200]{0,1:T(8,128)S(1)}, f32[1024,200]{0,1:T(8,128)}, u32[]{:S(2)}) copy-start(f32[1024,200]{0,1:T(8,128)} %copy-done) | copy-start | bytes 2457604
  278.8 9.2 %copy-start.3 = (f32[1024,200]{0,1:T(8,128)S(1)}, f32[1024,200]{0,1:T(8,128)}, u32[]{:S(2)}) copy-start(f32[1024,200]{0,1:T(8,128)} %copy-done.2) | copy-start | bytes 2457604
  312.7 13.4 %copy-start.4 = (f32[1024,200]{0,1:T(8,128)S(1)}, f32[1024,200]{0,1:T(8,128)}, u32[]{:S(2)}) copy-start(f32[1024,200]{0,1:T(8,128)} %copy-done.2) | copy-start | bytes 2457604
  312.7 157.1 %all-to-all-start.2 = ((f32[64,8,3200]{2,1,0:T(8,128)}), f32[64,8,3200]{2,1,0:T(8,128)}, u32[]{:S(2)}, u32[]{:S(2)}) async-start(f32[64,8,3200]{2,1,0:T(8,128)} %reshape.216), calls=%async_computation.2 | async-start | bytes 13107200 | tf_op jit(solution)/shard_map/all_to_all | solution.py:117
  325.8 15.8 %collective-permute-start.11 = (f32[64,2176]{1,0:T(8,128)S(1)}, f32[64,2176]{1,0:T(8,128)S(1)}, u32[]{:S(2)}, u32[]{:S(2)}) collective-permute-start(f32[64,2176]{1,0:T(8,128)S(1)} %bitcast.34), channel_id=1, source_target_pairs={{0,192},{64,0},{128,64},{192,128},{1,193},{65,1},{129,65},{193,129... | collective-permute-start | bytes 1671176 | tf_op jit(solution)/shard_map/ppermute | solution.py:13
  332.0 4.3 copy-start.5
  336.3 178.4 %collective-permute-start.5 = (f32[1024,400]{0,1:T(8,128)}, f32[1024,400]{0,1:T(8,128)}, u32[]{:S(2)}, u32[]{:S(2)}) collective-permute-start(f32[1024,400]{0,1:T(8,128)} %get-tuple-element.11), channel_id=1, source_target_pairs={{0,64},{64,128},{128,192},{192,0},{1,65},{65,129},{129,193},{193,1... | collective-permute-start | bytes 4915208 | tf_op jit(solution)/shard_map/ppermute | solution.py:13
  337.5 177.1 %collective-permute-start.4 = (f32[1024,400]{0,1:T(8,128)}, f32[1024,400]{0,1:T(8,128)}, u32[]{:S(2)}, u32[]{:S(2)}) collective-permute-start(f32[1024,400]{0,1:T(8,128)} %get-tuple-element.12), channel_id=1, source_target_pairs={{0,128},{64,192},{128,0},{192,64},{1,129},{65,193},{129,1},{193,65... | collective-permute-start | bytes 4915208 | tf_op jit(solution)/shard_map/ppermute | solution.py:13
  338.3 176.4 %collective-permute-start.3 = (f32[1024,400]{0,1:T(8,128)}, f32[1024,400]{0,1:T(8,128)}, u32[]{:S(2)}, u32[]{:S(2)}) collective-permute-start(f32[1024,400]{0,1:T(8,128)} %get-tuple-element.10), channel_id=1, source_target_pairs={{0,192},{64,0},{128,64},{192,128},{1,193},{65,1},{129,65},{193,129... | collective-permute-start | bytes 4915208 | tf_op jit(solution)/shard_map/ppermute | solution.py:13
  340.1 80.3 %collective-permute-start.10 = (f32[64,2176]{1,0:T(8,128)S(1)}, f32[64,2176]{1,0:T(8,128)S(1)}, u32[]{:S(2)}, u32[]{:S(2)}) collective-permute-start(f32[64,2176]{1,0:T(8,128)S(1)} %bitcast.35), channel_id=1, source_target_pairs={{0,128},{64,192},{128,0},{192,64},{1,129},{65,193},{129,1},{193,65... | collective-permute-start | bytes 1671176 | tf_op jit(solution)/shard_map/ppermute | solution.py:13
  341.6 91.8 %collective-permute-start.9 = (f32[64,2176]{1,0:T(8,128)S(1)}, f32[64,2176]{1,0:T(8,128)S(1)}, u32[]{:S(2)}, u32[]{:S(2)}) collective-permute-start(f32[64,2176]{1,0:T(8,128)S(1)} %bitcast.36), channel_id=1, source_target_pairs={{0,64},{64,128},{128,192},{192,0},{1,65},{65,129},{129,193},{193,1... | collective-permute-start | bytes 1671176 | tf_op jit(solution)/shard_map/ppermute | solution.py:13

commit v8 on v7

--- a/solution.py
+++ b/solution.py
@@ -117,13 +117,10 @@
     arrived = lax.all_to_all(payload, "shard", split_axis=0, concat_axis=0, tiled=True)
     arrived_grads = arrived.reshape(n_shard * capacity, width)
 
-    entity_grad = (
-        jnp.zeros((rows_own, width), jnp.float32)
-        .at[asked_rows.reshape(-1)]
-        .add(arrived_grads)
+    base = lax.dynamic_update_slice_in_dim(
+        jnp.zeros((rows_own, width), jnp.float32), carried, span_start, 0
     )
-    current = lax.dynamic_slice_in_dim(entity_grad, span_start, negatives, 0)
-    entity_grad = lax.dynamic_update_slice_in_dim(entity_grad, current + carried, span_start, 0)
+    entity_grad = base.at[asked_rows.reshape(-1)].add(arrived_grads)
     return (entity_grad, relation_grad)
 
 

time: 537 us -> 528 us (0.983)
  waiting for transfers between devices: 230 us -> 212 us
    ppermute x12, waiting for transfers between devices: 119 us -> 101 us  [shifted(): return lax.ppermute(value, axis, [(i, (i + by) % n) for i in range(n)])]
    unnamed x32 -> x27, local copies, waits for them, and re-layouts: 17.9 us -> 14.7 us
  transfers between devices with their start and end apart: 16 -> 16, of which waited for: 7 -> 8; matrix products, arithmetic and copies ran while one was open for 25% -> 20% of each run, Pallas kernels for 0% -> 0%
where the time goes in v8:
time: 528 us; the launch traced here: 519 us
  waiting for transfers between devices  212 us (40%)
  local copies, waits for them, and re-layouts  144 us (27%)
  other arithmetic  56.7 us (11%)
  starting transfers between devices  54 us (10%)
  matrix products  25.4 us (5%)
  blocking collectives  24.2 us (5%)
    ppermute x12, waiting for transfers between devices, shifted(): return lax.ppermute(value, axis, [(i, (i + by) % n) for i in range(n)])  101 us
    all_to_all x1, waiting for transfers between devices, shards(): lax.all_to_all(table[asked_rows], 'shard', split_axis=0, concat_axis=0, t...  83.2 us
    scatter-add x1, other arithmetic, shards(): entity_grad = base.at[asked_rows.reshape(-1)].add(arrived_grads)  30.2 us
    all_to_all x1, blocking collectives, shards(): lax.all_to_all(mine.reshape(n_shard, 1, per_peer), 'shard', 0, 0, tiled=T...  24.2 us
    all_to_all x1, waiting for transfers between devices, shards(): lax.all_to_all(payload, 'shard', split_axis=0, concat_axis=0, tiled=True)  21.6 us
    scatter x2, local copies, waits for them, and re-layouts, shards(): outgoing = jnp.zeros((n_shard * capacity, width), jnp.float32).at[source_...  20.5 us
    ppermute x12, starting transfers between devices, shifted(): return lax.ppermute(value, axis, [(i, (i + by) % n) for i in range(n)])  17.8 us
    gather x1, local copies, waits for them, and re-layouts, shards(): table[asked_rows]  17.4 us
  transfers between devices with their start and end apart: 16, of which 8 were waited for; matrix products, arithmetic and copies ran while one was open for 20% of the time, Pallas kernels for 0%

profile of v8, /device:TPU:1, one launch (start us, length us, event | category | flops | bytes accessed | tf_op | source)
XLA Modules:
  0.0 518.6 jit_solution(15553350595487654579)
XLA Ops:
  4.9 8.1 %scatter_custom_fusion = s32[4096]{0:T(1024)S(1)} fusion(s32[2048]{0:T(1024)S(1)} %bitcast.45, s32[2048]{0:T(1024)S(1)} %reshape.266, s32[]{:T(128)} %constant.82.clone.1), kind=kCustom, calls=%fused_computation.61 | custom fusion | bytes 16388 | tf_op jit(solution)/shard_map/scatter | solution.py:52
  13.7 13.2 %all-to-all-start = ((s32[64,1,64]{2,1,0:T(1,128)}), s32[64,1,64]{2,1,0:T(1,128)S(1)}, u32[]{:S(2)}, u32[]{:S(2)}) async-start(s32[64,1,64]{2,1,0:T(1,128)} %all_to_all.23), calls=%async_computation | async-start | bytes 65536 | tf_op jit(solution)/shard_map/all_to_all | solution.py:55
  26.8 2.8 copy.44
  29.6 6.4 %all-to-all-done = s32[64,1,64]{2,1,0:T(1,128)S(1)} async-done(((s32[64,1,64]{2,1,0:T(1,128)}), s32[64,1,64]{2,1,0:T(1,128)S(1)}, u32[]{:S(2)}, u32[]{:S(2)}) %all-to-all-start) | async-done | bytes 16416 | tf_op jit(solution)/shard_map/all_to_all | solution.py:55
  36.2 17.4 %gather_fusion = bf16[4096,400]{1,0:T(8,128)(2,1)} fusion(bf16[2048,400]{1,0:T(8,128)(2,1)S(1)} %copy.44, s32[4096]{0:T(1024)S(1)} %broadcast_clamp_fusion), kind=kCustom, calls=%fused_computation | custom fusion | bytes 6569984 | tf_op jit(solution)/shard_map/gather | solution.py:56
  53.6 5.8 %all-to-all-start.1 = ((bf16[64,64,400]{2,1,0:T(8,128)(2,1)}), bf16[64,64,400]{2,1,0:T(8,128)(2,1)}, u32[]{:S(2)}, u32[]{:S(2)}) async-start(bf16[64,64,400]{2,1,0:T(8,128)(2,1)} %bitcast.36), calls=%async_computation.1 | async-start | bytes 8388608 | tf_op jit(solution)/shard_map/all_to_all | solution.py:56
  61.1 2.5 collective-permute-start.2
  65.2 2.3 copy.46
  67.5 4.0 gather_fusion.2
  72.2 83.2 %all-to-all-done.1 = bf16[64,64,400]{2,1,0:T(8,128)(2,1)} async-done(((bf16[64,64,400]{2,1,0:T(8,128)(2,1)}), bf16[64,64,400]{2,1,0:T(8,128)(2,1)}, u32[]{:S(2)}, u32[]{:S(2)}) %all-to-all-start.1) | async-done | bytes 3276832 | tf_op jit(solution)/shard_map/all_to_all | solution.py:56
  155.3 6.7 %gather_fusion.3 = bf16[1024,400]{1,0:T(8,128)(2,1)S(1)} fusion(bf16[4096,400]{1,0:T(8,128)(2,1)} %bitcast.4, s32[1024]{0:T(1024)S(1)} %get-tuple-element.30), kind=kCustom, calls=%fused_computation.3 | custom fusion | bytes 1642496 | tf_op jit(solution)/shard_map/gather | solution.py:62
  162.1 7.8 %gather_fusion.1 = bf16[1024,400]{1,0:T(8,128)(2,1)} fusion(bf16[4096,400]{1,0:T(8,128)(2,1)} %bitcast.4, s32[1024]{0:T(1024)S(1)} %get-tuple-element.31), kind=kCustom, calls=%fused_computation.1 | custom fusion | bytes 1642496 | tf_op jit(solution)/shard_map/gather | solution.py:61
  172.8 9.4 %multiply_convert_fusion = bf16[1024,4096]{1,0:T(8,128)(2,1)S(1)} fusion(bf16[1024,400]{0,1:T(8,128)(2,1)} %collective-permute-done.2, bf16[1024,400]{0,1:T(8,128)(2,1)} %collective-permute-done.1, bf16[1024,400]{0,1:T(8,128)(2,1)} %collective-permute-done, bf16[1024,400]{0,1:T(8,128)(2,1)} %constant_dynamic-slice_fusion, ...), kind=kOutput, calls=%fused_computation.10 | convolution fusion | flops 3391160320 | bytes 13303808 | tf_op jit(solution)/shard_map/dot_general | solution.py:70
  182.2 8.4 %fusion.5 = f32[1024,400]{0,1:T(8,128)S(1)} fusion(bf16[1024,400]{0,1:T(8,128)(2,1)S(1)} %copy.49, bf16[1024,4096]{1,0:T(8,128)(2,1)S(1)} %multiply_convert_fusion, f32[1024]{0:T(1024)S(1)} %divide_add_fusion, bf16[1024,400]{0,1:T(8,128)(2,1)} %collective-permute-done.2, bf16[1024,400]{0,1:T(8,128)(2,1)} %collective-permute-done.1, ...), kind=kOutput, calls=%fused_computation.21 | convolution fusion | flops 3369779200 | bytes 14127104 | tf_op jit(solution)/shard_map/dot_general | solution.py:74
  194.4 8.1 %scatter_custom_fusion.4 = f32[1345,400]{1,0:T(8,128)S(1)} fusion(s32[1024]{0:T(1024)S(1)} %get-tuple-element.28, f32[1024,400]{1,0:T(8,128)} %copy.52, f32[]{:T(128)} %constant.80.clone.1), kind=kCustom, calls=%fused_computation.30 | custom fusion | flops 409600 | bytes 2152512 | tf_op jit(solution)/shard_map/scatter-add | solution.py:91
  202.5 3.7 reshape.218
  206.2 3.1 pad.4
  216.4 11.0 %collective-permute-done.6 = f32[64,2176]{1,0:T(8,128)S(1)} collective-permute-done((f32[64,2176]{1,0:T(8,128)}, f32[64,2176]{1,0:T(8,128)S(1)}, u32[]{:S(2)}, u32[]{:S(2)}) %collective-permute-start.6) | collective-permute-done | bytes 557088 | tf_op jit(solution)/shard_map/ppermute | solution.py:13
  227.4 13.0 %collective-permute-done.7 = f32[64,2176]{1,0:T(8,128)} collective-permute-done((f32[64,2176]{1,0:T(8,128)S(1)}, f32[64,2176]{1,0:T(8,128)}, u32[]{:S(2)}, u32[]{:S(2)}) %collective-permute-start.7) | collective-permute-done | bytes 557088 | tf_op jit(solution)/shard_map/ppermute | solution.py:13
  242.2 24.2 %all_to_all.36 = f32[64,1,2176]{2,1,0:T(1,128)S(1)} all-to-all(f32[64,1,2176]{2,1,0:T(1,128)S(1)} %reshape.220), channel_id=1, replica_groups=mesh['blk'=4,'shard'=64] {'shard'}, dimensions={0} | all-to-all | bytes 1114112 | tf_op jit(solution)/shard_map/all_to_all | solution.py:99
  267.9 6.6 %all-to-all-start.4 = ((f32[64,1,2176]{2,1,0:T(1,128)}), f32[64,1,2176]{2,1,0:T(1,128)S(1)}, u32[]{:S(2)}, u32[]{:S(2)}) async-start(f32[64,1,2176]{2,1,0:T(1,128)} %broadcast_in_dim.51), calls=%async_computation.4 | async-start | bytes 1114112 | tf_op jit(solution)/shard_map/all_to_all | solution.py:18
  275.8 1.8 copy.51
  277.7 2.7 pad_maximum_fusion.3
  280.4 2.8 copy.50
  283.2 9.2 %scatter_custom_fusion.1 = f32[4096,400]{1,0:T(8,128)} fusion(s32[1024]{0:T(1024)S(1)} %get-tuple-element.9, f32[1024,400]{1,0:T(8,128)} %copy.50, f32[]{:T(128)} %constant.80.clone.1), kind=kCustom, calls=%fused_computation.13 | custom fusion | bytes 6554112 | tf_op jit(solution)/shard_map/scatter | solution.py:112
  292.4 11.4 %scatter_fusion = f32[4096,400]{1,0:T(8,128)} fusion(f32[4096,400]{1,0:T(8,128)} %scatter_custom_fusion.1, s32[1024]{0:T(1024)S(1)} %get-tuple-element.8, f32[1024,400]{1,0:T(8,128)S(1)} %copy.51), kind=kCustom, calls=%fused_computation.7 | custom fusion | bytes 4919296 | tf_op jit(solution)/shard_map/scatter | solution.py:114
  303.7 10.1 %reshape.216 = f32[64,8,3200]{2,1,0:T(8,128)} reshape(f32[4096,400]{1,0:T(8,128)} %scatter_fusion) | data formatting | bytes 13107200 | tf_op jit(solution)/shard_map/reshape | solution.py:116
  313.8 10.6 %all-to-all-start.2 = ((f32[64,8,3200]{2,1,0:T(8,128)}), f32[64,8,3200]{2,1,0:T(8,128)}, u32[]{:S(2)}, u32[]{:S(2)}) async-start(f32[64,8,3200]{2,1,0:T(8,128)} %reshape.216), calls=%async_computation.2 | async-start | bytes 13107200 | tf_op jit(solution)/shard_map/all_to_all | solution.py:117
  324.4 5.9 %fusion.18 = f32[4096,400]{0,1:T(8,128)S(1)} fusion(bf16[1024,4096]{1,0:T(8,128)(2,1)} %copy-done.9, f32[1024,200]{0,1:T(8,128)S(1)} %copy-done.4, f32[1024,200]{0,1:T(8,128)S(1)} %copy-done.1), kind=kOutput, calls=%fused_computation.55 | convolution fusion | flops 3357081600 | bytes 16580608 | tf_op jit(solution)/shard_map/dot_general | solution.py:77
  330.4 2.5 fusion.31
  334.1 2.2 collective-permute-start.3
  339.2 1.9 collective-permute-start.10
  341.7 30.1 %collective-permute-done.3 = f32[1024,400]{0,1:T(8,128)} collective-permute-done((f32[1024,400]{0,1:T(8,128)}, f32[1024,400]{0,1:T(8,128)}, u32[]{:S(2)}, u32[]{:S(2)}) %collective-permute-start.3) | collective-permute-done | bytes 1638432 | tf_op jit(solution)/shard_map/ppermute | solution.py:13
  371.7 3.9 collective-permute-start.11
  375.6 44.9 %collective-permute-done.5 = f32[1024,400]{0,1:T(8,128)} collective-permute-done((f32[1024,400]{0,1:T(8,128)}, f32[1024,400]{0,1:T(8,128)}, u32[]{:S(2)}, u32[]{:S(2)}) %collective-permute-start.5) | collective-permute-done | bytes 1638432 | tf_op jit(solution)/shard_map/ppermute | solution.py:13
  420.6 4.9 fusion.7
  425.5 1.8 copy.48
  427.4 2.6 broadcast_in_dim.21
  431.5 1.8 collective-permute-done.9
  434.7 2.1 gather_fusion.4
  436.8 1.8 broadcast_select_fusion
  440.1 3.1 slice.78
  443.2 4.0 reshape.221
  447.2 2.1 copy.54
  449.3 21.6 %all-to-all-done.2 = f32[64,8,3200]{2,1,0:T(8,128)} async-done(((f32[64,8,3200]{2,1,0:T(8,128)}), f32[64,8,3200]{2,1,0:T(8,128)}, u32[]{:S(2)}, u32[]{:S(2)}) %all-to-all-start.2) | async-done | bytes 6553632 | tf_op jit(solution)/shard_map/all_to_all | solution.py:117
  470.9 11.8 %reshape.290 = f32[4096,400]{1,0:T(8,128)} reshape(f32[64,8,3200]{2,1,0:T(8,128)} %all-to-all-done.2) | data formatting | bytes 13107200 | tf_op jit(solution)/shard_map/reshape | solution.py:118
  482.7 30.2 %scatter_fusion.1 = f32[2048,400]{1,0:T(8,128)} fusion(f32[2048,400]{1,0:T(8,128)} %constant_dynamic-update-slice_fusion, s32[4096]{0:T(1024)S(1)} %bitcast.44, f32[4096,400]{1,0:T(8,128)} %reshape.290), kind=kCustom, calls=%fused_computation.8 | custom fusion | flops 1638400 | bytes 19677184 | tf_op jit(solution)/shard_map/scatter-add | solution.py:123
  513.0 5.2 copy.53
  (83 shorter events, 35.6 us)
Async XLA Ops:
  3.5 0.9 copy-start.7
  13.7 22.4 %all-to-all-start = ((s32[64,1,64]{2,1,0:T(1,128)}), s32[64,1,64]{2,1,0:T(1,128)S(1)}, u32[]{:S(2)}, u32[]{:S(2)}) async-start(s32[64,1,64]{2,1,0:T(1,128)} %all_to_all.23), calls=%async_computation | async-start | bytes 65536 | tf_op jit(solution)/shard_map/all_to_all | solution.py:55
  53.6 6.5 %copy-start.6 = (bf16[2048,400]{0,1:T(8,128)(2,1)S(1)}, bf16[2048,400]{0,1:T(8,128)(2,1)}, u32[]{:S(2)}) copy-start(bf16[2048,400]{0,1:T(8,128)(2,1)} %param.6) | copy-start | bytes 4915204
  53.6 101.8 %all-to-all-start.1 = ((bf16[64,64,400]{2,1,0:T(8,128)(2,1)}), bf16[64,64,400]{2,1,0:T(8,128)(2,1)}, u32[]{:S(2)}, u32[]{:S(2)}) async-start(bf16[64,64,400]{2,1,0:T(8,128)(2,1)} %bitcast.36), calls=%async_computation.1 | async-start | bytes 8388608 | tf_op jit(solution)/shard_map/all_to_all | solution.py:56
  59.4 5.8 %copy-start.8 = (s32[1024]{0:T(1024)S(1)}, s32[1024]{0:T(1024)}, u32[]{:S(2)}) copy-start(s32[1024]{0:T(1024)} %param.10) | copy-start | bytes 12292
  61.1 111.7 %collective-permute-start.2 = (bf16[1024,400]{0,1:T(8,128)(2,1)}, bf16[1024,400]{0,1:T(8,128)(2,1)}, u32[]{:S(2)}, u32[]{:S(2)}) collective-permute-start(bf16[1024,400]{0,1:T(8,128)(2,1)} %constant_dynamic-slice_fusion), channel_id=1, source_target_pairs={{0,192},{64,0},{128,64},{192,128},{1,193},{65,1},{129,65},{193,129... | collective-permute-start | bytes 2457608 | tf_op jit(solution)/shard_map/ppermute | solution.py:13
  63.5 109.3 %collective-permute-start.1 = (bf16[1024,400]{0,1:T(8,128)(2,1)}, bf16[1024,400]{0,1:T(8,128)(2,1)}, u32[]{:S(2)}, u32[]{:S(2)}) collective-permute-start(bf16[1024,400]{0,1:T(8,128)(2,1)} %constant_dynamic-slice_fusion), channel_id=1, source_target_pairs={{0,128},{64,192},{128,0},{192,64},{1,129},{65,193},{129,1},{193,65... | collective-permute-start | bytes 2457608 | tf_op jit(solution)/shard_map/ppermute | solution.py:13
  64.1 108.8 %collective-permute-start = (bf16[1024,400]{0,1:T(8,128)(2,1)}, bf16[1024,400]{0,1:T(8,128)(2,1)}, u32[]{:S(2)}, u32[]{:S(2)}) collective-permute-start(bf16[1024,400]{0,1:T(8,128)(2,1)} %constant_dynamic-slice_fusion), channel_id=1, source_target_pairs={{0,64},{64,128},{128,192},{192,0},{1,65},{65,129},{129,193},{193,1... | collective-permute-start | bytes 2457608 | tf_op jit(solution)/shard_map/ppermute | solution.py:13
  172.5 9.7 %copy-start = (f32[1024,200]{0,1:T(8,128)}, f32[1024,200]{0,1:T(8,128)S(1)}, u32[]{:S(2)}) copy-start(f32[1024,200]{0,1:T(8,128)S(1)} %get-tuple-element.17) | copy-start | bytes 2457604
  172.5 9.7 %copy-start.2 = (f32[1024,200]{0,1:T(8,128)}, f32[1024,200]{0,1:T(8,128)S(1)}, u32[]{:S(2)}) copy-start(f32[1024,200]{0,1:T(8,128)S(1)} %get-tuple-element.18) | copy-start | bytes 2457604
  182.2 8.4 %copy-start.9 = (bf16[1024,4096]{1,0:T(8,128)(2,1)}, bf16[1024,4096]{1,0:T(8,128)(2,1)S(1)}, u32[]{:S(2)}) copy-start(bf16[1024,4096]{1,0:T(8,128)(2,1)S(1)} %multiply_convert_fusion) | copy-start | bytes 25165828
  212.2 15.2 %collective-permute-start.6 = (f32[64,2176]{1,0:T(8,128)}, f32[64,2176]{1,0:T(8,128)S(1)}, u32[]{:S(2)}, u32[]{:S(2)}) collective-permute-start(f32[64,2176]{1,0:T(8,128)} %get-tuple-element.19), channel_id=1, source_target_pairs={{0,64},{64,128},{128,192},{192,0},{1,65},{65,129},{129,193},{193,1... | collective-permute-start | bytes 1671176 | tf_op jit(solution)/shard_map/ppermute | solution.py:13
  213.4 14.0 %collective-permute-start.8 = (f32[64,2176]{1,0:T(8,128)}, f32[64,2176]{1,0:T(8,128)}, u32[]{:S(2)}, u32[]{:S(2)}) collective-permute-start(f32[64,2176]{1,0:T(8,128)} %get-tuple-element.20), channel_id=1, source_target_pairs={{0,192},{64,0},{128,64},{192,128},{1,193},{65,1},{129,65},{193,129... | collective-permute-start | bytes 1671176 | tf_op jit(solution)/shard_map/ppermute | solution.py:13
  214.9 25.6 %collective-permute-start.7 = (f32[64,2176]{1,0:T(8,128)S(1)}, f32[64,2176]{1,0:T(8,128)}, u32[]{:S(2)}, u32[]{:S(2)}) collective-permute-start(f32[64,2176]{1,0:T(8,128)S(1)} %get-tuple-element.21), channel_id=1, source_target_pairs={{0,128},{64,192},{128,0},{192,64},{1,129},{65,193},{129,1},{193,65... | collective-permute-start | bytes 1671176 | tf_op jit(solution)/shard_map/ppermute | solution.py:13
  241.8 32.7 %copy-start.1 = (f32[1024,200]{0,1:T(8,128)S(1)}, f32[1024,200]{0,1:T(8,128)}, u32[]{:S(2)}) copy-start(f32[1024,200]{0,1:T(8,128)} %copy-done) | copy-start | bytes 2457604
  241.8 32.7 %copy-start.3 = (f32[1024,200]{0,1:T(8,128)S(1)}, f32[1024,200]{0,1:T(8,128)}, u32[]{:S(2)}) copy-start(f32[1024,200]{0,1:T(8,128)} %copy-done.2) | copy-start | bytes 2457604
  267.9 45.9 %all-to-all-start.4 = ((f32[64,1,2176]{2,1,0:T(1,128)}), f32[64,1,2176]{2,1,0:T(1,128)S(1)}, u32[]{:S(2)}, u32[]{:S(2)}) async-start(f32[64,1,2176]{2,1,0:T(1,128)} %broadcast_in_dim.51), calls=%async_computation.4 | async-start | bytes 1114112 | tf_op jit(solution)/shard_map/all_to_all | solution.py:18
  313.8 10.6 %copy-start.4 = (f32[1024,200]{0,1:T(8,128)S(1)}, f32[1024,200]{0,1:T(8,128)}, u32[]{:S(2)}) copy-start(f32[1024,200]{0,1:T(8,128)} %copy-done.2) | copy-start | bytes 2457604
  313.8 157.1 %all-to-all-start.2 = ((f32[64,8,3200]{2,1,0:T(8,128)}), f32[64,8,3200]{2,1,0:T(8,128)}, u32[]{:S(2)}, u32[]{:S(2)}) async-start(f32[64,8,3200]{2,1,0:T(8,128)} %reshape.216), calls=%async_computation.2 | async-start | bytes 13107200 | tf_op jit(solution)/shard_map/all_to_all | solution.py:117
  330.4 3.7 copy-start.5
  334.1 37.6 %collective-permute-start.3 = (f32[1024,400]{0,1:T(8,128)}, f32[1024,400]{0,1:T(8,128)}, u32[]{:S(2)}, u32[]{:S(2)}) collective-permute-start(f32[1024,400]{0,1:T(8,128)} %get-tuple-element.10), channel_id=1, source_target_pairs={{0,192},{64,0},{128,64},{192,128},{1,193},{65,1},{129,65},{193,129... | collective-permute-start | bytes 4915208 | tf_op jit(solution)/shard_map/ppermute | solution.py:13
  336.3 84.3 %collective-permute-start.5 = (f32[1024,400]{0,1:T(8,128)}, f32[1024,400]{0,1:T(8,128)}, u32[]{:S(2)}, u32[]{:S(2)}) collective-permute-start(f32[1024,400]{0,1:T(8,128)} %get-tuple-element.11), channel_id=1, source_target_pairs={{0,64},{64,128},{128,192},{192,0},{1,65},{65,129},{129,193},{193,1... | collective-permute-start | bytes 4915208 | tf_op jit(solution)/shard_map/ppermute | solution.py:13
  336.3 84.3 %collective-permute-start.4 = (f32[1024,400]{0,1:T(8,128)S(1)}, f32[1024,400]{0,1:T(8,128)}, u32[]{:S(2)}, u32[]{:S(2)}) collective-permute-start(f32[1024,400]{0,1:T(8,128)S(1)} %get-tuple-element.12), channel_id=1, source_target_pairs={{0,128},{64,192},{128,0},{192,64},{1,129},{65,193},{129,1},{193,65... | collective-permute-start | bytes 4915208 | tf_op jit(solution)/shard_map/ppermute | solution.py:13
  339.2 92.3 %collective-permute-start.10 = (f32[64,2176]{1,0:T(8,128)S(1)}, f32[64,2176]{1,0:T(8,128)S(1)}, u32[]{:S(2)}, u32[]{:S(2)}) collective-permute-start(f32[64,2176]{1,0:T(8,128)S(1)} %bitcast.37), channel_id=1, source_target_pairs={{0,128},{64,192},{128,0},{192,64},{1,129},{65,193},{129,1},{193,65... | collective-permute-start | bytes 1671176 | tf_op jit(solution)/shard_map/ppermute | solution.py:13
  341.0 92.3 %collective-permute-start.9 = (f32[64,2176]{1,0:T(8,128)S(1)}, f32[64,2176]{1,0:T(8,128)}, u32[]{:S(2)}, u32[]{:S(2)}) collective-permute-start(f32[64,2176]{1,0:T(8,128)S(1)} %bitcast.38), channel_id=1, source_target_pairs={{0,64},{64,128},{128,192},{192,0},{1,65},{65,129},{129,193},{193,1... | collective-permute-start | bytes 1671176 | tf_op jit(solution)/shard_map/ppermute | solution.py:13
  371.7 61.6 %collective-permute-start.11 = (f32[64,2176]{1,0:T(8,128)S(1)}, f32[64,2176]{1,0:T(8,128)}, u32[]{:S(2)}, u32[]{:S(2)}) collective-permute-start(f32[64,2176]{1,0:T(8,128)S(1)} %bitcast.39), channel_id=1, source_target_pairs={{0,192},{64,0},{128,64},{192,128},{1,193},{65,1},{129,65},{193,129... | collective-permute-start | bytes 1671176 | tf_op jit(solution)/shard_map/ppermute | solution.py:13

commit v9 on v8

--- a/solution.py
+++ b/solution.py
@@ -91,10 +91,21 @@
     local_relation = jnp.zeros((rel_rows_n, width), jnp.float32).at[rel_ids].add(rel_term)
     quarters = jnp.pad(local_relation.reshape(-1), (0, n_blk * n_shard * per_peer - total))
     quarters = quarters.reshape(n_blk, n_shard, per_peer)
-    mine = lax.dynamic_index_in_dim(quarters, me_blk, 0, keepdims=False)
+    received = []
     for d in range(1, n_blk):
         outgoing_quarter = lax.dynamic_index_in_dim(quarters, (me_blk + d) % n_blk, 0, keepdims=False)
-        mine = mine + shifted(outgoing_quarter, "blk", n_blk, d)
+        received.append(shifted(outgoing_quarter, "blk", n_blk, d))
+    outgoing = (
+        jnp.zeros((n_shard * capacity, width), jnp.float32)
+        .at[source_slots]
+        .set(source_grad)
+        .at[target_slots]
+        .set(target_grad)
+    )
+    received, outgoing = lax.optimization_barrier((received, outgoing))
+    mine = lax.dynamic_index_in_dim(quarters, me_blk, 0, keepdims=False)
+    for part in received:
+        mine = mine + part
 
     small = lax.all_to_all(
         mine.reshape(n_shard, 1, per_peer), "shard", 0, 0, tiled=True
@@ -106,13 +117,6 @@
 
     sub = 8
     grad_lanes = capacity * width // sub
-    outgoing = (
-        jnp.zeros((n_shard * capacity, width), jnp.float32)
-        .at[source_slots]
-        .set(source_grad)
-        .at[target_slots]
-        .set(target_grad)
-    )
     payload = outgoing.reshape(n_shard, sub, grad_lanes)
     arrived = lax.all_to_all(payload, "shard", split_axis=0, concat_axis=0, tiled=True)
     arrived_grads = arrived.reshape(n_shard * capacity, width)

time: 528 us -> 509 us (0.964)
  waiting for transfers between devices: 212 us -> 196 us
    ppermute x12, waiting for transfers between devices: 101 us -> 76.7 us  [shifted(): return lax.ppermute(value, axis, [(i, (i + by) % n) for i in range(n)])]
    all_to_all x1, waiting for transfers between devices: 0.01 us -> 7.98 us  [spread(): return lax.all_to_all(copies, axis, 0, 0, tiled=False)]
    unnamed x27 -> x25, local copies, waits for them, and re-layouts: 14.7 us -> 15 us
  transfers between devices with their start and end apart: 16 -> 16, of which waited for: 8 -> 7; matrix products, arithmetic and copies ran while one was open for 20% -> 21% of each run, Pallas kernels for 0% -> 0%
where the time goes in v9:
time: 509 us; the launch traced here: 500 us
  waiting for transfers between devices  196 us (39%)
  local copies, waits for them, and re-layouts  146 us (29%)
  other arithmetic  57.5 us (11%)
  starting transfers between devices  49 us (10%)
  matrix products  25.4 us (5%)
  blocking collectives  24.3 us (5%)
    all_to_all x1, waiting for transfers between devices, shards(): lax.all_to_all(table[asked_rows], 'shard', split_axis=0, concat_axis=0, t...  83.4 us
    ppermute x12, waiting for transfers between devices, shifted(): return lax.ppermute(value, axis, [(i, (i + by) % n) for i in range(n)])  76.7 us
    scatter-add x1, other arithmetic, shards(): entity_grad = base.at[asked_rows.reshape(-1)].add(arrived_grads)  29.5 us
    all_to_all x1, blocking collectives, shards(): lax.all_to_all(mine.reshape(n_shard, 1, per_peer), 'shard', 0, 0, tiled=T...  24.3 us
    scatter x2, local copies, waits for them, and re-layouts, shards(): outgoing = jnp.zeros((n_shard * capacity, width), jnp.float32).at[source_...  21.3 us
    all_to_all x1, waiting for transfers between devices, shards(): lax.all_to_all(payload, 'shard', split_axis=0, concat_axis=0, tiled=True)  21.2 us
    ppermute x12, starting transfers between devices, shifted(): return lax.ppermute(value, axis, [(i, (i + by) % n) for i in range(n)])  17.3 us
    gather x1, local copies, waits for them, and re-layouts, shards(): table[asked_rows]  17.3 us
  transfers between devices with their start and end apart: 16, of which 7 were waited for; matrix products, arithmetic and copies ran while one was open for 21% of the time, Pallas kernels for 0%

profile of v9, /device:TPU:1, one launch (start us, length us, event | category | flops | bytes accessed | tf_op | source)
XLA Modules:
  0.0 499.8 jit_solution(18389992114627629292)
XLA Ops:
  4.9 8.1 %scatter_custom_fusion = s32[4096]{0:T(1024)S(1)} fusion(s32[2048]{0:T(1024)S(1)} %bitcast.45, s32[2048]{0:T(1024)S(1)} %reshape.266, s32[]{:T(128)} %constant.82.clone.1), kind=kCustom, calls=%fused_computation.61 | custom fusion | bytes 16388 | tf_op jit(solution)/shard_map/scatter | solution.py:52
  13.7 13.2 %all-to-all-start = ((s32[64,1,64]{2,1,0:T(1,128)}), s32[64,1,64]{2,1,0:T(1,128)S(1)}, u32[]{:S(2)}, u32[]{:S(2)}) async-start(s32[64,1,64]{2,1,0:T(1,128)} %all_to_all.23), calls=%async_computation | async-start | bytes 65536 | tf_op jit(solution)/shard_map/all_to_all | solution.py:55
  26.8 2.8 copy.44
  29.6 6.4 %all-to-all-done = s32[64,1,64]{2,1,0:T(1,128)S(1)} async-done(((s32[64,1,64]{2,1,0:T(1,128)}), s32[64,1,64]{2,1,0:T(1,128)S(1)}, u32[]{:S(2)}, u32[]{:S(2)}) %all-to-all-start) | async-done | bytes 16416 | tf_op jit(solution)/shard_map/all_to_all | solution.py:55
  36.2 17.3 %gather_fusion = bf16[4096,400]{1,0:T(8,128)(2,1)} fusion(bf16[2048,400]{1,0:T(8,128)(2,1)S(1)} %copy.44, s32[4096]{0:T(1024)S(1)} %broadcast_clamp_fusion), kind=kCustom, calls=%fused_computation | custom fusion | bytes 6569984 | tf_op jit(solution)/shard_map/gather | solution.py:56
  53.4 5.8 %all-to-all-start.1 = ((bf16[64,64,400]{2,1,0:T(8,128)(2,1)}), bf16[64,64,400]{2,1,0:T(8,128)(2,1)}, u32[]{:S(2)}, u32[]{:S(2)}) async-start(bf16[64,64,400]{2,1,0:T(8,128)(2,1)} %bitcast.36), calls=%async_computation.1 | async-start | bytes 8388608 | tf_op jit(solution)/shard_map/all_to_all | solution.py:56
  60.9 2.5 collective-permute-start.2
  65.1 2.0 copy.46
  67.1 4.0 gather_fusion.2
  71.8 83.4 %all-to-all-done.1 = bf16[64,64,400]{2,1,0:T(8,128)(2,1)} async-done(((bf16[64,64,400]{2,1,0:T(8,128)(2,1)}), bf16[64,64,400]{2,1,0:T(8,128)(2,1)}, u32[]{:S(2)}, u32[]{:S(2)}) %all-to-all-start.1) | async-done | bytes 3276832 | tf_op jit(solution)/shard_map/all_to_all | solution.py:56
  155.2 6.7 %gather_fusion.3 = bf16[1024,400]{1,0:T(8,128)(2,1)S(1)} fusion(bf16[4096,400]{1,0:T(8,128)(2,1)} %bitcast.4, s32[1024]{0:T(1024)S(1)} %get-tuple-element.38), kind=kCustom, calls=%fused_computation.3 | custom fusion | bytes 1642496 | tf_op jit(solution)/shard_map/gather | solution.py:62
  161.9 7.8 %gather_fusion.1 = bf16[1024,400]{1,0:T(8,128)(2,1)} fusion(bf16[4096,400]{1,0:T(8,128)(2,1)} %bitcast.4, s32[1024]{0:T(1024)S(1)} %get-tuple-element.39), kind=kCustom, calls=%fused_computation.1 | custom fusion | bytes 1642496 | tf_op jit(solution)/shard_map/gather | solution.py:61
  172.7 9.4 %multiply_convert_fusion = bf16[1024,4096]{1,0:T(8,128)(2,1)S(1)} fusion(bf16[1024,400]{0,1:T(8,128)(2,1)} %collective-permute-done.2, bf16[1024,400]{0,1:T(8,128)(2,1)} %collective-permute-done.1, bf16[1024,400]{0,1:T(8,128)(2,1)} %collective-permute-done, bf16[1024,400]{0,1:T(8,128)(2,1)} %constant_dynamic-slice_fusion, ...), kind=kOutput, calls=%fused_computation.10 | convolution fusion | flops 3391160320 | bytes 13303808 | tf_op jit(solution)/shard_map/dot_general | solution.py:70
  182.1 8.4 %fusion.5 = f32[1024,400]{0,1:T(8,128)S(1)} fusion(bf16[1024,400]{0,1:T(8,128)(2,1)S(1)} %copy.49, bf16[1024,4096]{1,0:T(8,128)(2,1)S(1)} %multiply_convert_fusion, f32[1024]{0:T(1024)S(1)} %divide_add_fusion, bf16[1024,400]{0,1:T(8,128)(2,1)} %collective-permute-done.2, bf16[1024,400]{0,1:T(8,128)(2,1)} %collective-permute-done.1, ...), kind=kOutput, calls=%fused_computation.21 | convolution fusion | flops 3369779200 | bytes 14127104 | tf_op jit(solution)/shard_map/dot_general | solution.py:74
  194.3 8.3 %scatter_custom_fusion.1 = f32[1345,400]{1,0:T(8,128)S(1)} fusion(s32[1024]{0:T(1024)S(1)} %get-tuple-element.36, f32[1024,400]{1,0:T(8,128)} %copy.50, f32[]{:T(128)} %constant.80.clone.1), kind=kCustom, calls=%fused_computation.30 | custom fusion | flops 409600 | bytes 2152512 | tf_op jit(solution)/shard_map/scatter-add | solution.py:91
  202.6 3.7 reshape.216
  206.3 3.1 pad.4
  212.4 2.5 collective-permute-start.8
  216.0 2.6 fusion.11
  218.6 2.8 copy.52
  221.4 2.8 pad_maximum_fusion.4
  224.2 2.8 copy.51
  227.0 9.3 %scatter_custom_fusion.2 = f32[4096,400]{1,0:T(8,128)} fusion(s32[1024]{0:T(1024)S(1)} %get-tuple-element.17, f32[1024,400]{1,0:T(8,128)} %copy.51, f32[]{:T(128)} %constant.80.clone.1), kind=kCustom, calls=%fused_computation.13 | custom fusion | bytes 6554112 | tf_op jit(solution)/shard_map/scatter | solution.py:101
  236.3 12.0 %scatter_fusion = f32[4096,400]{1,0:T(8,128)} fusion(f32[4096,400]{1,0:T(8,128)} %scatter_custom_fusion.2, s32[1024]{0:T(1024)S(1)} %get-tuple-element.16, f32[1024,400]{1,0:T(8,128)} %copy.52), kind=kCustom, calls=%fused_computation.8 | custom fusion | bytes 4919296 | tf_op jit(solution)/shard_map/scatter | solution.py:103
  250.2 24.3 %all_to_all.36 = f32[64,1,2176]{2,1,0:T(1,128)S(1)} all-to-all(f32[64,1,2176]{2,1,0:T(1,128)S(1)} %reshape.220), channel_id=1, replica_groups=mesh['blk'=4,'shard'=64] {'shard'}, dimensions={0} | all-to-all | bytes 1114112 | tf_op jit(solution)/shard_map/all_to_all | solution.py:110
  275.9 6.2 %all-to-all-start.4 = ((f32[64,1,2176]{2,1,0:T(1,128)}), f32[64,1,2176]{2,1,0:T(1,128)S(1)}, u32[]{:S(2)}, u32[]{:S(2)}) async-start(f32[64,1,2176]{2,1,0:T(1,128)} %broadcast_in_dim.51), calls=%async_computation.4 | async-start | bytes 1114112 | tf_op jit(solution)/shard_map/all_to_all | solution.py:18
  282.2 10.1 %reshape.218 = f32[64,8,3200]{2,1,0:T(8,128)} reshape(f32[4096,400]{1,0:T(8,128)} %scatter_fusion) | data formatting | bytes 13107200 | tf_op jit(solution)/shard_map/reshape | solution.py:120
  292.3 8.0 %all-to-all-done.4 = f32[64,1,2176]{2,1,0:T(1,128)S(1)} async-done(((f32[64,1,2176]{2,1,0:T(1,128)}), f32[64,1,2176]{2,1,0:T(1,128)S(1)}, u32[]{:S(2)}, u32[]{:S(2)}) %all-to-all-start.4) | async-done | bytes 557088 | tf_op jit(solution)/shard_map/all_to_all | solution.py:18
  300.2 6.4 %all-to-all-start.2 = ((f32[64,8,3200]{2,1,0:T(8,128)}), f32[64,8,3200]{2,1,0:T(8,128)}, u32[]{:S(2)}, u32[]{:S(2)}) async-start(f32[64,8,3200]{2,1,0:T(8,128)} %reshape.218), calls=%async_computation.2 | async-start | bytes 13107200 | tf_op jit(solution)/shard_map/all_to_all | solution.py:121
  306.7 5.9 %fusion.18 = f32[4096,400]{0,1:T(8,128)S(1)} fusion(bf16[1024,4096]{1,0:T(8,128)(2,1)} %copy-done.8, f32[1024,200]{0,1:T(8,128)S(1)} %copy-done.3, f32[1024,200]{0,1:T(8,128)S(1)} %copy-done.1), kind=kOutput, calls=%fused_computation.55 | convolution fusion | flops 3357081600 | bytes 16580608 | tf_op jit(solution)/shard_map/dot_general | solution.py:77
  312.6 2.4 fusion.31
  316.9 2.1 collective-permute-start.3
  324.5 29.7 %collective-permute-done.3 = f32[1024,400]{0,1:T(8,128)} collective-permute-done((f32[1024,400]{0,1:T(8,128)}, f32[1024,400]{0,1:T(8,128)}, u32[]{:S(2)}, u32[]{:S(2)}) %collective-permute-start.3) | collective-permute-done | bytes 1638432 | tf_op jit(solution)/shard_map/ppermute | solution.py:13
  354.2 3.9 collective-permute-start.11
  358.0 45.1 %collective-permute-done.5 = f32[1024,400]{0,1:T(8,128)} collective-permute-done((f32[1024,400]{0,1:T(8,128)}, f32[1024,400]{0,1:T(8,128)}, u32[]{:S(2)}, u32[]{:S(2)}) %collective-permute-start.5) | collective-permute-done | bytes 1638432 | tf_op jit(solution)/shard_map/ppermute | solution.py:13
  403.1 4.9 fusion.7
  408.1 1.8 copy.48
  409.9 2.6 broadcast_in_dim.21
  414.1 1.9 collective-permute-done.9
  417.3 2.1 gather_fusion.4
  419.4 1.8 broadcast_select_fusion
  422.8 3.1 slice.78
  425.8 4.0 reshape.221
  429.8 2.1 copy.54
  431.9 21.2 %all-to-all-done.2 = f32[64,8,3200]{2,1,0:T(8,128)} async-done(((f32[64,8,3200]{2,1,0:T(8,128)}), f32[64,8,3200]{2,1,0:T(8,128)}, u32[]{:S(2)}, u32[]{:S(2)}) %all-to-all-start.2) | async-done | bytes 6553632 | tf_op jit(solution)/shard_map/all_to_all | solution.py:121
  453.1 11.8 %reshape.298 = f32[4096,400]{1,0:T(8,128)} reshape(f32[64,8,3200]{2,1,0:T(8,128)} %all-to-all-done.2) | data formatting | bytes 13107200 | tf_op jit(solution)/shard_map/reshape | solution.py:122
  465.0 29.5 %scatter_fusion.1 = f32[2048,400]{1,0:T(8,128)} fusion(f32[2048,400]{1,0:T(8,128)} %constant_dynamic-update-slice_fusion, s32[4096]{0:T(1024)S(1)} %bitcast.44, f32[4096,400]{1,0:T(8,128)} %reshape.298), kind=kCustom, calls=%fused_computation.9 | custom fusion | flops 1638400 | bytes 19677184 | tf_op jit(solution)/shard_map/scatter-add | solution.py:127
  494.4 5.2 %copy.53 = f32[2048,400]{0,1:T(8,128)} copy(f32[2048,400]{1,0:T(8,128)} %scatter_fusion.1) | data formatting | bytes 6553600
  (81 shorter events, 34.1 us)
Async XLA Ops:
  3.5 0.9 copy-start.6
  13.7 22.4 %all-to-all-start = ((s32[64,1,64]{2,1,0:T(1,128)}), s32[64,1,64]{2,1,0:T(1,128)S(1)}, u32[]{:S(2)}, u32[]{:S(2)}) async-start(s32[64,1,64]{2,1,0:T(1,128)} %all_to_all.23), calls=%async_computation | async-start | bytes 65536 | tf_op jit(solution)/shard_map/all_to_all | solution.py:55
  53.4 6.5 %copy-start.5 = (bf16[2048,400]{0,1:T(8,128)(2,1)S(1)}, bf16[2048,400]{0,1:T(8,128)(2,1)}, u32[]{:S(2)}) copy-start(bf16[2048,400]{0,1:T(8,128)(2,1)} %param.6) | copy-start | bytes 4915204
  53.4 101.8 %all-to-all-start.1 = ((bf16[64,64,400]{2,1,0:T(8,128)(2,1)}), bf16[64,64,400]{2,1,0:T(8,128)(2,1)}, u32[]{:S(2)}, u32[]{:S(2)}) async-start(bf16[64,64,400]{2,1,0:T(8,128)(2,1)} %bitcast.36), calls=%async_computation.1 | async-start | bytes 8388608 | tf_op jit(solution)/shard_map/all_to_all | solution.py:56
  59.3 5.8 %copy-start.7 = (s32[1024]{0:T(1024)S(1)}, s32[1024]{0:T(1024)}, u32[]{:S(2)}) copy-start(s32[1024]{0:T(1024)} %param.10) | copy-start | bytes 12292
  60.9 111.7 %collective-permute-start.2 = (bf16[1024,400]{0,1:T(8,128)(2,1)}, bf16[1024,400]{0,1:T(8,128)(2,1)}, u32[]{:S(2)}, u32[]{:S(2)}) collective-permute-start(bf16[1024,400]{0,1:T(8,128)(2,1)} %constant_dynamic-slice_fusion), channel_id=1, source_target_pairs={{0,192},{64,0},{128,64},{192,128},{1,193},{65,1},{129,65},{193,129... | collective-permute-start | bytes 2457608 | tf_op jit(solution)/shard_map/ppermute | solution.py:13
  63.4 109.3 %collective-permute-start.1 = (bf16[1024,400]{0,1:T(8,128)(2,1)}, bf16[1024,400]{0,1:T(8,128)(2,1)}, u32[]{:S(2)}, u32[]{:S(2)}) collective-permute-start(bf16[1024,400]{0,1:T(8,128)(2,1)} %constant_dynamic-slice_fusion), channel_id=1, source_target_pairs={{0,128},{64,192},{128,0},{192,64},{1,129},{65,193},{129,1},{193,65... | collective-permute-start | bytes 2457608 | tf_op jit(solution)/shard_map/ppermute | solution.py:13
  63.9 108.8 %collective-permute-start = (bf16[1024,400]{0,1:T(8,128)(2,1)}, bf16[1024,400]{0,1:T(8,128)(2,1)}, u32[]{:S(2)}, u32[]{:S(2)}) collective-permute-start(bf16[1024,400]{0,1:T(8,128)(2,1)} %constant_dynamic-slice_fusion), channel_id=1, source_target_pairs={{0,64},{64,128},{128,192},{192,0},{1,65},{65,129},{129,193},{193,1... | collective-permute-start | bytes 2457608 | tf_op jit(solution)/shard_map/ppermute | solution.py:13
  172.4 9.7 %copy-start = (f32[1024,200]{0,1:T(8,128)}, f32[1024,200]{0,1:T(8,128)S(1)}, u32[]{:S(2)}) copy-start(f32[1024,200]{0,1:T(8,128)S(1)} %get-tuple-element.25) | copy-start | bytes 2457604
  172.4 9.7 %copy-start.2 = (f32[1024,200]{0,1:T(8,128)}, f32[1024,200]{0,1:T(8,128)S(1)}, u32[]{:S(2)}) copy-start(f32[1024,200]{0,1:T(8,128)S(1)} %get-tuple-element.26) | copy-start | bytes 2457604
  182.1 8.4 %copy-start.8 = (bf16[1024,4096]{1,0:T(8,128)(2,1)}, bf16[1024,4096]{1,0:T(8,128)(2,1)S(1)}, u32[]{:S(2)}) copy-start(bf16[1024,4096]{1,0:T(8,128)(2,1)S(1)} %multiply_convert_fusion) | copy-start | bytes 25165828
  211.2 4.9 copy-start.1
  212.4 35.9 %collective-permute-start.8 = (f32[64,2176]{1,0:T(8,128)}, f32[64,2176]{1,0:T(8,128)}, u32[]{:S(2)}, u32[]{:S(2)}) collective-permute-start(f32[64,2176]{1,0:T(8,128)} %get-tuple-element.27), channel_id=1, source_target_pairs={{0,192},{64,0},{128,64},{192,128},{1,193},{65,1},{129,65},{193,129... | collective-permute-start | bytes 1671176 | tf_op jit(solution)/shard_map/ppermute | solution.py:13
  214.9 33.4 %collective-permute-start.7 = (f32[64,2176]{1,0:T(8,128)}, f32[64,2176]{1,0:T(8,128)}, u32[]{:S(2)}, u32[]{:S(2)}) collective-permute-start(f32[64,2176]{1,0:T(8,128)} %get-tuple-element.28), channel_id=1, source_target_pairs={{0,128},{64,192},{128,0},{192,64},{1,129},{65,193},{129,1},{193,65... | collective-permute-start | bytes 1671176 | tf_op jit(solution)/shard_map/ppermute | solution.py:13
  215.4 32.9 %collective-permute-start.6 = (f32[64,2176]{1,0:T(8,128)}, f32[64,2176]{1,0:T(8,128)}, u32[]{:S(2)}, u32[]{:S(2)}) collective-permute-start(f32[64,2176]{1,0:T(8,128)} %get-tuple-element.29), channel_id=1, source_target_pairs={{0,64},{64,128},{128,192},{192,0},{1,65},{65,129},{129,193},{193,1... | collective-permute-start | bytes 1671176 | tf_op jit(solution)/shard_map/ppermute | solution.py:13
  275.9 24.3 %all-to-all-start.4 = ((f32[64,1,2176]{2,1,0:T(1,128)}), f32[64,1,2176]{2,1,0:T(1,128)S(1)}, u32[]{:S(2)}, u32[]{:S(2)}) async-start(f32[64,1,2176]{2,1,0:T(1,128)} %broadcast_in_dim.51), calls=%async_computation.4 | async-start | bytes 1114112 | tf_op jit(solution)/shard_map/all_to_all | solution.py:18
  292.3 14.4 %copy-start.3 = (f32[1024,200]{0,1:T(8,128)S(1)}, f32[1024,200]{0,1:T(8,128)}, u32[]{:S(2)}) copy-start(f32[1024,200]{0,1:T(8,128)} %copy-done.2) | copy-start | bytes 2457604
  300.2 152.9 %all-to-all-start.2 = ((f32[64,8,3200]{2,1,0:T(8,128)}), f32[64,8,3200]{2,1,0:T(8,128)}, u32[]{:S(2)}, u32[]{:S(2)}) async-start(f32[64,8,3200]{2,1,0:T(8,128)} %reshape.218), calls=%async_computation.2 | async-start | bytes 13107200 | tf_op jit(solution)/shard_map/all_to_all | solution.py:121
  312.6 4.2 copy-start.4
  316.9 37.3 %collective-permute-start.3 = (f32[1024,400]{0,1:T(8,128)}, f32[1024,400]{0,1:T(8,128)}, u32[]{:S(2)}, u32[]{:S(2)}) collective-permute-start(f32[1024,400]{0,1:T(8,128)} %get-tuple-element.18), channel_id=1, source_target_pairs={{0,192},{64,0},{128,64},{192,128},{1,193},{65,1},{129,65},{193,129... | collective-permute-start | bytes 4915208 | tf_op jit(solution)/shard_map/ppermute | solution.py:13
  318.9 84.2 %collective-permute-start.5 = (f32[1024,400]{0,1:T(8,128)}, f32[1024,400]{0,1:T(8,128)}, u32[]{:S(2)}, u32[]{:S(2)}) collective-permute-start(f32[1024,400]{0,1:T(8,128)} %get-tuple-element.19), channel_id=1, source_target_pairs={{0,64},{64,128},{128,192},{192,0},{1,65},{65,129},{129,193},{193,1... | collective-permute-start | bytes 4915208 | tf_op jit(solution)/shard_map/ppermute | solution.py:13
  318.9 84.2 %collective-permute-start.4 = (f32[1024,400]{0,1:T(8,128)}, f32[1024,400]{0,1:T(8,128)}, u32[]{:S(2)}, u32[]{:S(2)}) collective-permute-start(f32[1024,400]{0,1:T(8,128)} %get-tuple-element.20), channel_id=1, source_target_pairs={{0,128},{64,192},{128,0},{192,64},{1,129},{65,193},{129,1},{193,65... | collective-permute-start | bytes 4915208 | tf_op jit(solution)/shard_map/ppermute | solution.py:13
  321.6 92.5 %collective-permute-start.10 = (f32[64,2176]{1,0:T(8,128)S(1)}, f32[64,2176]{1,0:T(8,128)S(1)}, u32[]{:S(2)}, u32[]{:S(2)}) collective-permute-start(f32[64,2176]{1,0:T(8,128)S(1)} %bitcast.37), channel_id=1, source_target_pairs={{0,128},{64,192},{128,0},{192,64},{1,129},{65,193},{129,1},{193,65... | collective-permute-start | bytes 1671176 | tf_op jit(solution)/shard_map/ppermute | solution.py:13
  323.4 92.6 %collective-permute-start.9 = (f32[64,2176]{1,0:T(8,128)S(1)}, f32[64,2176]{1,0:T(8,128)}, u32[]{:S(2)}, u32[]{:S(2)}) collective-permute-start(f32[64,2176]{1,0:T(8,128)S(1)} %bitcast.38), channel_id=1, source_target_pairs={{0,64},{64,128},{128,192},{192,0},{1,65},{65,129},{129,193},{193,1... | collective-permute-start | bytes 1671176 | tf_op jit(solution)/shard_map/ppermute | solution.py:13
  354.2 61.8 %collective-permute-start.11 = (f32[64,2176]{1,0:T(8,128)S(1)}, f32[64,2176]{1,0:T(8,128)}, u32[]{:S(2)}, u32[]{:S(2)}) collective-permute-start(f32[64,2176]{1,0:T(8,128)S(1)} %bitcast.39), channel_id=1, source_target_pairs={{0,192},{64,0},{128,64},{192,128},{1,193},{65,1},{129,65},{193,129... | collective-permute-start | bytes 1671176 | tf_op jit(solution)/shard_map/ppermute | solution.py:13

commit v10 on v9

--- a/solution.py
+++ b/solution.py
@@ -107,10 +107,7 @@
     for part in received:
         mine = mine + part
 
-    small = lax.all_to_all(
-        mine.reshape(n_shard, 1, per_peer), "shard", 0, 0, tiled=True
-    ).sum(axis=(0, 1))
-    quarter = spread(small, "shard", n_shard)
+    quarter = lax.psum(mine, "shard")
     held = jnp.stack([quarter] + [shifted(quarter, "blk", n_blk, d) for d in range(1, n_blk)])
     order = (me_blk - jnp.arange(n_blk, dtype=jnp.int32)) % n_blk
     relation_grad = jnp.take(held, order, axis=0).reshape(-1)[:total].reshape(rel_rows_n, width)

time: 509 us -> 686 us (1.35)
  waiting for transfers between devices: 196 us -> 391 us
  blocking collectives: 24.3 us -> 0 us
  between operations: 2.09 us -> 15.7 us
  starting transfers between devices: 49 us -> 39.9 us
    psum x0 -> x1, waiting for transfers between devices: none -> 211 us  [shards(): quarter = lax.psum(mine, 'shard')]
    all_to_all x1 -> x0, blocking collectives: 24.3 us -> none  [shards(): lax.all_to_all(mine.reshape(n_shard, 1, per_peer), 'shard', 0, 0, tiled=T...]
    all_to_all x1, waiting for transfers between devices: 21.2 us -> 0.01 us  [shards(): lax.all_to_all(payload, 'shard', split_axis=0, concat_axis=0, tiled=True)]
    ppermute x12, waiting for transfers between devices: 76.7 us -> 90.3 us  [shifted(): return lax.ppermute(value, axis, [(i, (i + by) % n) for i in range(n)])]
    all_to_all x1 -> x0, waiting for transfers between devices: 7.98 us -> none  [spread(): return lax.all_to_all(copies, axis, 0, 0, tiled=False)]
    unnamed x25 -> x26, local copies, waits for them, and re-layouts: 15 us -> 15.4 us
  transfers between devices with their start and end apart: 16 -> 16, of which waited for: 7 -> 5; matrix products, arithmetic and copies ran while one was open for 21% -> 14% of each run, Pallas kernels for 0% -> 0%
where the time goes in v10:
time: 686 us; the launch traced here: 674 us
  waiting for transfers between devices  391 us (57%)
  local copies, waits for them, and re-layouts  145 us (21%)
  other arithmetic  57.5 us (8%)
  starting transfers between devices  39.9 us (6%)
  matrix products  25.6 us (4%)
  between operations  15.7 us (2%)
    psum x1, waiting for transfers between devices, shards(): quarter = lax.psum(mine, 'shard')  211 us
    ppermute x12, waiting for transfers between devices, shifted(): return lax.ppermute(value, axis, [(i, (i + by) % n) for i in range(n)])  90.3 us
    all_to_all x1, waiting for transfers between devices, shards(): lax.all_to_all(table[asked_rows], 'shard', split_axis=0, concat_axis=0, t...  83.2 us
    scatter-add x1, other arithmetic, shards(): entity_grad = base.at[asked_rows.reshape(-1)].add(arrived_grads)  31.6 us
    scatter x2, local copies, waits for them, and re-layouts, shards(): outgoing = jnp.zeros((n_shard * capacity, width), jnp.float32).at[source_...  21.4 us
    gather x1, local copies, waits for them, and re-layouts, shards(): table[asked_rows]  17.3 us
    unnamed x26, local copies, waits for them, and re-layouts  15.4 us
    ppermute x12, starting transfers between devices, shifted(): return lax.ppermute(value, axis, [(i, (i + by) % n) for i in range(n)])  14.3 us
  transfers between devices with their start and end apart: 16, of which 5 were waited for; matrix products, arithmetic and copies ran while one was open for 14% of the time, Pallas kernels for 0%

profile of v10, /device:TPU:1, one launch (start us, length us, event | category | flops | bytes accessed | tf_op | source)
XLA Modules:
  0.0 674.0 jit_solution(6011177792562457636)
XLA Ops:
  11.4 8.1 %scatter_custom_fusion = s32[4096]{0:T(1024)S(1)} fusion(s32[2048]{0:T(1024)S(1)} %bitcast.40, s32[2048]{0:T(1024)S(1)} %reshape.255, s32[]{:T(128)} %constant.82.clone.1), kind=kCustom, calls=%fused_computation.59 | custom fusion | bytes 16388 | tf_op jit(solution)/shard_map/scatter | solution.py:52
  20.2 13.2 %all-to-all-start = ((s32[64,1,64]{2,1,0:T(1,128)}), s32[64,1,64]{2,1,0:T(1,128)S(1)}, u32[]{:S(2)}, u32[]{:S(2)}) async-start(s32[64,1,64]{2,1,0:T(1,128)} %all_to_all.14), calls=%async_computation | async-start | bytes 65536 | tf_op jit(solution)/shard_map/all_to_all | solution.py:55
  33.4 2.8 copy.30
  36.2 6.4 all-to-all-done
  42.7 17.3 %gather_fusion = bf16[4096,400]{1,0:T(8,128)(2,1)} fusion(bf16[2048,400]{1,0:T(8,128)(2,1)S(1)} %copy.30, s32[4096]{0:T(1024)S(1)} %broadcast_clamp_fusion), kind=kCustom, calls=%fused_computation | custom fusion | bytes 6569984 | tf_op jit(solution)/shard_map/gather | solution.py:56
  60.0 5.8 all-to-all-start.1
  67.5 2.5 collective-permute-start.2
  71.7 2.3 copy.32
  73.9 4.0 gather_fusion.2
  78.6 83.2 %all-to-all-done.1 = bf16[64,64,400]{2,1,0:T(8,128)(2,1)} async-done(((bf16[64,64,400]{2,1,0:T(8,128)(2,1)}), bf16[64,64,400]{2,1,0:T(8,128)(2,1)}, u32[]{:S(2)}, u32[]{:S(2)}) %all-to-all-start.1) | async-done | bytes 3276832 | tf_op jit(solution)/shard_map/all_to_all | solution.py:56
  161.8 6.7 gather_fusion.3
  168.5 7.8 %gather_fusion.1 = bf16[1024,400]{1,0:T(8,128)(2,1)} fusion(bf16[4096,400]{1,0:T(8,128)(2,1)} %bitcast.4, s32[1024]{0:T(1024)S(1)} %get-tuple-element.35), kind=kCustom, calls=%fused_computation.1 | custom fusion | bytes 1642496 | tf_op jit(solution)/shard_map/gather | solution.py:61
  179.3 9.4 %multiply_convert_fusion = bf16[1024,4096]{1,0:T(8,128)(2,1)S(1)} fusion(bf16[1024,400]{0,1:T(8,128)(2,1)} %collective-permute-done.2, bf16[1024,400]{0,1:T(8,128)(2,1)} %collective-permute-done.1, bf16[1024,400]{0,1:T(8,128)(2,1)} %collective-permute-done, bf16[1024,400]{0,1:T(8,128)(2,1)} %constant_dynamic-slice_fusion, ...), kind=kOutput, calls=%fused_computation.10 | convolution fusion | flops 3391160320 | bytes 13303808 | tf_op jit(solution)/shard_map/dot_general | solution.py:70
  188.7 8.4 %fusion.5 = f32[1024,400]{0,1:T(8,128)S(1)} fusion(bf16[1024,400]{0,1:T(8,128)(2,1)S(1)} %copy.35, bf16[1024,4096]{1,0:T(8,128)(2,1)S(1)} %multiply_convert_fusion, f32[1024]{0:T(1024)S(1)} %divide_add_fusion, bf16[1024,400]{0,1:T(8,128)(2,1)} %collective-permute-done.2, bf16[1024,400]{0,1:T(8,128)(2,1)} %collective-permute-done.1, ...), kind=kOutput, calls=%fused_computation.21 | convolution fusion | flops 3369779200 | bytes 14127104 | tf_op jit(solution)/shard_map/dot_general | solution.py:74
  197.1 1.8 multiply_add_fusion
  199.0 1.8 copy.36
  200.8 8.1 %scatter_custom_fusion.1 = f32[1345,400]{1,0:T(8,128)S(1)} fusion(s32[1024]{0:T(1024)S(1)} %get-tuple-element.32, f32[1024,400]{1,0:T(8,128)} %copy.36, f32[]{:T(128)} %constant.80.clone.1), kind=kCustom, calls=%fused_computation.30 | custom fusion | flops 409600 | bytes 2152512 | tf_op jit(solution)/shard_map/scatter-add | solution.py:91
  208.9 3.7 reshape.206
  212.6 3.1 pad.4
  215.7 1.8 reshape.207
  218.8 2.5 collective-permute-start.8
  223.7 2.8 copy.38
  226.5 2.8 pad_maximum_fusion.4
  229.3 2.8 copy.37
  232.1 9.4 %scatter_custom_fusion.2 = f32[4096,400]{1,0:T(8,128)} fusion(s32[1024]{0:T(1024)S(1)} %get-tuple-element.15, f32[1024,400]{1,0:T(8,128)} %copy.37, f32[]{:T(128)} %constant.80.clone.1), kind=kCustom, calls=%fused_computation.13 | custom fusion | bytes 6554112 | tf_op jit(solution)/shard_map/scatter | solution.py:101
  241.5 12.0 %scatter_fusion = f32[4096,400]{1,0:T(8,128)} fusion(f32[4096,400]{1,0:T(8,128)} %scatter_custom_fusion.2, s32[1024]{0:T(1024)S(1)} %get-tuple-element.14, f32[1024,400]{1,0:T(8,128)} %copy.38), kind=kCustom, calls=%fused_computation.8 | custom fusion | bytes 4919296 | tf_op jit(solution)/shard_map/scatter | solution.py:103
  253.5 10.1 %reshape.208 = f32[64,8,3200]{2,1,0:T(8,128)} reshape(f32[4096,400]{1,0:T(8,128)} %scatter_fusion) | data formatting | bytes 13107200 | tf_op jit(solution)/shard_map/reshape | solution.py:117
  263.6 6.6 all-to-all-start.2
  270.2 2.3 fusion.14
  273.9 210.7 %all-reduce.3.cloned.1.call-done = f32[64,2176]{1,0:T(8,128)} async-done(((f32[64,2176]{1,0:T(8,128)}), f32[64,2176]{1,0:T(8,128)}) %all-reduce.3.cloned.1.call-update) | async-done | bytes 557072 | tf_op jit(solution)/shard_map/psum | solution.py:110
  484.6 2.4 collective-permute-start.11
  487.0 6.2 fusion.18
  493.2 2.3 fusion.31
  495.6 1.9 copy-done.4
  499.5 2.4 collective-permute-start.10
  502.1 77.1 %collective-permute-done.10 = f32[64,2176]{1,0:T(8,128)S(1)} collective-permute-done((f32[64,2176]{1,0:T(8,128)S(1)}, f32[64,2176]{1,0:T(8,128)S(1)}, u32[]{:S(2)}, u32[]{:S(2)}) %collective-permute-start.10) | collective-permute-done | bytes 557088 | tf_op jit(solution)/shard_map/ppermute | solution.py:13
  579.3 13.1 %collective-permute-done.9 = f32[64,2176]{1,0:T(8,128)S(1)} collective-permute-done((f32[64,2176]{1,0:T(8,128)S(1)}, f32[64,2176]{1,0:T(8,128)S(1)}, u32[]{:S(2)}, u32[]{:S(2)}) %collective-permute-start.9) | collective-permute-done | bytes 557088 | tf_op jit(solution)/shard_map/ppermute | solution.py:13
  592.5 2.1 gather_fusion.4
  594.6 1.8 broadcast_select_fusion
  597.9 3.1 slice.78
  601.0 4.0 reshape.210
  605.0 2.1 copy.40
  607.1 4.9 fusion.7
  612.1 1.8 copy.34
  613.9 2.6 broadcast_in_dim.19
  618.1 11.8 %reshape.287 = f32[4096,400]{1,0:T(8,128)} reshape(f32[64,8,3200]{2,1,0:T(8,128)} %all-to-all-done.2) | data formatting | bytes 13107200 | tf_op jit(solution)/shard_map/reshape | solution.py:119
  629.9 31.6 %scatter_fusion.1 = f32[2048,400]{1,0:T(8,128)} fusion(f32[2048,400]{1,0:T(8,128)} %constant_dynamic-update-slice_fusion, s32[4096]{0:T(1024)S(1)} %bitcast.39, f32[4096,400]{1,0:T(8,128)} %reshape.287), kind=kCustom, calls=%fused_computation.9 | custom fusion | flops 1638400 | bytes 19677184 | tf_op jit(solution)/shard_map/scatter-add | solution.py:124
  661.5 5.2 copy.39
  (79 shorter events, 22.0 us)
Async XLA Ops:
  10.0 0.9 copy-start.7
  20.2 22.4 %all-to-all-start = ((s32[64,1,64]{2,1,0:T(1,128)}), s32[64,1,64]{2,1,0:T(1,128)S(1)}, u32[]{:S(2)}, u32[]{:S(2)}) async-start(s32[64,1,64]{2,1,0:T(1,128)} %all_to_all.14), calls=%async_computation | async-start | bytes 65536 | tf_op jit(solution)/shard_map/all_to_all | solution.py:55
  60.0 6.5 copy-start.5
  60.0 101.8 %all-to-all-start.1 = ((bf16[64,64,400]{2,1,0:T(8,128)(2,1)}), bf16[64,64,400]{2,1,0:T(8,128)(2,1)}, u32[]{:S(2)}, u32[]{:S(2)}) async-start(bf16[64,64,400]{2,1,0:T(8,128)(2,1)} %bitcast.32), calls=%async_computation.1 | async-start | bytes 8388608 | tf_op jit(solution)/shard_map/all_to_all | solution.py:56
  65.8 5.8 copy-start.8
  67.5 111.7 %collective-permute-start.2 = (bf16[1024,400]{0,1:T(8,128)(2,1)}, bf16[1024,400]{0,1:T(8,128)(2,1)}, u32[]{:S(2)}, u32[]{:S(2)}) collective-permute-start(bf16[1024,400]{0,1:T(8,128)(2,1)} %constant_dynamic-slice_fusion), channel_id=1, source_target_pairs={{0,192},{64,0},{128,64},{192,128},{1,193},{65,1},{129,65},{193,129... | collective-permute-start | bytes 2457608 | tf_op jit(solution)/shard_map/ppermute | solution.py:13
  70.0 109.3 %collective-permute-start.1 = (bf16[1024,400]{0,1:T(8,128)(2,1)}, bf16[1024,400]{0,1:T(8,128)(2,1)}, u32[]{:S(2)}, u32[]{:S(2)}) collective-permute-start(bf16[1024,400]{0,1:T(8,128)(2,1)} %constant_dynamic-slice_fusion), channel_id=1, source_target_pairs={{0,128},{64,192},{128,0},{192,64},{1,129},{65,193},{129,1},{193,65... | collective-permute-start | bytes 2457608 | tf_op jit(solution)/shard_map/ppermute | solution.py:13
  70.5 108.8 %collective-permute-start = (bf16[1024,400]{0,1:T(8,128)(2,1)}, bf16[1024,400]{0,1:T(8,128)(2,1)}, u32[]{:S(2)}, u32[]{:S(2)}) collective-permute-start(bf16[1024,400]{0,1:T(8,128)(2,1)} %constant_dynamic-slice_fusion), channel_id=1, source_target_pairs={{0,64},{64,128},{128,192},{192,0},{1,65},{65,129},{129,193},{193,1... | collective-permute-start | bytes 2457608 | tf_op jit(solution)/shard_map/ppermute | solution.py:13
  178.9 9.7 %copy-start = (f32[1024,200]{0,1:T(8,128)}, f32[1024,200]{0,1:T(8,128)S(1)}, u32[]{:S(2)}) copy-start(f32[1024,200]{0,1:T(8,128)S(1)} %get-tuple-element.23) | copy-start | bytes 2457604
  178.9 9.7 %copy-start.2 = (f32[1024,200]{0,1:T(8,128)}, f32[1024,200]{0,1:T(8,128)S(1)}, u32[]{:S(2)}) copy-start(f32[1024,200]{0,1:T(8,128)S(1)} %get-tuple-element.24) | copy-start | bytes 2457604
  188.7 8.4 %copy-start.9 = (bf16[1024,4096]{1,0:T(8,128)(2,1)}, bf16[1024,4096]{1,0:T(8,128)(2,1)S(1)}, u32[]{:S(2)}) copy-start(bf16[1024,4096]{1,0:T(8,128)(2,1)S(1)} %multiply_convert_fusion) | copy-start | bytes 25165828
  217.5 4.9 copy-start.1
  217.5 4.9 copy-start.3
  218.8 34.8 %collective-permute-start.8 = (f32[64,2176]{1,0:T(8,128)}, f32[64,2176]{1,0:T(8,128)}, u32[]{:S(2)}, u32[]{:S(2)}) collective-permute-start(f32[64,2176]{1,0:T(8,128)} %get-tuple-element.25), channel_id=1, source_target_pairs={{0,192},{64,0},{128,64},{192,128},{1,193},{65,1},{129,65},{193,129... | collective-permute-start | bytes 1671176 | tf_op jit(solution)/shard_map/ppermute | solution.py:13
  221.2 32.3 %collective-permute-start.7 = (f32[64,2176]{1,0:T(8,128)}, f32[64,2176]{1,0:T(8,128)}, u32[]{:S(2)}, u32[]{:S(2)}) collective-permute-start(f32[64,2176]{1,0:T(8,128)} %get-tuple-element.26), channel_id=1, source_target_pairs={{0,128},{64,192},{128,0},{192,64},{1,129},{65,193},{129,1},{193,65... | collective-permute-start | bytes 1671176 | tf_op jit(solution)/shard_map/ppermute | solution.py:13
  221.8 31.8 %collective-permute-start.6 = (f32[64,2176]{1,0:T(8,128)}, f32[64,2176]{1,0:T(8,128)}, u32[]{:S(2)}, u32[]{:S(2)}) collective-permute-start(f32[64,2176]{1,0:T(8,128)} %get-tuple-element.27), channel_id=1, source_target_pairs={{0,64},{64,128},{128,192},{192,0},{1,65},{65,129},{129,193},{193,1... | collective-permute-start | bytes 1671176 | tf_op jit(solution)/shard_map/ppermute | solution.py:13
  263.6 354.5 %all-to-all-start.2 = ((f32[64,8,3200]{2,1,0:T(8,128)}), f32[64,8,3200]{2,1,0:T(8,128)}, u32[]{:S(2)}, u32[]{:S(2)}) async-start(f32[64,8,3200]{2,1,0:T(8,128)} %reshape.208), calls=%async_computation.2 | async-start | bytes 13107200 | tf_op jit(solution)/shard_map/all_to_all | solution.py:118
  270.2 214.4 %all-reduce.3.cloned.1.call-start = ((), (), s32[]{:S(2)}) async-start(), calls=%async_computation.3 | async-start | bytes 1114112 | tf_op jit(solution)/shard_map/psum | solution.py:110
  484.6 17.2 %collective-permute-start.11 = (f32[64,2176]{1,0:T(8,128)}, f32[64,2176]{1,0:T(8,128)S(1)}, u32[]{:S(2)}, u32[]{:S(2)}) collective-permute-start(f32[64,2176]{1,0:T(8,128)} %all-reduce.3.cloned.1.call-done), channel_id=1, source_target_pairs={{0,192},{64,0},{128,64},{192,128},{1,193},{65,1},{129,65},{193,129... | collective-permute-start | bytes 1671176 | tf_op jit(solution)/shard_map/ppermute | solution.py:13
  493.2 4.2 copy-start.4
  493.2 6.2 copy-start.6
  497.4 109.7 %collective-permute-start.3 = (f32[1024,400]{0,1:T(8,128)}, f32[1024,400]{0,1:T(8,128)}, u32[]{:S(2)}, u32[]{:S(2)}) collective-permute-start(f32[1024,400]{0,1:T(8,128)} %get-tuple-element.16), channel_id=1, source_target_pairs={{0,192},{64,0},{128,64},{192,128},{1,193},{65,1},{129,65},{193,129... | collective-permute-start | bytes 4915208 | tf_op jit(solution)/shard_map/ppermute | solution.py:13
  498.0 109.1 %collective-permute-start.5 = (f32[1024,400]{0,1:T(8,128)}, f32[1024,400]{0,1:T(8,128)}, u32[]{:S(2)}, u32[]{:S(2)}) collective-permute-start(f32[1024,400]{0,1:T(8,128)} %get-tuple-element.17), channel_id=1, source_target_pairs={{0,64},{64,128},{128,192},{192,0},{1,65},{65,129},{129,193},{193,1... | collective-permute-start | bytes 4915208 | tf_op jit(solution)/shard_map/ppermute | solution.py:13
  498.9 108.2 %collective-permute-start.4 = (f32[1024,400]{0,1:T(8,128)}, f32[1024,400]{0,1:T(8,128)}, u32[]{:S(2)}, u32[]{:S(2)}) collective-permute-start(f32[1024,400]{0,1:T(8,128)} %get-tuple-element.18), channel_id=1, source_target_pairs={{0,128},{64,192},{128,0},{192,64},{1,129},{65,193},{129,1},{193,65... | collective-permute-start | bytes 4915208 | tf_op jit(solution)/shard_map/ppermute | solution.py:13
  499.5 79.8 %collective-permute-start.10 = (f32[64,2176]{1,0:T(8,128)S(1)}, f32[64,2176]{1,0:T(8,128)S(1)}, u32[]{:S(2)}, u32[]{:S(2)}) collective-permute-start(f32[64,2176]{1,0:T(8,128)S(1)} %copy-done.6), channel_id=1, source_target_pairs={{0,128},{64,192},{128,0},{192,64},{1,129},{65,193},{129,1},{193,65... | collective-permute-start | bytes 1671176 | tf_op jit(solution)/shard_map/ppermute | solution.py:13
  501.9 90.5 %collective-permute-start.9 = (f32[64,2176]{1,0:T(8,128)S(1)}, f32[64,2176]{1,0:T(8,128)S(1)}, u32[]{:S(2)}, u32[]{:S(2)}) collective-permute-start(f32[64,2176]{1,0:T(8,128)S(1)} %copy-done.6), channel_id=1, source_target_pairs={{0,64},{64,128},{128,192},{192,0},{1,65},{65,129},{129,193},{193,1... | collective-permute-start | bytes 1671176 | tf_op jit(solution)/shard_map/ppermute | solution.py:13
Sparse Core Ops, SparseCore 0:
  275.1 209.4 all-reduce.2
